TPU v7x, 256 devices: a whole 4x4x8 slice. The times are simulated.
256 devices in a mesh: dp: 32 (over y, x, core), mp: 8 (over z).
Axes of the slice: x: 4, y: 4, z: 8, core: 2. Of those that a mesh axis runs over, the one named last changes fastest.
Arguments:
- weights: float32 [8, 2657088], P('mp', 'dp'), may hold values from -60 to 60
- moment_first: float32 [8, 2657088], P('mp', 'dp'), may hold values from -0.6 to 0.6
- moment_second: float32 [8, 2657088], P('mp', 'dp'), may hold values from 0.01 to 1
- gradients: bfloat16 [8, 2657088], P('mp', 'dp'), may hold values from -6 to 6
- tensor_order: int32 [7], replicated, may hold values from 0 to 6, each once
Outputs:
- new_weights: float32 [8, 2657088], P('mp', 'dp')
- new_first: float32 [8, 2657088], P('mp', 'dp')
- new_second: float32 [8, 2657088], P('mp', 'dp')
- scaled_update: float32 [8, 2657088], P('mp', 'dp')
- training_copy: bfloat16 [8, 2657088], P('mp')
- trust: float32 [7], replicated
Inputs may be any that keep to these rules, and one draw needn't show every extreme that they name: `tensor_order`: a permutation of 0 to 6.
All inputs are finite; a program needn't handle non-finite values.
Results may differ from a plain program's by a relative error of at most 0.0075.
Values may be sent and summed in bfloat16 or wider, within the bound.
No kernel may reach another device: no remote copies, remote signals or barrier semaphores. Data moves between devices by JAX's collectives and lax.ppermute only.
A program may use at most 192 MiB of HBM per device.

v0:
```python
import math

import jax
import jax.numpy as jnp
from jax import lax
from jax.sharding import PartitionSpec as P

D = 2304
EXPERTS = 8
SLOTS = 7


fix_first = 1.0 - math.exp(1000.0 * math.log(0.9))
fix_second = 1.0 - math.exp(1000.0 * math.log(0.999))
decay_values = (0.01, 0.01, 0.01, 0.01, 0.0, 0.0, 0.0)
step_rate = 0.1


def tensor_kind(places, order, parts):
    lengths = jnp.array(
        [D * D // parts] * 4 + [EXPERTS * D // parts, D // parts, D // parts], jnp.int32
    )
    kinds = jnp.arange(SLOTS, dtype=jnp.int32)
    slot_lengths = jnp.sum(jnp.where(order[:, None] == kinds[None, :], lengths[None, :], 0), axis=1)
    boundary = jnp.cumsum(slot_lengths)
    slot = jnp.zeros_like(places)
    for number in range(SLOTS - 1):
        slot = slot + (places >= boundary[number]).astype(jnp.int32)
    result = jnp.zeros_like(places)
    for number in range(SLOTS):
        result = jnp.where(slot == number, order[number], result)
    return result


def per_entry(kind, table):
    result = jnp.zeros(kind.shape, jnp.float32)
    for number in range(SLOTS):
        result = jnp.where(kind == number, table[number], result)
    return result


def kind_sums(kind, values):
    kinds = jnp.arange(SLOTS, dtype=jnp.int32)[:, None]
    return jnp.sum(jnp.where(kind == kinds, values, 0.0), axis=1)


def on_device(weights, moment_first, moment_second, gradients, tensor_order):
    parts = lax.axis_size("mp")
    width = weights.shape[1]
    places = lax.axis_index("dp") * width + lax.broadcasted_iota(jnp.int32, (1, width), 1)
    kind = tensor_kind(places, tensor_order, parts)
    wpart = kind_sums(kind, weights * weights)
    grads = gradients.astype(jnp.float32)
    new_first = 0.9 * moment_first + 0.1 * grads
    new_second = 0.999 * moment_second + 0.001 * grads * grads
    decay = per_entry(kind, jnp.array(decay_values, jnp.float32))
    raw = new_first / fix_first / (jnp.sqrt(new_second / fix_second) + 1e-06) + decay * weights
    upart = kind_sums(kind, raw * raw)
    wsq, usq = lax.psum((wpart, upart), ("dp", "mp"))
    trust = jnp.sqrt(wsq) / (jnp.sqrt(usq) + 1e-06)
    scaled_update = per_entry(kind, trust) * raw
    new_weights = weights - step_rate * scaled_update
    training_copy = lax.all_gather(new_weights.astype(jnp.bfloat16), "dp", axis=1, tiled=True)
    return (new_weights, new_first, new_second, scaled_update, training_copy, trust)


def solution(mesh):
    return jax.shard_map(
        on_device,
        mesh=mesh,
        in_specs=(P("mp", "dp"), P("mp", "dp"), P("mp", "dp"), P("mp", "dp"), P()),
        out_specs=(P("mp", "dp"), P("mp", "dp"), P("mp", "dp"), P("mp", "dp"), P("mp", None), P()),
        check_vma=False,
    )
```

profile of v0, /device:TPU:1, one launch (start us, length us, event | category | flops | bytes accessed | tf_op | source)
XLA Modules:
  0.0 327.9 jit_solution(2176446493614914482)
XLA Ops:
  7.2 0.0 copy-start.2
  7.2 0.0 copy-start
  7.2 0.0 all-reduce.4.cloned.1.call-start
  7.2 1.6 fusion.20
  8.8 0.9 select_reduce_fusion.2
  9.7 0.2 reduce-window.4
  9.9 0.7 fusion.19
  10.5 8.5 %select_select_fusion = s32[83034]{0:T(1024)S(1)} fusion(s32[]{:T(128)} %bitcast.13, s32[]{:T(128)} %bitcast.12, s32[]{:T(128)} %bitcast.11, s32[]{:T(128)} %bitcast.10, s32[]{:T(128)} %bitcast.9, s32[]{:T(128)} %bitcast.8, s32[]{:T(128)} %bitcast.7, s32[]{:T(128)} %bitcast.6, s32[]{:T(128)} %bitcast.5, s32[]{:T(128)} %bitcast.4, s32[]{:T(128)} %bitcast.3, ...), kind=kLoop, calls=%fused_computation.31 | loop fusion | flops 2657088 | bytes 332192 | tf_op jit(solution)/shard_map/jit(_where)/select_n | solution.py:31
  19.0 19.6 %multiply_reduce_fusion = (f32[83034]{0:T(1024)S(1)}, f32[1,83034]{1,0:T(1,128)S(1)}, f32[1,83034]{1,0:T(1,128)}, f32[1,83034]{1,0:T(1,128)}, f32[83034]{0:T(1024)S(1)}) fusion(f32[1,83034]{1,0:T(1,128)} %param.7, s32[]{:T(128)} %bitcast.13, s32[]{:T(128)} %bitcast.12, s32[]{:T(128)} %bitcast.11, s32[]{:T(128)} %bitcast.10, s32[]{:T(128)} %bitcast.9, ...), kind=kLoop, calls=%fused_computation.51 | loop fusion | flops 5065074 | bytes 2823212 | tf_op jit(solution)/shard_map/mul | solution.py:58
  38.6 0.9 select_reduce_fusion.1
  39.5 81.6 %all-reduce.1 = (f32[7]{0:T(128)S(1)}, f32[7]{0:T(128)S(1)}) all-reduce(f32[7]{0:T(128)S(1)} %get-tuple-element.7, f32[7]{0:T(128)S(1)} %get-tuple-element.6), channel_id=1, replica_groups=mesh['dp'=32,'mp'=8] {'dp','mp'}, use_global_device_ids=true, to_apply=%region_5.6 | all-reduce | flops 14 | bytes 112 | tf_op jit(solution)/shard_map/psum | solution.py:59
  121.1 0.0 copy-start.1
  121.1 0.7 fusion.18
  121.7 0.0 copy-done.2
  121.8 0.6 dynamic-slice
  123.0 0.0 copy-done
  123.0 20.9 %convert_reduce_fusion = (bf16[83034]{0:T(1024)(128)(2,1)S(1)}, f32[1,83034]{1,0:T(1,128)}, f32[1,83034]{1,0:T(1,128)}) fusion(f32[1,83034]{1,0:T(1,128)S(1)} %copy-done, f32[1,83034]{1,0:T(1,128)S(1)} %get-tuple-element.14, f32[]{:T(128)} %bitcast.20, f32[]{:T(128)} %bitcast.19, f32[]{:T(128)} %bitcast.18, f32[]{:T(128)} %bitcast.17, f32[]{:T(128)} %bitcast.16, ...), kind=kLoop, calls=%fused_computation.49 | loop fusion | flops 4151700 | bytes 1494696 | tf_op jit(solution)/shard_map/convert_element_type | solution.py:63
  143.9 2.6 broadcast.606
  146.5 0.0 copy-done.1
  146.5 3.8 %dynamic-update-slice = bf16[2657088]{0:T(1024)(128)(2,1)} dynamic-update-slice(bf16[2657088]{0:T(1024)(128)(2,1)} %broadcast.606, bf16[83034]{0:T(1024)(128)(2,1)S(1)} %get-tuple-element.10, u32[]{:T(128)} %bitcast.21) | dynamic-update-slice | bytes 332140
  150.3 0.0 all-reduce.4.cloned.1.call-update
  150.3 118.8 %all-reduce.4.cloned.1.call-done = bf16[2657088]{0:T(1024)(128)(2,1)} async-done(((bf16[2657088]{0:T(1024)(128)(2,1)}), bf16[2657088]{0:T(1024)(128)(2,1)}) %all-reduce.4.cloned.1.call-update) | async-done | bytes 5314192
  269.2 51.9 %reshape.250 = bf16[1,2657088]{1,0:T(2,128)(2,1)} reshape(bf16[2657088]{0:T(1024)(128)(2,1)} %all-reduce.4.cloned.1.call-done) | data formatting | bytes 10628352
  (1 shorter events, 0.0 us)
Async XLA Ops:
  7.2 114.6 %copy-start.2 = (u32[256]{0:T(256)S(1)}, u32[256]{0:T(256)}, u32[]{:S(2)}) copy-start(u32[256]{0:T(256)} %constant.70) | copy-start | bytes 3076
  7.2 115.8 %copy-start = (f32[1,83034]{1,0:T(1,128)S(1)}, f32[1,83034]{1,0:T(1,128)}, u32[]{:S(2)}) copy-start(f32[1,83034]{1,0:T(1,128)} %param.7) | copy-start | bytes 996412
  7.2 262.0 %all-reduce.4.cloned.1.call-start = ((), (), s32[]{:S(2)}) async-start(), calls=%async_computation | async-start | bytes 10629120
  121.1 25.4 %copy-start.1 = (f32[7]{0:T(128)}, f32[7]{0:T(128)S(1)}, u32[]{:S(2)}) copy-start(f32[7]{0:T(128)S(1)} %add_divide_fusion) | copy-start | bytes 88
Sparse Core Ops, SparseCore 0:
  150.5 118.6 all-reduce.3
where the time goes:
time: 329 us; the launch traced here: 328 us
  waiting for transfers between devices  119 us (36%)
  blocking collectives  81.6 us (25%)
  local copies, waits for them, and re-layouts  61.8 us (19%)
  other arithmetic  50.9 us (15%)
  between operations  14.7 us (4%)
    unnamed x2, waiting for transfers between devices  119 us
    psum x1, blocking collectives, on_device(): wsq, usq = lax.psum((wpart, upart), ('dp', 'mp'))  81.6 us
    unnamed x10, local copies, waits for them, and re-layouts  58.9 us
    convert_element_type x1, other arithmetic, on_device(): new_weights.astype(jnp.bfloat16)  20.9 us
    mul x1, other arithmetic, on_device(): upart = kind_sums(kind, raw * raw)  19.6 us
    select_n x1, other arithmetic, tensor_kind(): result = jnp.where(slot == number, order[number], result)  8.48 us
  transfers between devices with their start and end apart: 1, of which 1 were waited for; matrix products, arithmetic and copies ran while one was open for 0% of the time, Pallas kernels for 0%

commit v1 on v0

--- a/solution.py
+++ b/solution.py
@@ -44,6 +44,24 @@
     return jnp.sum(jnp.where(kind == kinds, values, 0.0), axis=1)
 
 
+def tree_sum(x, axis):
+    size = lax.axis_size(axis)
+    step = 1
+    while step < size:
+        pairs = [(i, i ^ step) for i in range(size)]
+        x = x + lax.ppermute(x, axis, pairs)
+        step *= 2
+    return x
+
+
+def gather_row(piece, axis):
+    width = piece.shape[1]
+    padded = -(-width // 2048) * 2048
+    dense = jnp.pad(piece[0], (0, padded - width)).reshape(padded // 128, 128)
+    whole = lax.all_gather(dense, axis, axis=0, tiled=False)
+    return whole.reshape(whole.shape[0], padded)[:, :width].reshape(1, -1)
+
+
 def on_device(weights, moment_first, moment_second, gradients, tensor_order):
     parts = lax.axis_size("mp")
     width = weights.shape[1]
@@ -56,11 +74,12 @@
     decay = per_entry(kind, jnp.array(decay_values, jnp.float32))
     raw = new_first / fix_first / (jnp.sqrt(new_second / fix_second) + 1e-06) + decay * weights
     upart = kind_sums(kind, raw * raw)
-    wsq, usq = lax.psum((wpart, upart), ("dp", "mp"))
+    both = tree_sum(tree_sum(jnp.concatenate([wpart, upart]), "dp"), "mp")
+    wsq, usq = both[:SLOTS], both[SLOTS:]
     trust = jnp.sqrt(wsq) / (jnp.sqrt(usq) + 1e-06)
     scaled_update = per_entry(kind, trust) * raw
     new_weights = weights - step_rate * scaled_update
-    training_copy = lax.all_gather(new_weights.astype(jnp.bfloat16), "dp", axis=1, tiled=True)
+    training_copy = gather_row(new_weights.astype(jnp.bfloat16), "dp")
     return (new_weights, new_first, new_second, scaled_update, training_copy, trust)
 
 

time: 329 us -> 231 us (0.70)
  blocking collectives: 81.6 us -> 0 us
  waiting for transfers between devices: 119 us -> 78.6 us
  local copies, waits for them, and re-layouts: 61.8 us -> 74 us
  starting transfers between devices: 0.04 us -> 12.2 us
    unnamed x2 -> x1, waiting for transfers between devices: 119 us -> 0.02 us
    psum x1 -> x0, blocking collectives: 81.6 us -> none  [on_device(): wsq, usq = lax.psum((wpart, upart), ('dp', 'mp'))]
    all_gather x0 -> x1, waiting for transfers between devices: none -> 62 us  [gather_row(): whole = lax.all_gather(dense, axis, axis=0, tiled=False)]
    reshape x0 -> x1, local copies, waits for them, and re-layouts: none -> 51.9 us  [gather_row(): return whole.reshape(whole.shape[0], padded)[:, :width].reshape(1, -1)]
    unnamed x10 -> x6, local copies, waits for them, and re-layouts: 58.9 us -> 15.8 us
    ppermute x0 -> x8, waiting for transfers between devices: none -> 16.6 us  [tree_sum(): x = x + lax.ppermute(x, axis, pairs)]
    ppermute x0 -> x8, starting transfers between devices: none -> 12.1 us  [tree_sum(): x = x + lax.ppermute(x, axis, pairs)]
  transfers between devices with their start and end apart: 1 -> 9, of which waited for: 1 -> 9; matrix products, arithmetic and copies ran while one was open for 0% -> 0% of each run, Pallas kernels for 0% -> 0%
where the time goes in v1:
time: 231 us; the launch traced here: 230 us
  waiting for transfers between devices  78.6 us (34%)
  local copies, waits for them, and re-layouts  74 us (32%)
  other arithmetic  51.1 us (22%)
  between operations  14.1 us (6%)
  starting transfers between devices  12.2 us (5%)
    all_gather x1, waiting for transfers between devices, gather_row(): whole = lax.all_gather(dense, axis, axis=0, tiled=False)  62 us
    reshape x1, local copies, waits for them, and re-layouts, gather_row(): return whole.reshape(whole.shape[0], padded)[:, :width].reshape(1, -1)  51.9 us
    convert_element_type x1, other arithmetic, on_device(): training_copy = gather_row(new_weights.astype(jnp.bfloat16), 'dp')  20.9 us
    mul x1, other arithmetic, on_device(): upart = kind_sums(kind, raw * raw)  19.6 us
    ppermute x8, waiting for transfers between devices, tree_sum(): x = x + lax.ppermute(x, axis, pairs)  16.6 us
    unnamed x6, local copies, waits for them, and re-layouts  15.8 us
    ppermute x8, starting transfers between devices, tree_sum(): x = x + lax.ppermute(x, axis, pairs)  12.1 us
    select_n x1, other arithmetic, tensor_kind(): result = jnp.where(slot == number, order[number], result)  8.48 us
  transfers between devices with their start and end apart: 9, of which 9 were waited for; matrix products, arithmetic and copies ran while one was open for 0% of the time, Pallas kernels for 0%

profile of v1, /device:TPU:1, one launch (start us, length us, event | category | flops | bytes accessed | tf_op | source)
XLA Modules:
  0.0 230.0 jit_solution(13813029866252390763)
XLA Ops:
  7.2 0.0 copy-start
  7.2 0.0 all-gather.2.cloned.1.call-start
  7.2 1.6 fusion.20
  8.8 0.9 select_reduce_fusion.2
  9.7 0.2 reduce-window.4
  9.8 0.7 fusion.19
  10.5 8.5 %select_select_fusion = s32[83034]{0:T(1024)S(1)} fusion(s32[]{:T(128)} %bitcast.13, s32[]{:T(128)} %bitcast.12, s32[]{:T(128)} %bitcast.11, s32[]{:T(128)} %bitcast.10, s32[]{:T(128)} %bitcast.9, s32[]{:T(128)} %bitcast.8, s32[]{:T(128)} %bitcast.7, s32[]{:T(128)} %bitcast.6, s32[]{:T(128)} %bitcast.5, s32[]{:T(128)} %bitcast.4, s32[]{:T(128)} %bitcast.3, ...), kind=kLoop, calls=%fused_computation.32 | loop fusion | flops 2657088 | bytes 332192 | tf_op jit(solution)/shard_map/jit(_where)/select_n | solution.py:31
  19.0 19.6 %multiply_reduce_fusion = (f32[83034]{0:T(1024)S(1)}, f32[1,83034]{1,0:T(1,128)S(1)}, f32[1,83034]{1,0:T(1,128)}, f32[1,83034]{1,0:T(1,128)}, f32[83034]{0:T(1024)S(1)}) fusion(f32[1,83034]{1,0:T(1,128)} %param.7, s32[]{:T(128)} %bitcast.13, s32[]{:T(128)} %bitcast.12, s32[]{:T(128)} %bitcast.11, s32[]{:T(128)} %bitcast.10, s32[]{:T(128)} %bitcast.9, ...), kind=kLoop, calls=%fused_computation.52 | loop fusion | flops 5065074 | bytes 2823212 | tf_op jit(solution)/shard_map/mul | solution.py:76
  38.6 0.9 select_reduce_fusion.1
  39.5 0.1 pad_maximum_fusion
  39.6 3.2 %collective-permute-start = (f32[14]{0:T(128)S(1)}, f32[14]{0:T(128)S(1)}, u32[]{:S(2)}, u32[]{:S(2)}) collective-permute-start(f32[14]{0:T(128)S(1)} %pad_maximum_fusion), channel_id=1, source_target_pairs={{0,8},{8,0},{16,24},{24,16},{32,40},{40,32},{48,56},{56,48},{64,72... | collective-permute-start | bytes 176 | tf_op jit(solution)/shard_map/ppermute | solution.py:52
  42.8 0.8 collective-permute-done
  43.6 0.1 fusion.21
  43.7 0.0 collective-permute-start.1
  43.7 2.4 %collective-permute-done.1 = f32[14]{0:T(128)S(1)} collective-permute-done((f32[14]{0:T(128)S(1)}, f32[14]{0:T(128)S(1)}, u32[]{:S(2)}, u32[]{:S(2)}) %collective-permute-start.1) | collective-permute-done | bytes 88 | tf_op jit(solution)/shard_map/ppermute | solution.py:52
  46.1 1.0 collective-permute-start.2
  47.1 2.9 %collective-permute-done.2 = f32[14]{0:T(128)S(1)} collective-permute-done((f32[14]{0:T(128)S(1)}, f32[14]{0:T(128)S(1)}, u32[]{:S(2)}, u32[]{:S(2)}) %collective-permute-start.2) | collective-permute-done | bytes 88 | tf_op jit(solution)/shard_map/ppermute | solution.py:52
  50.0 0.0 collective-permute-start.3
  50.0 2.4 %collective-permute-done.3 = f32[14]{0:T(128)S(1)} collective-permute-done((f32[14]{0:T(128)S(1)}, f32[14]{0:T(128)S(1)}, u32[]{:S(2)}, u32[]{:S(2)}) %collective-permute-start.3) | collective-permute-done | bytes 88 | tf_op jit(solution)/shard_map/ppermute | solution.py:52
  52.5 1.2 collective-permute-start.4
  53.7 2.7 %collective-permute-done.4 = f32[14]{0:T(128)S(1)} collective-permute-done((f32[14]{0:T(128)S(1)}, f32[14]{0:T(128)S(1)}, u32[]{:S(2)}, u32[]{:S(2)}) %collective-permute-start.4) | collective-permute-done | bytes 88 | tf_op jit(solution)/shard_map/ppermute | solution.py:52
  56.4 0.0 collective-permute-start.5
  56.4 2.4 %collective-permute-done.5 = f32[14]{0:T(128)S(1)} collective-permute-done((f32[14]{0:T(128)S(1)}, f32[14]{0:T(128)S(1)}, u32[]{:S(2)}, u32[]{:S(2)}) %collective-permute-start.5) | collective-permute-done | bytes 88 | tf_op jit(solution)/shard_map/ppermute | solution.py:52
  58.8 1.5 collective-permute-start.6
  60.3 1.9 collective-permute-done.6
  62.1 5.2 %collective-permute-start.7 = (f32[14]{0:T(128)S(1)}, f32[14]{0:T(128)S(1)}, u32[]{:S(2)}, u32[]{:S(2)}) collective-permute-start(f32[14]{0:T(128)S(1)} %add.194), channel_id=1, source_target_pairs={{0,4},{1,5},{2,6},{3,7},{4,0},{5,1},{6,2},{7,3},{8,12},{9,13},{10,... | collective-permute-start | bytes 176 | tf_op jit(solution)/shard_map/ppermute | solution.py:52
  67.3 1.1 collective-permute-done.7
  68.5 0.1 add_divide_fusion
  68.5 0.0 copy-start.1
  68.6 0.7 fusion.18
  69.2 0.0 copy-done
  69.2 20.9 %convert_reduce_fusion = (bf16[83034]{0:T(1024)(128)(2,1)S(1)}, f32[1,83034]{1,0:T(1,128)}, f32[1,83034]{1,0:T(1,128)}) fusion(f32[1,83034]{1,0:T(1,128)S(1)} %copy-done, f32[1,83034]{1,0:T(1,128)S(1)} %get-tuple-element.12, f32[]{:T(128)} %bitcast.20, f32[]{:T(128)} %bitcast.19, f32[]{:T(128)} %bitcast.18, f32[]{:T(128)} %bitcast.17, f32[]{:T(128)} %bitcast.16, ...), kind=kLoop, calls=%fused_computation.50 | loop fusion | flops 4151700 | bytes 1494696 | tf_op jit(solution)/shard_map/convert_element_type | solution.py:82
  90.1 0.7 pad_bitcast_fusion
  90.8 0.0 all-gather.2.cloned.1.call-update
  90.8 62.0 %all-gather.2.cloned.1.call-done = bf16[32,656,128]{2,1,0:T(8,128)(2,1)} async-done(((bf16[1,656,128]{2,1,0:T(8,128)(2,1)}), bf16[32,656,128]{2,1,0:T(8,128)(2,1)}) %all-gather.2.cloned.1.call-update) | async-done | bytes 5373968 | tf_op jit(solution)/shard_map/all_gather | solution.py:61
  152.8 3.9 %copy.15 = bf16[4,8,656,128]{3,1,2,0:T(8,128)(2,1)S(1)} copy(bf16[4,8,656,128]{3,2,1,0:T(8,128)(2,1)} %bitcast.28) | data formatting | bytes 10747904
  156.7 0.0 copy-done.1
  156.7 2.7 %slice.126 = bf16[32,83034]{1,0:T(8,128)(2,1)} slice(bf16[32,83968]{1,0:T(8,128)(2,1)S(1)} %bitcast.27), slice={[0:32], [0:83034]} | slice | bytes 10628352 | tf_op jit(solution)/shard_map/slice | solution.py:62
  159.4 11.9 %reshape.259 = bf16[2657088]{0:T(1024)(128)(2,1)} reshape(bf16[32,83034]{1,0:T(8,128)(2,1)} %slice.126) | data formatting | bytes 10628352
  171.3 51.9 %reshape.255 = bf16[1,2657088]{1,0:T(2,128)(2,1)} reshape(bf16[2657088]{0:T(1024)(128)(2,1)} %reshape.259) | data formatting | bytes 10628352 | tf_op jit(solution)/shard_map/reshape | solution.py:62
  (7 shorter events, 0.0 us)
Async XLA Ops:
  7.2 62.1 %copy-start = (f32[1,83034]{1,0:T(1,128)S(1)}, f32[1,83034]{1,0:T(1,128)}, u32[]{:S(2)}) copy-start(f32[1,83034]{1,0:T(1,128)} %param.7) | copy-start | bytes 996412
  7.2 145.6 %all-gather.2.cloned.1.call-start = ((), (), s32[]{:S(2)}) async-start(), calls=%async_computation | async-start | bytes 5541888 | tf_op jit(solution)/shard_map/all_gather | solution.py:61
  39.6 4.0 %collective-permute-start = (f32[14]{0:T(128)S(1)}, f32[14]{0:T(128)S(1)}, u32[]{:S(2)}, u32[]{:S(2)}) collective-permute-start(f32[14]{0:T(128)S(1)} %pad_maximum_fusion), channel_id=1, source_target_pairs={{0,8},{8,0},{16,24},{24,16},{32,40},{40,32},{48,56},{56,48},{64,72... | collective-permute-start | bytes 176 | tf_op jit(solution)/shard_map/ppermute | solution.py:52
  43.7 2.4 %collective-permute-start.1 = (f32[14]{0:T(128)S(1)}, f32[14]{0:T(128)S(1)}, u32[]{:S(2)}, u32[]{:S(2)}) collective-permute-start(f32[14]{0:T(128)S(1)} %fusion.21), channel_id=1, source_target_pairs={{0,16},{8,24},{16,0},{24,8},{32,48},{40,56},{48,32},{56,40},{64,80... | collective-permute-start | bytes 176 | tf_op jit(solution)/shard_map/ppermute | solution.py:52
  46.1 3.9 %collective-permute-start.2 = (f32[14]{0:T(128)S(1)}, f32[14]{0:T(128)S(1)}, u32[]{:S(2)}, u32[]{:S(2)}) collective-permute-start(f32[14]{0:T(128)S(1)} %add.189), channel_id=1, source_target_pairs={{0,32},{8,40},{16,48},{24,56},{32,0},{40,8},{48,16},{56,24},{64,96... | collective-permute-start | bytes 176 | tf_op jit(solution)/shard_map/ppermute | solution.py:52
  50.0 2.4 %collective-permute-start.3 = (f32[14]{0:T(128)S(1)}, f32[14]{0:T(128)S(1)}, u32[]{:S(2)}, u32[]{:S(2)}) collective-permute-start(f32[14]{0:T(128)S(1)} %add.190), channel_id=1, source_target_pairs={{0,64},{8,72},{16,80},{24,88},{32,96},{40,104},{48,112},{56,120},{... | collective-permute-start | bytes 176 | tf_op jit(solution)/shard_map/ppermute | solution.py:52
  52.5 3.9 %collective-permute-start.4 = (f32[14]{0:T(128)S(1)}, f32[14]{0:T(128)S(1)}, u32[]{:S(2)}, u32[]{:S(2)}) collective-permute-start(f32[14]{0:T(128)S(1)} %add.191), channel_id=1, source_target_pairs={{0,128},{8,136},{16,144},{24,152},{32,160},{40,168},{48,176},{56,1... | collective-permute-start | bytes 176 | tf_op jit(solution)/shard_map/ppermute | solution.py:52
  56.4 2.4 %collective-permute-start.5 = (f32[14]{0:T(128)S(1)}, f32[14]{0:T(128)S(1)}, u32[]{:S(2)}, u32[]{:S(2)}) collective-permute-start(f32[14]{0:T(128)S(1)} %add.192), channel_id=1, source_target_pairs={{0,1},{1,0},{2,3},{3,2},{4,5},{5,4},{6,7},{7,6},{8,9},{9,8},{10,11... | collective-permute-start | bytes 176 | tf_op jit(solution)/shard_map/ppermute | solution.py:52
  58.8 3.3 %collective-permute-start.6 = (f32[14]{0:T(128)S(1)}, f32[14]{0:T(128)S(1)}, u32[]{:S(2)}, u32[]{:S(2)}) collective-permute-start(f32[14]{0:T(128)S(1)} %add.193), channel_id=1, source_target_pairs={{0,2},{1,3},{2,0},{3,1},{4,6},{5,7},{6,4},{7,5},{8,10},{9,11},{10,... | collective-permute-start | bytes 176 | tf_op jit(solution)/shard_map/ppermute | solution.py:52
  62.1 6.3 %collective-permute-start.7 = (f32[14]{0:T(128)S(1)}, f32[14]{0:T(128)S(1)}, u32[]{:S(2)}, u32[]{:S(2)}) collective-permute-start(f32[14]{0:T(128)S(1)} %add.194), channel_id=1, source_target_pairs={{0,4},{1,5},{2,6},{3,7},{4,0},{5,1},{6,2},{7,3},{8,12},{9,13},{10,... | collective-permute-start | bytes 176 | tf_op jit(solution)/shard_map/ppermute | solution.py:52
  68.5 88.1 %copy-start.1 = (f32[7]{0:T(128)}, f32[7]{0:T(128)S(1)}, u32[]{:S(2)}) copy-start(f32[7]{0:T(128)S(1)} %add_divide_fusion) | copy-start | bytes 88
Sparse Core Ops, SparseCore 0:
  90.9 61.8 all-gather.1

commit v2 on v1

--- a/solution.py
+++ b/solution.py
@@ -40,8 +40,7 @@
 
 
 def kind_sums(kind, values):
-    kinds = jnp.arange(SLOTS, dtype=jnp.int32)[:, None]
-    return jnp.sum(jnp.where(kind == kinds, values, 0.0), axis=1)
+    return jnp.stack([jnp.sum(jnp.where(kind == k, values, 0.0)) for k in range(SLOTS)])
 
 
 def tree_sum(x, axis):
@@ -54,33 +53,50 @@
     return x
 
 
-def gather_row(piece, axis):
-    width = piece.shape[1]
-    padded = -(-width // 2048) * 2048
-    dense = jnp.pad(piece[0], (0, padded - width)).reshape(padded // 128, 128)
-    whole = lax.all_gather(dense, axis, axis=0, tiled=False)
-    return whole.reshape(whole.shape[0], padded)[:, :width].reshape(1, -1)
+def to_dense(row, padded):
+    return jnp.pad(row[0], (0, padded - row.shape[1])).reshape(padded // 128, 128)
+
+
+def from_dense(block, width):
+    return block.reshape(-1)[:width].reshape(1, width)
 
 
 def on_device(weights, moment_first, moment_second, gradients, tensor_order):
     parts = lax.axis_size("mp")
     width = weights.shape[1]
-    places = lax.axis_index("dp") * width + lax.broadcasted_iota(jnp.int32, (1, width), 1)
+    padded = -(-width // 2048) * 2048
+    w = to_dense(weights, padded)
+    m1 = to_dense(moment_first, padded)
+    m2 = to_dense(moment_second, padded)
+    grads = to_dense(gradients, padded).astype(jnp.float32)
+    rows = padded // 128
+    places = (
+        lax.axis_index("dp") * width
+        + lax.broadcasted_iota(jnp.int32, (rows, 128), 0) * 128
+        + lax.broadcasted_iota(jnp.int32, (rows, 128), 1)
+    )
     kind = tensor_kind(places, tensor_order, parts)
-    wpart = kind_sums(kind, weights * weights)
-    grads = gradients.astype(jnp.float32)
-    new_first = 0.9 * moment_first + 0.1 * grads
-    new_second = 0.999 * moment_second + 0.001 * grads * grads
+    new_first = 0.9 * m1 + 0.1 * grads
+    new_second = 0.999 * m2 + 0.001 * grads * grads
     decay = per_entry(kind, jnp.array(decay_values, jnp.float32))
-    raw = new_first / fix_first / (jnp.sqrt(new_second / fix_second) + 1e-06) + decay * weights
+    raw = new_first / fix_first / (jnp.sqrt(new_second / fix_second) + 1e-06) + decay * w
+    wpart = kind_sums(kind, w * w)
     upart = kind_sums(kind, raw * raw)
     both = tree_sum(tree_sum(jnp.concatenate([wpart, upart]), "dp"), "mp")
     wsq, usq = both[:SLOTS], both[SLOTS:]
     trust = jnp.sqrt(wsq) / (jnp.sqrt(usq) + 1e-06)
     scaled_update = per_entry(kind, trust) * raw
-    new_weights = weights - step_rate * scaled_update
-    training_copy = gather_row(new_weights.astype(jnp.bfloat16), "dp")
-    return (new_weights, new_first, new_second, scaled_update, training_copy, trust)
+    new_weights = w - step_rate * scaled_update
+    whole = lax.all_gather(new_weights.astype(jnp.bfloat16), "dp", axis=0, tiled=False)
+    training_copy = whole.reshape(whole.shape[0], padded)[:, :width].reshape(1, -1)
+    return (
+        from_dense(new_weights, width),
+        from_dense(new_first, width),
+        from_dense(new_second, width),
+        from_dense(scaled_update, width),
+        training_copy,
+        trust,
+    )
 
 
 def solution(mesh):

time: 231 us -> 221 us (0.957)
  other arithmetic: 51.1 us -> 37.4 us
  local copies, waits for them, and re-layouts: 74 us -> 86.1 us
  waiting for transfers between devices: 78.6 us -> 70.1 us
    mul x1, other arithmetic: 19.6 us -> 4.64 us  [on_device(): scaled_update = per_entry(kind, trust) * raw]
    reduce_sum x1, other arithmetic: 0.89 us -> 10.2 us  [kind_sums(): jnp.sum(jnp.where(kind == k, values, 0.0))]
    concatenate x0 -> x1, local copies, waits for them, and re-layouts: none -> 8.93 us  [on_device(): both = tree_sum(tree_sum(jnp.concatenate([wpart, upart]), 'dp'), 'mp')]
    all_gather x1, waiting for transfers between devices: 62 us -> 53.4 us  [on_device(): lax.all_gather(new_weights.astype(jnp.bfloat16), 'dp', axis=0, tiled=False)]
    select_n x1 -> x0, other arithmetic: 8.48 us -> none  [tensor_kind(): result = jnp.where(slot == number, order[number], result)]
    unnamed x0 -> x4, other arithmetic: none -> 7.22 us
    convert_element_type x1, other arithmetic: 20.9 us -> 14.1 us  [on_device(): new_weights.astype(jnp.bfloat16)]
    reshape x1 -> x5, local copies, waits for them, and re-layouts: 51.9 us -> 55.7 us  [the longest x1 51.9 us: on_device(): whole.reshape(whole.shape[0], padded)[:, :width].reshape(1, -1)]
  transfers between devices with their start and end apart: 9 -> 9, of which waited for: 9 -> 9; matrix products, arithmetic and copies ran while one was open for 0% -> 4% of each run, Pallas kernels for 0% -> 0%
where the time goes in v2:
time: 221 us; the launch traced here: 220 us
  local copies, waits for them, and re-layouts  86.1 us (39%)
  waiting for transfers between devices  70.1 us (32%)
  other arithmetic  37.4 us (17%)
  between operations  14.1 us (6%)
  starting transfers between devices  12.2 us (6%)
    all_gather x1, waiting for transfers between devices, on_device(): lax.all_gather(new_weights.astype(jnp.bfloat16), 'dp', axis=0, tiled=False)  53.4 us
    reshape x1, local copies, waits for them, and re-layouts, on_device(): whole.reshape(whole.shape[0], padded)[:, :width].reshape(1, -1)  51.9 us
    ppermute x8, waiting for transfers between devices, tree_sum(): x = x + lax.ppermute(x, axis, pairs)  16.7 us
    unnamed x4, local copies, waits for them, and re-layouts  15.8 us
    convert_element_type x1, other arithmetic, on_device(): new_weights.astype(jnp.bfloat16)  14.1 us
    ppermute x8, starting transfers between devices, tree_sum(): x = x + lax.ppermute(x, axis, pairs)  12.2 us
    reduce_sum x1, other arithmetic, kind_sums(): jnp.sum(jnp.where(kind == k, values, 0.0))  10.2 us
    concatenate x1, local copies, waits for them, and re-layouts, on_device(): both = tree_sum(tree_sum(jnp.concatenate([wpart, upart]), 'dp'), 'mp')  8.93 us
  transfers between devices with their start and end apart: 9, of which 9 were waited for; matrix products, arithmetic and copies ran while one was open for 4% of the time, Pallas kernels for 0%

profile of v2, /device:TPU:1, one launch (start us, length us, event | category | flops | bytes accessed | tf_op | source)
XLA Modules:
  0.0 219.9 jit_solution(67019762102073822)
XLA Ops:
  7.2 0.0 all-gather.2.cloned.1.call-start
  7.2 1.6 fusion.32
  8.8 0.9 select_reduce_fusion.14
  9.7 0.2 reduce-window.4
  9.8 0.7 fusion.31
  10.5 1.8 reduce.14
  12.3 1.8 reduce.15
  14.1 1.8 reduce.17
  15.9 1.9 reduce.16
  17.8 10.2 %select_reduce_fusion.7 = (f32[]{:T(128)}, f32[]{:T(128)}, f32[]{:T(128)}, f32[]{:T(128)}, f32[]{:T(128)}, /*index=5*/f32[]{:T(128)}, f32[]{:T(128)}, f32[]{:T(1...) fusion(f32[83034]{0:T(1024)S(1)} %reduce.14, ...), kind=kLoop, calls=%fused_computation.44 | loop fusion | flops 7473138 | bytes 2760600 | tf_op jit(solution)/shard_map/reduce_sum | solution.py:43
  28.0 8.9 %concatenate.3 = f32[14]{0:T(128)S(1)} concatenate(f32[1]{0:T(128)} %bitcast.17, f32[1]{0:T(128)} %bitcast.18, f32[1]{0:T(128)} %bitcast.19, f32[1]{0:T(128)} %bitcast.20, f32[1]{0:T(128)} %bitcast.21, f32[1]{0:T(128)} %bitcast.22, f32[1]{0:T(128)} %bitcast.23, f32[1]{0:T(128)} %bitcast.24, f32[1]{0:T(128)} %bitcast.25, f32[1]{0:T(128)} %bitcast.26, f32[1]{0:T(128)} %bitcast.27, ...), dimensions={0} | concatenate | bytes 112 | tf_op jit(solution)/shard_map/concatenate | solution.py:85
  36.9 3.3 %collective-permute-start = (f32[14]{0:T(128)S(1)}, f32[14]{0:T(128)S(1)}, u32[]{:S(2)}, u32[]{:S(2)}) collective-permute-start(f32[14]{0:T(128)S(1)} %concatenate.3), channel_id=1, source_target_pairs={{0,8},{8,0},{16,24},{24,16},{32,40},{40,32},{48,56},{56,48},{64,72... | collective-permute-start | bytes 176 | tf_op jit(solution)/shard_map/ppermute | solution.py:51
  40.2 0.8 collective-permute-done
  41.0 0.0 collective-permute-start.1
  41.0 2.4 %collective-permute-done.1 = f32[14]{0:T(128)S(1)} collective-permute-done((f32[14]{0:T(128)S(1)}, f32[14]{0:T(128)S(1)}, u32[]{:S(2)}, u32[]{:S(2)}) %collective-permute-start.1) | collective-permute-done | bytes 88 | tf_op jit(solution)/shard_map/ppermute | solution.py:51
  43.4 1.0 collective-permute-start.2
  44.5 2.9 %collective-permute-done.2 = f32[14]{0:T(128)S(1)} collective-permute-done((f32[14]{0:T(128)S(1)}, f32[14]{0:T(128)S(1)}, u32[]{:S(2)}, u32[]{:S(2)}) %collective-permute-start.2) | collective-permute-done | bytes 88 | tf_op jit(solution)/shard_map/ppermute | solution.py:51
  47.4 0.0 collective-permute-start.3
  47.4 2.4 %collective-permute-done.3 = f32[14]{0:T(128)S(1)} collective-permute-done((f32[14]{0:T(128)S(1)}, f32[14]{0:T(128)S(1)}, u32[]{:S(2)}, u32[]{:S(2)}) %collective-permute-start.3) | collective-permute-done | bytes 88 | tf_op jit(solution)/shard_map/ppermute | solution.py:51
  49.8 1.2 collective-permute-start.4
  51.0 2.7 %collective-permute-done.4 = f32[14]{0:T(128)S(1)} collective-permute-done((f32[14]{0:T(128)S(1)}, f32[14]{0:T(128)S(1)}, u32[]{:S(2)}, u32[]{:S(2)}) %collective-permute-start.4) | collective-permute-done | bytes 88 | tf_op jit(solution)/shard_map/ppermute | solution.py:51
  53.7 0.0 collective-permute-start.5
  53.7 2.4 %collective-permute-done.5 = f32[14]{0:T(128)S(1)} collective-permute-done((f32[14]{0:T(128)S(1)}, f32[14]{0:T(128)S(1)}, u32[]{:S(2)}, u32[]{:S(2)}) %collective-permute-start.5) | collective-permute-done | bytes 88 | tf_op jit(solution)/shard_map/ppermute | solution.py:51
  56.1 1.5 collective-permute-start.6
  57.6 1.9 collective-permute-done.6
  59.4 5.2 %collective-permute-start.7 = (f32[14]{0:T(128)S(1)}, f32[14]{0:T(128)S(1)}, u32[]{:S(2)}, u32[]{:S(2)}) collective-permute-start(f32[14]{0:T(128)S(1)} %add.340), channel_id=1, source_target_pairs={{0,4},{1,5},{2,6},{3,7},{4,0},{5,1},{6,2},{7,3},{8,12},{9,13},{10,... | collective-permute-start | bytes 176 | tf_op jit(solution)/shard_map/ppermute | solution.py:51
  64.7 1.1 collective-permute-done.7
  65.8 0.1 add_divide_fusion
  65.9 0.0 copy-start
  65.9 0.7 fusion.30
  66.5 14.1 %fusion.26 = bf16[1,656,128]{2,1,0:T(8,128)(2,1)} fusion(f32[83034]{0:T(1024)S(1)} %reduce.15, f32[83034]{0:T(1024)S(1)} %reduce.17, f32[83034]{0:T(1024)S(1)} %reduce.14, f32[]{:T(128)} %bitcast.37, f32[]{:T(128)} %bitcast.36, f32[]{:T(128)} %bitcast.35, f32[]{:T(128)} %bitcast.34, f32[]{:T(128)} %bitcast.33, f32[]{:T(128)} %bitcast.32, f32[]{:T(128)} %bitcast.31, ...), kind=kLoop, calls=%fused_computation.58 | loop fusion | flops 5877760 | bytes 1333116 | tf_op jit(solution)/shard_map/convert_element_type | solution.py:90
  80.6 0.0 all-gather.2.cloned.1.call-update
  80.7 1.0 reshape.393
  81.6 1.0 reshape.392
  82.6 4.6 %select_multiply_fusion = f32[83968]{0:T(1024)S(1)} fusion(f32[83968]{0:T(1024)S(1)} %get-tuple-element.27, pred[83968]{0:T(1024)(128)(4,1)S(1)} %get-tuple-element.36, pred[83968]{0:T(1024)(128)(4,1)S(1)} %get-tuple-element.35, pred[83968]{0:T(1024)(128)(4,1)S(1)} %get-tuple-element.34, pred[83968]{0:T(1024)(128)(4,1)S(1)} %get-tuple-element.33, ...), kind=kLoop, calls=%fused_computation.33 | loop fusion | flops 671744 | bytes 1259548 | tf_op jit(solution)/shard_map/mul | solution.py:88
  87.3 1.0 reshape.394
  88.2 1.0 reshape.391
  89.2 53.4 %all-gather.2.cloned.1.call-done = bf16[32,656,128]{2,1,0:T(8,128)(2,1)} async-done(((bf16[1,656,128]{2,1,0:T(8,128)(2,1)}), bf16[32,656,128]{2,1,0:T(8,128)(2,1)}) %all-gather.2.cloned.1.call-update) | async-done | bytes 5373968 | tf_op jit(solution)/shard_map/all_gather | solution.py:90
  142.6 3.9 %copy.15 = bf16[4,8,656,128]{3,1,2,0:T(8,128)(2,1)S(1)} copy(bf16[4,8,656,128]{3,2,1,0:T(8,128)(2,1)} %bitcast.95) | data formatting | bytes 10747904
  146.5 0.0 copy-done
  146.5 2.7 %slice.146 = bf16[32,83034]{1,0:T(8,128)(2,1)} slice(bf16[32,83968]{1,0:T(8,128)(2,1)S(1)} %bitcast.94), slice={[0:32], [0:83034]} | slice | bytes 10628352 | tf_op jit(solution)/shard_map/slice | solution.py:91
  149.3 11.9 %reshape.439 = bf16[2657088]{0:T(1024)(128)(2,1)} reshape(bf16[32,83034]{1,0:T(8,128)(2,1)} %slice.146) | data formatting | bytes 10628352
  161.2 51.9 %reshape.397 = bf16[1,2657088]{1,0:T(2,128)(2,1)} reshape(bf16[2657088]{0:T(1024)(128)(2,1)} %reshape.439) | data formatting | bytes 10628352 | tf_op jit(solution)/shard_map/reshape | solution.py:91
  (10 shorter events, 0.1 us)
Async XLA Ops:
  7.2 135.5 %all-gather.2.cloned.1.call-start = ((), (), s32[]{:S(2)}) async-start(), calls=%async_computation | async-start | bytes 5541888 | tf_op jit(solution)/shard_map/all_gather | solution.py:90
  36.9 4.1 %collective-permute-start = (f32[14]{0:T(128)S(1)}, f32[14]{0:T(128)S(1)}, u32[]{:S(2)}, u32[]{:S(2)}) collective-permute-start(f32[14]{0:T(128)S(1)} %concatenate.3), channel_id=1, source_target_pairs={{0,8},{8,0},{16,24},{24,16},{32,40},{40,32},{48,56},{56,48},{64,72... | collective-permute-start | bytes 176 | tf_op jit(solution)/shard_map/ppermute | solution.py:51
  41.0 2.4 %collective-permute-start.1 = (f32[14]{0:T(128)S(1)}, f32[14]{0:T(128)S(1)}, u32[]{:S(2)}, u32[]{:S(2)}) collective-permute-start(f32[14]{0:T(128)S(1)} %add.334), channel_id=1, source_target_pairs={{0,16},{8,24},{16,0},{24,8},{32,48},{40,56},{48,32},{56,40},{64,80... | collective-permute-start | bytes 176 | tf_op jit(solution)/shard_map/ppermute | solution.py:51
  43.4 3.9 %collective-permute-start.2 = (f32[14]{0:T(128)S(1)}, f32[14]{0:T(128)S(1)}, u32[]{:S(2)}, u32[]{:S(2)}) collective-permute-start(f32[14]{0:T(128)S(1)} %add.335), channel_id=1, source_target_pairs={{0,32},{8,40},{16,48},{24,56},{32,0},{40,8},{48,16},{56,24},{64,96... | collective-permute-start | bytes 176 | tf_op jit(solution)/shard_map/ppermute | solution.py:51
  47.4 2.4 %collective-permute-start.3 = (f32[14]{0:T(128)S(1)}, f32[14]{0:T(128)S(1)}, u32[]{:S(2)}, u32[]{:S(2)}) collective-permute-start(f32[14]{0:T(128)S(1)} %add.336), channel_id=1, source_target_pairs={{0,64},{8,72},{16,80},{24,88},{32,96},{40,104},{48,112},{56,120},{... | collective-permute-start | bytes 176 | tf_op jit(solution)/shard_map/ppermute | solution.py:51
  49.8 3.9 %collective-permute-start.4 = (f32[14]{0:T(128)S(1)}, f32[14]{0:T(128)S(1)}, u32[]{:S(2)}, u32[]{:S(2)}) collective-permute-start(f32[14]{0:T(128)S(1)} %add.337), channel_id=1, source_target_pairs={{0,128},{8,136},{16,144},{24,152},{32,160},{40,168},{48,176},{56,1... | collective-permute-start | bytes 176 | tf_op jit(solution)/shard_map/ppermute | solution.py:51
  53.7 2.4 %collective-permute-start.5 = (f32[14]{0:T(128)S(1)}, f32[14]{0:T(128)S(1)}, u32[]{:S(2)}, u32[]{:S(2)}) collective-permute-start(f32[14]{0:T(128)S(1)} %add.338), channel_id=1, source_target_pairs={{0,1},{1,0},{2,3},{3,2},{4,5},{5,4},{6,7},{7,6},{8,9},{9,8},{10,11... | collective-permute-start | bytes 176 | tf_op jit(solution)/shard_map/ppermute | solution.py:51
  56.1 3.3 %collective-permute-start.6 = (f32[14]{0:T(128)S(1)}, f32[14]{0:T(128)S(1)}, u32[]{:S(2)}, u32[]{:S(2)}) collective-permute-start(f32[14]{0:T(128)S(1)} %add.339), channel_id=1, source_target_pairs={{0,2},{1,3},{2,0},{3,1},{4,6},{5,7},{6,4},{7,5},{8,10},{9,11},{10,... | collective-permute-start | bytes 176 | tf_op jit(solution)/shard_map/ppermute | solution.py:51
  59.4 6.3 %collective-permute-start.7 = (f32[14]{0:T(128)S(1)}, f32[14]{0:T(128)S(1)}, u32[]{:S(2)}, u32[]{:S(2)}) collective-permute-start(f32[14]{0:T(128)S(1)} %add.340), channel_id=1, source_target_pairs={{0,4},{1,5},{2,6},{3,7},{4,0},{5,1},{6,2},{7,3},{8,12},{9,13},{10,... | collective-permute-start | bytes 176 | tf_op jit(solution)/shard_map/ppermute | solution.py:51
  65.9 80.7 %copy-start = (f32[7]{0:T(128)}, f32[7]{0:T(128)S(1)}, u32[]{:S(2)}) copy-start(f32[7]{0:T(128)S(1)} %add_divide_fusion) | copy-start | bytes 88
Sparse Core Ops, SparseCore 0:
  80.8 61.7 all-gather.1

commit v3 on v2

--- a/solution.py
+++ b/solution.py
@@ -40,7 +40,8 @@
 
 
 def kind_sums(kind, values):
-    return jnp.stack([jnp.sum(jnp.where(kind == k, values, 0.0)) for k in range(SLOTS)])
+    kinds = jnp.arange(SLOTS, dtype=jnp.int32)[:, None, None]
+    return jnp.sum(jnp.where(kind[None] == kinds, values[None], 0.0), axis=1)
 
 
 def tree_sum(x, axis):
@@ -83,6 +84,7 @@
     wpart = kind_sums(kind, w * w)
     upart = kind_sums(kind, raw * raw)
     both = tree_sum(tree_sum(jnp.concatenate([wpart, upart]), "dp"), "mp")
+    both = jnp.sum(both, axis=1)
     wsq, usq = both[:SLOTS], both[SLOTS:]
     trust = jnp.sqrt(wsq) / (jnp.sqrt(usq) + 1e-06)
     scaled_update = per_entry(kind, trust) * raw

time: 221 us -> 221 us (level)
  other arithmetic: 37.4 us -> 54 us
  local copies, waits for them, and re-layouts: 86.1 us -> 77.3 us
  waiting for transfers between devices: 70.1 us -> 61.9 us
    reduce_sum x1 -> x2, other arithmetic: 10.2 us -> 0.51 us  [the longest x1 0.4 us: kind_sums(): return jnp.sum(jnp.where(kind[None] == kinds, values[None], 0.0), axis=1)]
    mul x0 -> x1, other arithmetic: none -> 8.96 us  [on_device(): upart = kind_sums(kind, raw * raw)]
    concatenate x1 -> x0, local copies, waits for them, and re-layouts: 8.93 us -> none  [on_device(): both = tree_sum(tree_sum(jnp.concatenate([wpart, upart]), 'dp'), 'mp')]
    mul x1, other arithmetic: 4.64 us -> 13.4 us  [on_device(): scaled_update = per_entry(kind, trust) * raw]
    all_gather x1, waiting for transfers between devices: 53.4 us -> 44.7 us  [on_device(): lax.all_gather(new_weights.astype(jnp.bfloat16), 'dp', axis=0, tiled=False)]
    select_n x0 -> x1, other arithmetic: none -> 8.58 us  [tensor_kind(): result = jnp.where(slot == number, order[number], result)]
  transfers between devices with their start and end apart: 9 -> 9, of which waited for: 9 -> 9; matrix products, arithmetic and copies ran while one was open for 4% -> 8% of each run, Pallas kernels for 0% -> 0%
where the time goes in v3:
time: 221 us; the launch traced here: 220 us
  local copies, waits for them, and re-layouts  77.3 us (35%)
  waiting for transfers between devices  61.9 us (28%)
  other arithmetic  54 us (24%)
  between operations  14.1 us (6%)
  starting transfers between devices  12.3 us (6%)
    reshape x1, local copies, waits for them, and re-layouts, on_device(): whole.reshape(whole.shape[0], padded)[:, :width].reshape(1, -1)  51.9 us
    all_gather x1, waiting for transfers between devices, on_device(): lax.all_gather(new_weights.astype(jnp.bfloat16), 'dp', axis=0, tiled=False)  44.7 us
    ppermute x8, waiting for transfers between devices, tree_sum(): x = x + lax.ppermute(x, axis, pairs)  17.2 us
    unnamed x4, local copies, waits for them, and re-layouts  16 us
    convert_element_type x1, other arithmetic, on_device(): new_weights.astype(jnp.bfloat16)  14.1 us
    mul x1, other arithmetic, on_device(): scaled_update = per_entry(kind, trust) * raw  13.4 us
    ppermute x8, starting transfers between devices, tree_sum(): x = x + lax.ppermute(x, axis, pairs)  12.2 us
    mul x1, other arithmetic, on_device(): upart = kind_sums(kind, raw * raw)  8.96 us
  transfers between devices with their start and end apart: 9, of which 9 were waited for; matrix products, arithmetic and copies ran while one was open for 8% of the time, Pallas kernels for 0%

profile of v3, /device:TPU:1, one launch (start us, length us, event | category | flops | bytes accessed | tf_op | source)
XLA Modules:
  0.0 219.6 jit_solution(15064433684068417720)
XLA Ops:
  7.2 0.0 all-gather.2.cloned.1.call-start
  7.2 1.5 fusion.42
  8.7 0.9 select_reduce_fusion.2
  9.6 0.2 reduce-window.4
  9.8 0.7 fusion.41
  10.4 1.8 reduce
  12.2 1.8 reduce.1
  14.0 1.8 reduce.3
  15.8 1.9 reduce.2
  17.7 8.6 %select_select_fusion.2 = s32[656,128]{1,0:T(8,128)S(1)} fusion(s32[]{:T(128)} %bitcast.10, s32[]{:T(128)} %bitcast.8, s32[]{:T(128)} %bitcast.15, s32[]{:T(128)} %bitcast.14, s32[]{:T(128)} %bitcast.13, s32[]{:T(128)} %bitcast.12, s32[]{:T(128)} %bitcast.11, s32[]{:T(128)} %bitcast.6, s32[]{:T(128)} %bitcast.5, s32[]{:T(128)} %bitcast.4, s32[]{:T(128)} %bitcast.3, ...), kind=kLoop, calls=%fused_computation.53 | loop fusion | flops 2686976 | bytes 338548 | tf_op jit(solution)/shard_map/jit(_where)/select_n | solution.py:31
  26.2 9.0 %fusion.11 = (f32[656,128]{1,0:T(8,128)S(1)}, f32[656,128]{1,0:T(8,128)S(1)}) fusion(f32[83034]{0:T(1024)S(1)} %reduce, f32[83034]{0:T(1024)S(1)} %reduce.1, f32[83034]{0:T(1024)S(1)} %reduce.3, s32[]{:T(128)} %bitcast.15, s32[]{:T(128)} %bitcast.14, s32[]{:T(128)} %bitcast.13, s32[]{:T(128)} %bitcast.12, s32[]{:T(128)} %bitcast.11, s32[]{:T(128)} %bitcast.10, ...), kind=kLoop, calls=%fused_computation.22 | loop fusion | flops 5122048 | bytes 1836896 | tf_op jit(solution)/shard_map/mul | solution.py:85
  35.2 0.4 select_reduce_fusion.1
  35.6 3.3 %collective-permute-start = (f32[14,128]{1,0:T(8,128)S(1)}, f32[14,128]{1,0:T(8,128)S(1)}, u32[]{:S(2)}, u32[]{:S(2)}) collective-permute-start(f32[14,128]{1,0:T(8,128)S(1)} %pad_maximum_fusion), channel_id=1, source_target_pairs={{0,8},{8,0},{16,24},{24,16},{32,40},{40,32},{48,56},{56,48},{64,72... | collective-permute-start | bytes 21512 | tf_op jit(solution)/shard_map/ppermute | solution.py:52
  38.9 0.8 collective-permute-done
  39.8 0.0 collective-permute-start.1
  39.8 2.5 %collective-permute-done.1 = f32[14,128]{1,0:T(8,128)S(1)} collective-permute-done((f32[14,128]{1,0:T(8,128)S(1)}, f32[14,128]{1,0:T(8,128)S(1)}, u32[]{:S(2)}, u32[]{:S(2)}) %collective-permute-start.1) | collective-permute-done | bytes 7200 | tf_op jit(solution)/shard_map/ppermute | solution.py:52
  42.3 1.0 collective-permute-start.2
  43.3 3.0 %collective-permute-done.2 = f32[14,128]{1,0:T(8,128)S(1)} collective-permute-done((f32[14,128]{1,0:T(8,128)S(1)}, f32[14,128]{1,0:T(8,128)S(1)}, u32[]{:S(2)}, u32[]{:S(2)}) %collective-permute-start.2) | collective-permute-done | bytes 7200 | tf_op jit(solution)/shard_map/ppermute | solution.py:52
  46.3 0.0 collective-permute-start.3
  46.3 2.5 %collective-permute-done.3 = f32[14,128]{1,0:T(8,128)S(1)} collective-permute-done((f32[14,128]{1,0:T(8,128)S(1)}, f32[14,128]{1,0:T(8,128)S(1)}, u32[]{:S(2)}, u32[]{:S(2)}) %collective-permute-start.3) | collective-permute-done | bytes 7200 | tf_op jit(solution)/shard_map/ppermute | solution.py:52
  48.8 1.2 collective-permute-start.4
  50.0 2.8 %collective-permute-done.4 = f32[14,128]{1,0:T(8,128)S(1)} collective-permute-done((f32[14,128]{1,0:T(8,128)S(1)}, f32[14,128]{1,0:T(8,128)S(1)}, u32[]{:S(2)}, u32[]{:S(2)}) %collective-permute-start.4) | collective-permute-done | bytes 7200 | tf_op jit(solution)/shard_map/ppermute | solution.py:52
  52.8 0.0 collective-permute-start.5
  52.8 2.5 %collective-permute-done.5 = f32[14,128]{1,0:T(8,128)S(1)} collective-permute-done((f32[14,128]{1,0:T(8,128)S(1)}, f32[14,128]{1,0:T(8,128)S(1)}, u32[]{:S(2)}, u32[]{:S(2)}) %collective-permute-start.5) | collective-permute-done | bytes 7200 | tf_op jit(solution)/shard_map/ppermute | solution.py:52
  55.3 1.5 collective-permute-start.6
  56.8 1.9 collective-permute-done.6
  58.7 5.2 %collective-permute-start.7 = (f32[14,128]{1,0:T(8,128)S(1)}, f32[14,128]{1,0:T(8,128)S(1)}, u32[]{:S(2)}, u32[]{:S(2)}) collective-permute-start(f32[14,128]{1,0:T(8,128)S(1)} %add.291), channel_id=1, source_target_pairs={{0,4},{1,5},{2,6},{3,7},{4,0},{5,1},{6,2},{7,3},{8,12},{9,13},{10,... | collective-permute-start | bytes 21512 | tf_op jit(solution)/shard_map/ppermute | solution.py:52
  63.9 1.2 collective-permute-done.7
  65.1 0.1 add_reduce_fusion
  65.3 0.1 add_divide_fusion
  65.3 0.0 copy-start
  65.3 0.7 fusion.40
  66.0 14.1 %fusion.35 = bf16[1,656,128]{2,1,0:T(8,128)(2,1)} fusion(f32[83034]{0:T(1024)S(1)} %reduce, f32[83034]{0:T(1024)S(1)} %reduce.1, f32[83034]{0:T(1024)S(1)} %reduce.3, f32[]{:T(128)} %bitcast.27, f32[]{:T(128)} %bitcast.26, f32[]{:T(128)} %bitcast.25, f32[]{:T(128)} %bitcast.24, f32[]{:T(128)} %bitcast.23, f32[]{:T(128)} %bitcast.22, f32[]{:T(128)} %bitcast.21, ...), kind=kLoop, calls=%fused_computation.61 | loop fusion | flops 5877760 | bytes 1333116 | tf_op jit(solution)/shard_map/convert_element_type | solution.py:92
  80.2 0.0 all-gather.2.cloned.1.call-update
  80.2 13.4 %add_multiply_fusion = (f32[83968]{0:T(1024)S(1)}, f32[83968]{0:T(1024)S(1)}, f32[83968]{0:T(1024)S(1)}) fusion(f32[83034]{0:T(1024)S(1)} %reduce, f32[]{:T(128)} %bitcast.27, f32[]{:T(128)} %bitcast.26, f32[]{:T(128)} %bitcast.25, f32[]{:T(128)} %bitcast.24, f32[]{:T(128)} %bitcast.23, f32[]{:T(128)} %bitcast.22, f32[]{:T(128)} %bitcast.21, s32[]{:T(128)} %bitcast.10, ...), kind=kLoop, calls=%fused_computation.50 | loop fusion | flops 5625856 | bytes 2172796 | tf_op jit(solution)/shard_map/mul | solution.py:90
  93.7 0.0 copy-done
  93.7 1.0 reshape.412
  94.6 1.0 reshape.415
  95.6 1.0 reshape.413
  96.5 1.0 reshape.414
  97.5 44.7 %all-gather.2.cloned.1.call-done = bf16[32,656,128]{2,1,0:T(8,128)(2,1)} async-done(((bf16[1,656,128]{2,1,0:T(8,128)(2,1)}), bf16[32,656,128]{2,1,0:T(8,128)(2,1)}) %all-gather.2.cloned.1.call-update) | async-done | bytes 5373968 | tf_op jit(solution)/shard_map/all_gather | solution.py:92
  142.2 3.9 %copy.15 = bf16[4,8,656,128]{3,1,2,0:T(8,128)(2,1)S(1)} copy(bf16[4,8,656,128]{3,2,1,0:T(8,128)(2,1)} %bitcast.120) | data formatting | bytes 10747904
  146.1 2.7 %slice.146 = bf16[32,83034]{1,0:T(8,128)(2,1)} slice(bf16[32,83968]{1,0:T(8,128)(2,1)S(1)} %bitcast.119), slice={[0:32], [0:83034]} | slice | bytes 10628352 | tf_op jit(solution)/shard_map/slice | solution.py:93
  148.8 12.1 %reshape.461 = bf16[2657088]{0:T(1024)(128)(2,1)} reshape(bf16[32,83034]{1,0:T(8,128)(2,1)} %slice.146) | data formatting | bytes 10628352
  160.9 51.9 %reshape.418 = bf16[1,2657088]{1,0:T(2,128)(2,1)} reshape(bf16[2657088]{0:T(1024)(128)(2,1)} %reshape.461) | data formatting | bytes 10628352 | tf_op jit(solution)/shard_map/reshape | solution.py:93
  (10 shorter events, 0.1 us)
Async XLA Ops:
  7.2 135.0 %all-gather.2.cloned.1.call-start = ((), (), s32[]{:S(2)}) async-start(), calls=%async_computation | async-start | bytes 5541888 | tf_op jit(solution)/shard_map/all_gather | solution.py:92
  35.6 4.1 %collective-permute-start = (f32[14,128]{1,0:T(8,128)S(1)}, f32[14,128]{1,0:T(8,128)S(1)}, u32[]{:S(2)}, u32[]{:S(2)}) collective-permute-start(f32[14,128]{1,0:T(8,128)S(1)} %pad_maximum_fusion), channel_id=1, source_target_pairs={{0,8},{8,0},{16,24},{24,16},{32,40},{40,32},{48,56},{56,48},{64,72... | collective-permute-start | bytes 21512 | tf_op jit(solution)/shard_map/ppermute | solution.py:52
  39.8 2.5 %collective-permute-start.1 = (f32[14,128]{1,0:T(8,128)S(1)}, f32[14,128]{1,0:T(8,128)S(1)}, u32[]{:S(2)}, u32[]{:S(2)}) collective-permute-start(f32[14,128]{1,0:T(8,128)S(1)} %fusion.36), channel_id=1, source_target_pairs={{0,16},{8,24},{16,0},{24,8},{32,48},{40,56},{48,32},{56,40},{64,80... | collective-permute-start | bytes 21512 | tf_op jit(solution)/shard_map/ppermute | solution.py:52
  42.3 4.0 %collective-permute-start.2 = (f32[14,128]{1,0:T(8,128)S(1)}, f32[14,128]{1,0:T(8,128)S(1)}, u32[]{:S(2)}, u32[]{:S(2)}) collective-permute-start(f32[14,128]{1,0:T(8,128)S(1)} %add.286), channel_id=1, source_target_pairs={{0,32},{8,40},{16,48},{24,56},{32,0},{40,8},{48,16},{56,24},{64,96... | collective-permute-start | bytes 21512 | tf_op jit(solution)/shard_map/ppermute | solution.py:52
  46.3 2.5 %collective-permute-start.3 = (f32[14,128]{1,0:T(8,128)S(1)}, f32[14,128]{1,0:T(8,128)S(1)}, u32[]{:S(2)}, u32[]{:S(2)}) collective-permute-start(f32[14,128]{1,0:T(8,128)S(1)} %add.287), channel_id=1, source_target_pairs={{0,64},{8,72},{16,80},{24,88},{32,96},{40,104},{48,112},{56,120},{... | collective-permute-start | bytes 21512 | tf_op jit(solution)/shard_map/ppermute | solution.py:52
  48.8 4.0 %collective-permute-start.4 = (f32[14,128]{1,0:T(8,128)S(1)}, f32[14,128]{1,0:T(8,128)S(1)}, u32[]{:S(2)}, u32[]{:S(2)}) collective-permute-start(f32[14,128]{1,0:T(8,128)S(1)} %add.288), channel_id=1, source_target_pairs={{0,128},{8,136},{16,144},{24,152},{32,160},{40,168},{48,176},{56,1... | collective-permute-start | bytes 21512 | tf_op jit(solution)/shard_map/ppermute | solution.py:52
  52.8 2.5 %collective-permute-start.5 = (f32[14,128]{1,0:T(8,128)S(1)}, f32[14,128]{1,0:T(8,128)S(1)}, u32[]{:S(2)}, u32[]{:S(2)}) collective-permute-start(f32[14,128]{1,0:T(8,128)S(1)} %add.289), channel_id=1, source_target_pairs={{0,1},{1,0},{2,3},{3,2},{4,5},{5,4},{6,7},{7,6},{8,9},{9,8},{10,11... | collective-permute-start | bytes 21512 | tf_op jit(solution)/shard_map/ppermute | solution.py:52
  55.3 3.4 %collective-permute-start.6 = (f32[14,128]{1,0:T(8,128)S(1)}, f32[14,128]{1,0:T(8,128)S(1)}, u32[]{:S(2)}, u32[]{:S(2)}) collective-permute-start(f32[14,128]{1,0:T(8,128)S(1)} %add.290), channel_id=1, source_target_pairs={{0,2},{1,3},{2,0},{3,1},{4,6},{5,7},{6,4},{7,5},{8,10},{9,11},{10,... | collective-permute-start | bytes 21512 | tf_op jit(solution)/shard_map/ppermute | solution.py:52
  58.7 6.4 %collective-permute-start.7 = (f32[14,128]{1,0:T(8,128)S(1)}, f32[14,128]{1,0:T(8,128)S(1)}, u32[]{:S(2)}, u32[]{:S(2)}) collective-permute-start(f32[14,128]{1,0:T(8,128)S(1)} %add.291), channel_id=1, source_target_pairs={{0,4},{1,5},{2,6},{3,7},{4,0},{5,1},{6,2},{7,3},{8,12},{9,13},{10,... | collective-permute-start | bytes 21512 | tf_op jit(solution)/shard_map/ppermute | solution.py:52
  65.3 28.3 %copy-start = (f32[7]{0:T(128)}, f32[7]{0:T(128)S(1)}, u32[]{:S(2)}) copy-start(f32[7]{0:T(128)S(1)} %add_divide_fusion) | copy-start | bytes 88
Sparse Core Ops, SparseCore 0:
  80.3 61.8 all-gather.1

commit v4 on v3

--- a/solution.py
+++ b/solution.py
@@ -3,6 +3,8 @@
 import jax
 import jax.numpy as jnp
 from jax import lax
+from jax.experimental import pallas as pl
+from jax.experimental.pallas import tpu as pltpu
 from jax.sharding import PartitionSpec as P
 
 D = 2304
@@ -62,34 +64,99 @@
     return block.reshape(-1)[:width].reshape(1, width)
 
 
+def slot_of(scalars_ref, rows):
+    places = (
+        scalars_ref[SLOTS - 1]
+        + lax.broadcasted_iota(jnp.int32, (rows, 128), 0) * 128
+        + lax.broadcasted_iota(jnp.int32, (rows, 128), 1)
+    )
+    slot = jnp.zeros((rows, 128), jnp.int32)
+    for number in range(SLOTS - 1):
+        slot = slot + (places >= scalars_ref[number]).astype(jnp.int32)
+    return slot
+
+
+def per_slot(slot, table_ref):
+    result = jnp.zeros(slot.shape, jnp.float32)
+    for number in range(SLOTS):
+        result = jnp.where(slot == number, table_ref[number], result)
+    return result
+
+
+def moments_kernel(scalars_ref, decay_ref, w_ref, m1_ref, m2_ref, g_ref, nf_ref, ns_ref, raw_ref, sums_ref):
+    rows = w_ref.shape[0]
+    slot = slot_of(scalars_ref, rows)
+    grads = g_ref[...].astype(jnp.float32)
+    new_first = 0.9 * m1_ref[...] + 0.1 * grads
+    new_second = 0.999 * m2_ref[...] + 0.001 * grads * grads
+    w = w_ref[...]
+    raw = new_first / fix_first / (jnp.sqrt(new_second / fix_second) + 1e-06) + per_slot(slot, decay_ref) * w
+    nf_ref[...] = new_first
+    ns_ref[...] = new_second
+    raw_ref[...] = raw
+    wsq = w * w
+    usq = raw * raw
+    sums_ref[...] = jnp.zeros(sums_ref.shape, jnp.float32)
+    for number in range(SLOTS):
+        mask = slot == number
+        sums_ref[pl.ds(number, 1), :] = jnp.sum(jnp.where(mask, wsq, 0.0), axis=0, keepdims=True)
+        sums_ref[pl.ds(8 + number, 1), :] = jnp.sum(jnp.where(mask, usq, 0.0), axis=0, keepdims=True)
+
+
+def update_kernel(scalars_ref, trust_ref, w_ref, raw_ref, su_ref, nw_ref, tc_ref):
+    rows = w_ref.shape[0]
+    slot = slot_of(scalars_ref, rows)
+    scaled_update = per_slot(slot, trust_ref) * raw_ref[...]
+    new_weights = w_ref[...] - step_rate * scaled_update
+    su_ref[...] = scaled_update
+    nw_ref[...] = new_weights
+    tc_ref[...] = new_weights.astype(jnp.bfloat16)
+
+
+SMEM = pl.BlockSpec(memory_space=pltpu.SMEM)
+VMEM = pl.BlockSpec(memory_space=pltpu.VMEM)
+
+
 def on_device(weights, moment_first, moment_second, gradients, tensor_order):
     parts = lax.axis_size("mp")
     width = weights.shape[1]
     padded = -(-width // 2048) * 2048
+    rows = padded // 128
     w = to_dense(weights, padded)
     m1 = to_dense(moment_first, padded)
     m2 = to_dense(moment_second, padded)
-    grads = to_dense(gradients, padded).astype(jnp.float32)
-    rows = padded // 128
-    places = (
-        lax.axis_index("dp") * width
-        + lax.broadcasted_iota(jnp.int32, (rows, 128), 0) * 128
-        + lax.broadcasted_iota(jnp.int32, (rows, 128), 1)
+    g = to_dense(gradients, padded)
+    lengths = jnp.array(
+        [D * D // parts] * 4 + [EXPERTS * D // parts, D // parts, D // parts], jnp.int32
     )
-    kind = tensor_kind(places, tensor_order, parts)
-    new_first = 0.9 * m1 + 0.1 * grads
-    new_second = 0.999 * m2 + 0.001 * grads * grads
-    decay = per_entry(kind, jnp.array(decay_values, jnp.float32))
-    raw = new_first / fix_first / (jnp.sqrt(new_second / fix_second) + 1e-06) + decay * w
-    wpart = kind_sums(kind, w * w)
-    upart = kind_sums(kind, raw * raw)
-    both = tree_sum(tree_sum(jnp.concatenate([wpart, upart]), "dp"), "mp")
-    both = jnp.sum(both, axis=1)
-    wsq, usq = both[:SLOTS], both[SLOTS:]
+    kinds = jnp.arange(SLOTS, dtype=jnp.int32)
+    matches = tensor_order[:, None] == kinds[None, :]
+    slot_lengths = jnp.sum(jnp.where(matches, lengths[None, :], 0), axis=1)
+    boundary = jnp.cumsum(slot_lengths)
+    scalars = jnp.concatenate(
+        [boundary[: SLOTS - 1], (lax.axis_index("dp") * width)[None], jnp.zeros((1,), jnp.int32)]
+    ).astype(jnp.int32)
+    decay_slot = jnp.sum(jnp.where(matches, jnp.array(decay_values, jnp.float32)[None, :], 0.0), axis=1)
+    dense = jax.ShapeDtypeStruct((rows, 128), jnp.float32)
+    new_first, new_second, raw, sums = pl.pallas_call(
+        moments_kernel,
+        out_shape=(dense, dense, dense, jax.ShapeDtypeStruct((16, 128), jnp.float32)),
+        in_specs=[SMEM, SMEM, VMEM, VMEM, VMEM, VMEM],
+        out_specs=(VMEM, VMEM, VMEM, VMEM),
+    )(scalars, decay_slot, w, m1, m2, g)
+    total = jnp.sum(tree_sum(tree_sum(sums, "dp"), "mp"), axis=1)
+    wsq_slot, usq_slot = total[:SLOTS], total[8 : 8 + SLOTS]
+    wsq = jnp.sum(jnp.where(matches, wsq_slot[:, None], 0.0), axis=0)
+    usq = jnp.sum(jnp.where(matches, usq_slot[:, None], 0.0), axis=0)
     trust = jnp.sqrt(wsq) / (jnp.sqrt(usq) + 1e-06)
-    scaled_update = per_entry(kind, trust) * raw
-    new_weights = w - step_rate * scaled_update
-    whole = lax.all_gather(new_weights.astype(jnp.bfloat16), "dp", axis=0, tiled=False)
+    trust_slot = jnp.sum(jnp.where(matches, trust[None, :], 0.0), axis=1)
+    scaled_update, new_weights, piece = pl.pallas_call(
+        update_kernel,
+        out_shape=(dense, dense, jax.ShapeDtypeStruct((rows, 128), jnp.bfloat16)),
+        in_specs=[SMEM, SMEM, VMEM, VMEM],
+        out_specs=(VMEM, VMEM, VMEM),
+    )(scalars, trust_slot, w, raw)
+    whole = lax.all_gather(piece, "dp", axis=0, tiled=False)
     training_copy = whole.reshape(whole.shape[0], padded)[:, :width].reshape(1, -1)
     return (
         from_dense(new_weights, width),

time: 221 us -> 201 us (0.910)
  other arithmetic: 54 us -> 11.8 us
  waiting for transfers between devices: 61.9 us -> 71.7 us
  local copies, waits for them, and re-layouts: 77.3 us -> 85.5 us
  Pallas kernels: 0 us -> 5.37 us
    mul x2 -> x0, other arithmetic: 22.4 us -> none  [the longest x1 13.4 us: on_device(): scaled_update = per_entry(kind, trust) * raw]
    convert_element_type x1 -> x0, other arithmetic: 14.1 us -> none  [on_device(): new_weights.astype(jnp.bfloat16)]
    all_gather x1, waiting for transfers between devices: 44.7 us -> 54.2 us  [on_device(): whole = lax.all_gather(piece, 'dp', axis=0, tiled=False)]
    select_n x1 -> x0, other arithmetic: 8.58 us -> none  [tensor_kind(): result = jnp.where(slot == number, order[number], result)]
    reshape x1 -> x2, local copies, waits for them, and re-layouts: 51.9 us -> 58.3 us  [on_device(): whole.reshape(whole.shape[0], padded)[:, :width].reshape(1, -1)]
    pallas_call x0 -> x2, Pallas kernels: none -> 5.37 us  [the longest x1 2.94 us: on_device(): pl.pallas_call(moments_kernel, out_shape=(dense, dense, dense, jax.ShapeD...]
    unnamed x4 -> x5, local copies, waits for them, and re-layouts: 16 us -> 12 us
    reshape x4, local copies, waits for them, and re-layouts: 3.81 us -> 7.72 us  [from_dense(): return block.reshape(-1)[:width].reshape(1, width)]
  transfers between devices with their start and end apart: 9 -> 9, of which waited for: 9 -> 9; matrix products, arithmetic and copies ran while one was open for 8% -> 4% of each run, Pallas kernels for 0% -> 0%
where the time goes in v4:
time: 201 us
  local copies, waits for them, and re-layouts  85.5 us (43%)
  waiting for transfers between devices  71.7 us (36%)
  between operations  14.1 us (7%)
  starting transfers between devices  12.1 us (6%)
  other arithmetic  11.8 us (6%)
  Pallas kernels  5.37 us (3%)
    reshape x2, local copies, waits for them, and re-layouts, on_device(): whole.reshape(whole.shape[0], padded)[:, :width].reshape(1, -1)  58.3 us
    all_gather x1, waiting for transfers between devices, on_device(): whole = lax.all_gather(piece, 'dp', axis=0, tiled=False)  54.2 us
    ppermute x8, waiting for transfers between devices, tree_sum(): x = x + lax.ppermute(x, axis, pairs)  17.5 us
    ppermute x8, starting transfers between devices, tree_sum(): x = x + lax.ppermute(x, axis, pairs)  12.1 us
    unnamed x5, local copies, waits for them, and re-layouts  12 us
    reshape x4, local copies, waits for them, and re-layouts, from_dense(): return block.reshape(-1)[:width].reshape(1, width)  7.72 us
    unnamed x4, other arithmetic  7.21 us
    slice x1, local copies, waits for them, and re-layouts, on_device(): whole.reshape(whole.shape[0], padded)[:, :width].reshape(1, -1)  5.16 us
  transfers between devices with their start and end apart: 9, of which 9 were waited for; matrix products, arithmetic and copies ran while one was open for 4% of the time, Pallas kernels for 0%

profile of v4, /device:TPU:1, one launch (start us, length us, event | category | flops | bytes accessed | tf_op | source)
XLA Modules:
  0.0 200.7 jit_solution(10158049754142226657)
XLA Ops:
  7.2 0.0 copy-start
  7.2 0.0 all-gather.3.cloned.1.call-start
  7.2 0.9 select_reduce_fusion.4
  8.1 0.2 reduce-window.4
  8.3 1.4 select_reduce_fusion.3.decay_ref
  9.6 1.9 reduce.3
  11.5 0.7 pad_bitcast_fusion.3.g_ref
  12.2 1.8 reduce
  14.0 0.8 pad_bitcast_fusion.2.w_ref
  14.7 1.8 reduce.1
  16.5 1.8 reduce.2
  18.3 0.9 pad_bitcast_fusion
  19.2 0.6 pad_add_fusion.scalars_ref
  19.8 2.9 %shard_map.118 = (f32[656,128]{1,0:T(8,128)}, f32[656,128]{1,0:T(8,128)}, f32[656,128]{1,0:T(8,128)}, f32[16,128]{1,0:T(8,128)}) custom-call(s32[8]{0:T(128)} %pad_add_fusion.scalars_ref, f32[7]{0:T(128)} %select_reduce_fusion.3.decay_ref, f32[656,128]{1,0:T(8,128)} %pad_bitcast_fusion.2.w_ref, f32[656,128]{1,0:T(8,128)} %get-tuple-element.25.m1_ref, ...), custom_call_target="tpu_custom_call" | custom-call | tf_op jit(solution)/shard_map/pallas_call | solution.py:141
  22.7 3.2 %collective-permute-start = (f32[16,128]{1,0:T(8,128)}, f32[16,128]{1,0:T(8,128)S(1)}, u32[]{:S(2)}, u32[]{:S(2)}) collective-permute-start(f32[16,128]{1,0:T(8,128)} %get-tuple-element.13), channel_id=1, source_target_pairs={{0,8},{8,0},{16,24},{24,16},{32,40},{40,32},{48,56},{56,48},{64,72... | collective-permute-start | bytes 24584 | tf_op jit(solution)/shard_map/ppermute | solution.py:54
  25.9 1.0 collective-permute-done
  27.0 0.7 add.39
  27.7 0.0 collective-permute-start.1
  27.7 2.5 %collective-permute-done.1 = f32[16,128]{1,0:T(8,128)S(1)} collective-permute-done((f32[16,128]{1,0:T(8,128)S(1)}, f32[16,128]{1,0:T(8,128)S(1)}, u32[]{:S(2)}, u32[]{:S(2)}) %collective-permute-start.1) | collective-permute-done | bytes 8224 | tf_op jit(solution)/shard_map/ppermute | solution.py:54
  30.2 1.0 collective-permute-start.2
  31.2 3.0 %collective-permute-done.2 = f32[16,128]{1,0:T(8,128)S(1)} collective-permute-done((f32[16,128]{1,0:T(8,128)S(1)}, f32[16,128]{1,0:T(8,128)S(1)}, u32[]{:S(2)}, u32[]{:S(2)}) %collective-permute-start.2) | collective-permute-done | bytes 8224 | tf_op jit(solution)/shard_map/ppermute | solution.py:54
  34.2 0.0 collective-permute-start.3
  34.2 2.5 %collective-permute-done.3 = f32[16,128]{1,0:T(8,128)S(1)} collective-permute-done((f32[16,128]{1,0:T(8,128)S(1)}, f32[16,128]{1,0:T(8,128)S(1)}, u32[]{:S(2)}, u32[]{:S(2)}) %collective-permute-start.3) | collective-permute-done | bytes 8224 | tf_op jit(solution)/shard_map/ppermute | solution.py:54
  36.7 1.2 collective-permute-start.4
  37.9 2.8 %collective-permute-done.4 = f32[16,128]{1,0:T(8,128)S(1)} collective-permute-done((f32[16,128]{1,0:T(8,128)S(1)}, f32[16,128]{1,0:T(8,128)S(1)}, u32[]{:S(2)}, u32[]{:S(2)}) %collective-permute-start.4) | collective-permute-done | bytes 8224 | tf_op jit(solution)/shard_map/ppermute | solution.py:54
  40.7 0.0 collective-permute-start.5
  40.7 2.5 %collective-permute-done.5 = f32[16,128]{1,0:T(8,128)S(1)} collective-permute-done((f32[16,128]{1,0:T(8,128)S(1)}, f32[16,128]{1,0:T(8,128)S(1)}, u32[]{:S(2)}, u32[]{:S(2)}) %collective-permute-start.5) | collective-permute-done | bytes 8224 | tf_op jit(solution)/shard_map/ppermute | solution.py:54
  43.2 1.5 collective-permute-start.6
  44.7 1.9 collective-permute-done.6
  46.6 5.2 %collective-permute-start.7 = (f32[16,128]{1,0:T(8,128)S(1)}, f32[16,128]{1,0:T(8,128)S(1)}, u32[]{:S(2)}, u32[]{:S(2)}) collective-permute-start(f32[16,128]{1,0:T(8,128)S(1)} %add.45), channel_id=1, source_target_pairs={{0,4},{1,5},{2,6},{3,7},{4,0},{5,1},{6,2},{7,3},{8,12},{9,13},{10,... | collective-permute-start | bytes 24584 | tf_op jit(solution)/shard_map/ppermute | solution.py:54
  51.8 1.2 collective-permute-done.7
  53.1 0.1 add_reduce_fusion
  53.2 0.1 fusion
  53.2 0.0 copy-done
  53.2 0.1 select_reduce_fusion.2
  53.3 0.0 copy-start.1
  53.4 0.7 select_reduce_fusion.trust_ref
  54.1 2.4 %shard_map.119 = (f32[656,128]{1,0:T(8,128)}, f32[656,128]{1,0:T(8,128)}, bf16[656,128]{1,0:T(8,128)(2,1)}) custom-call(s32[8]{0:T(128)} %pad_add_fusion.scalars_ref, f32[7]{0:T(128)} %select_reduce_fusion.trust_ref, f32[656,128]{1,0:T(8,128)} %pad_bitcast_fusion.2.w_ref, f32[656,128]{1,0:T(8,128)} %get-tuple-element.14.raw_ref), custom_call_target="tpu_custom_call" | custom-call | tf_op jit(solution)/shard_map/pallas_call | solution.py:153
  56.5 0.0 all-gather.3.cloned.1.call-update
  56.5 1.9 reshape.80
  58.4 1.9 reshape.82
  60.4 1.9 reshape.78
  62.3 1.9 reshape.84
  64.2 54.2 %all-gather.3.cloned.1.call-done = bf16[20992,128]{1,0:T(8,128)(2,1)} async-done(((bf16[656,128]{1,0:T(8,128)(2,1)}), bf16[20992,128]{1,0:T(8,128)(2,1)}) %all-gather.3.cloned.1.call-update) | async-done | bytes 5373968 | tf_op jit(solution)/shard_map/all_gather | solution.py:159
  118.5 6.4 %reshape.85 = bf16[32,83968]{1,0:T(8,128)(2,1)} reshape(bf16[20992,128]{1,0:T(8,128)(2,1)} %all-gather.3.cloned.1.call-done) | data formatting | bytes 10747904 | tf_op jit(solution)/shard_map/reshape | solution.py:160
  124.9 5.2 %slice.40 = bf16[32,83034]{1,0:T(8,128)(2,1)} slice(bf16[32,83968]{1,0:T(8,128)(2,1)} %reshape.85), slice={[0:32], [0:83034]} | slice | bytes 10628352 | tf_op jit(solution)/shard_map/slice | solution.py:160
  130.0 11.9 %reshape.93 = bf16[2657088]{0:T(1024)(128)(2,1)} reshape(bf16[32,83034]{1,0:T(8,128)(2,1)} %slice.40) | data formatting | bytes 10628352
  142.0 51.9 %reshape.86 = bf16[1,2657088]{1,0:T(2,128)(2,1)} reshape(bf16[2657088]{0:T(1024)(128)(2,1)} %reshape.93) | data formatting | bytes 10628352 | tf_op jit(solution)/shard_map/reshape | solution.py:160
  (9 shorter events, 0.0 us)
Async XLA Ops:
  7.2 46.1 %copy-start = (s32[7]{0:T(128)S(1)}, s32[7]{0:T(128)}, u32[]{:S(2)}) copy-start(s32[7]{0:T(128)} %param.11) | copy-start | bytes 88
  7.2 111.3 %all-gather.3.cloned.1.call-start = ((), (), s32[]{:S(2)}) async-start(), calls=%async_computation | async-start | bytes 5541888 | tf_op jit(solution)/shard_map/all_gather | solution.py:159
  22.7 4.2 %collective-permute-start = (f32[16,128]{1,0:T(8,128)}, f32[16,128]{1,0:T(8,128)S(1)}, u32[]{:S(2)}, u32[]{:S(2)}) collective-permute-start(f32[16,128]{1,0:T(8,128)} %get-tuple-element.13), channel_id=1, source_target_pairs={{0,8},{8,0},{16,24},{24,16},{32,40},{40,32},{48,56},{56,48},{64,72... | collective-permute-start | bytes 24584 | tf_op jit(solution)/shard_map/ppermute | solution.py:54
  27.7 2.5 %collective-permute-start.1 = (f32[16,128]{1,0:T(8,128)S(1)}, f32[16,128]{1,0:T(8,128)S(1)}, u32[]{:S(2)}, u32[]{:S(2)}) collective-permute-start(f32[16,128]{1,0:T(8,128)S(1)} %add.39), channel_id=1, source_target_pairs={{0,16},{8,24},{16,0},{24,8},{32,48},{40,56},{48,32},{56,40},{64,80... | collective-permute-start | bytes 24584 | tf_op jit(solution)/shard_map/ppermute | solution.py:54
  30.2 4.0 %collective-permute-start.2 = (f32[16,128]{1,0:T(8,128)S(1)}, f32[16,128]{1,0:T(8,128)S(1)}, u32[]{:S(2)}, u32[]{:S(2)}) collective-permute-start(f32[16,128]{1,0:T(8,128)S(1)} %add.40), channel_id=1, source_target_pairs={{0,32},{8,40},{16,48},{24,56},{32,0},{40,8},{48,16},{56,24},{64,96... | collective-permute-start | bytes 24584 | tf_op jit(solution)/shard_map/ppermute | solution.py:54
  34.2 2.5 %collective-permute-start.3 = (f32[16,128]{1,0:T(8,128)S(1)}, f32[16,128]{1,0:T(8,128)S(1)}, u32[]{:S(2)}, u32[]{:S(2)}) collective-permute-start(f32[16,128]{1,0:T(8,128)S(1)} %add.41), channel_id=1, source_target_pairs={{0,64},{8,72},{16,80},{24,88},{32,96},{40,104},{48,112},{56,120},{... | collective-permute-start | bytes 24584 | tf_op jit(solution)/shard_map/ppermute | solution.py:54
  36.7 4.0 %collective-permute-start.4 = (f32[16,128]{1,0:T(8,128)S(1)}, f32[16,128]{1,0:T(8,128)S(1)}, u32[]{:S(2)}, u32[]{:S(2)}) collective-permute-start(f32[16,128]{1,0:T(8,128)S(1)} %add.42), channel_id=1, source_target_pairs={{0,128},{8,136},{16,144},{24,152},{32,160},{40,168},{48,176},{56,1... | collective-permute-start | bytes 24584 | tf_op jit(solution)/shard_map/ppermute | solution.py:54
  40.7 2.5 %collective-permute-start.5 = (f32[16,128]{1,0:T(8,128)S(1)}, f32[16,128]{1,0:T(8,128)S(1)}, u32[]{:S(2)}, u32[]{:S(2)}) collective-permute-start(f32[16,128]{1,0:T(8,128)S(1)} %add.43), channel_id=1, source_target_pairs={{0,1},{1,0},{2,3},{3,2},{4,5},{5,4},{6,7},{7,6},{8,9},{9,8},{10,11... | collective-permute-start | bytes 24584 | tf_op jit(solution)/shard_map/ppermute | solution.py:54
  43.2 3.4 %collective-permute-start.6 = (f32[16,128]{1,0:T(8,128)S(1)}, f32[16,128]{1,0:T(8,128)S(1)}, u32[]{:S(2)}, u32[]{:S(2)}) collective-permute-start(f32[16,128]{1,0:T(8,128)S(1)} %add.44), channel_id=1, source_target_pairs={{0,2},{1,3},{2,0},{3,1},{4,6},{5,7},{6,4},{7,5},{8,10},{9,11},{10,... | collective-permute-start | bytes 24584 | tf_op jit(solution)/shard_map/ppermute | solution.py:54
  46.6 6.4 %collective-permute-start.7 = (f32[16,128]{1,0:T(8,128)S(1)}, f32[16,128]{1,0:T(8,128)S(1)}, u32[]{:S(2)}, u32[]{:S(2)}) collective-permute-start(f32[16,128]{1,0:T(8,128)S(1)} %add.45), channel_id=1, source_target_pairs={{0,4},{1,5},{2,6},{3,7},{4,0},{5,1},{6,2},{7,3},{8,12},{9,13},{10,... | collective-permute-start | bytes 24584 | tf_op jit(solution)/shard_map/ppermute | solution.py:54
  53.3 71.5 %copy-start.1 = (f32[7]{0:T(128)}, f32[7]{0:T(128)S(1)}, u32[]{:S(2)}) copy-start(f32[7]{0:T(128)S(1)} %add_divide_fusion) | copy-start | bytes 88
Sparse Core Ops, SparseCore 0:
  56.6 61.7 all-gather.2

commit v5 on v4

--- a/solution.py
+++ b/solution.py
@@ -57,11 +57,11 @@
 
 
 def to_dense(row, padded):
-    return jnp.pad(row[0], (0, padded - row.shape[1])).reshape(padded // 128, 128)
+    return jnp.pad(row, ((0, 0), (0, padded - row.shape[1]))).reshape(padded // 128, 128)
 
 
 def from_dense(block, width):
-    return block.reshape(-1)[:width].reshape(1, width)
+    return block.reshape(1, -1)[:, :width]
 
 
 def slot_of(scalars_ref, rows):

time: 201 us -> 202 us (level)
  other arithmetic: 11.8 us -> 5.93 us
  local copies, waits for them, and re-layouts: 85.5 us -> 90.8 us
    reshape x7 -> x0, local copies, waits for them, and re-layouts: 10.1 us -> none  [the longest x4 7.72 us: from_dense(): return block.reshape(-1)[:width].reshape(1, width)]
    pad x0 -> x4, local copies, waits for them, and re-layouts: none -> 8.44 us  [to_dense(): jnp.pad(row, ((0, 0), (0, padded - row.shape[1])))]
    unnamed x4 -> x0, other arithmetic: 7.21 us -> none
    slice x0 -> x4, local copies, waits for them, and re-layouts: none -> 6.89 us  [from_dense(): return block.reshape(1, -1)[:, :width]]
    unnamed x5 -> x3, local copies, waits for them, and re-layouts: 12 us -> 11.9 us
  transfers between devices with their start and end apart: 9 -> 9, of which waited for: 9 -> 9; matrix products, arithmetic and copies ran while one was open for 4% -> 3% of each run, Pallas kernels for 0% -> 0%
where the time goes in v5:
time: 202 us; the launch traced here: 201 us
  local copies, waits for them, and re-layouts  90.8 us (45%)
  waiting for transfers between devices  72.5 us (36%)
  between operations  14.1 us (7%)
  starting transfers between devices  12.1 us (6%)
  other arithmetic  5.93 us (3%)
  Pallas kernels  5.37 us (3%)
    reshape x2, local copies, waits for them, and re-layouts, on_device(): whole.reshape(whole.shape[0], padded)[:, :width].reshape(1, -1)  58.3 us
    all_gather x1, waiting for transfers between devices, on_device(): whole = lax.all_gather(piece, 'dp', axis=0, tiled=False)  55 us
    ppermute x8, waiting for transfers between devices, tree_sum(): x = x + lax.ppermute(x, axis, pairs)  17.5 us
    ppermute x8, starting transfers between devices, tree_sum(): x = x + lax.ppermute(x, axis, pairs)  12.1 us
    unnamed x3, local copies, waits for them, and re-layouts  11.9 us
    pad x4, local copies, waits for them, and re-layouts, to_dense(): jnp.pad(row, ((0, 0), (0, padded - row.shape[1])))  8.44 us
    slice x4, local copies, waits for them, and re-layouts, from_dense(): return block.reshape(1, -1)[:, :width]  6.89 us
    slice x1, local copies, waits for them, and re-layouts, on_device(): whole.reshape(whole.shape[0], padded)[:, :width].reshape(1, -1)  5.16 us
  transfers between devices with their start and end apart: 9, of which 9 were waited for; matrix products, arithmetic and copies ran while one was open for 3% of the time, Pallas kernels for 0%

profile of v5, /device:TPU:1, one launch (start us, length us, event | category | flops | bytes accessed | tf_op | source)
XLA Modules:
  0.0 200.8 jit_solution(7561307124321108848)
XLA Ops:
  7.2 0.0 all-gather.3.cloned.1.call-start
  7.2 0.9 select_reduce_fusion.4
  8.1 0.2 reduce-window.4
  8.3 1.4 select_reduce_fusion.3.decay_ref
  9.6 2.6 %pad_reduce_fusion = bf16[83968]{0:T(1024)(128)(2,1)} fusion(bf16[1,83034]{1,0:T(2,128)(2,1)} %param.10), kind=kLoop, calls=%fused_computation | loop fusion | bytes 334004 | tf_op jit(solution)/shard_map/jit(_pad)/pad | solution.py:60
  12.3 1.9 pad.14
  14.2 1.9 pad.15
  16.1 1.9 pad.16
  18.1 0.6 pad_add_fusion.scalars_ref
  18.7 2.9 %shard_map.118 = (f32[656,128]{1,0:T(8,128)}, f32[656,128]{1,0:T(8,128)}, f32[656,128]{1,0:T(8,128)}, f32[16,128]{1,0:T(8,128)}) custom-call(s32[8]{0:T(128)} %pad_add_fusion.scalars_ref, f32[7]{0:T(128)} %select_reduce_fusion.3.decay_ref, f32[656,128]{1,0:T(8,128)} %bitcast.12, f32[656,128]{1,0:T(8,128)} %bitcast.14, f32[656,128]{1,0:T(8,128)} %bitcast.15, ...), custom_call_target="tpu_custom_call" | custom-call | tf_op jit(solution)/shard_map/pallas_call | solution.py:141
  21.6 3.2 %collective-permute-start = (f32[16,128]{1,0:T(8,128)}, f32[16,128]{1,0:T(8,128)S(1)}, u32[]{:S(2)}, u32[]{:S(2)}) collective-permute-start(f32[16,128]{1,0:T(8,128)} %get-tuple-element.13), channel_id=1, source_target_pairs={{0,8},{8,0},{16,24},{24,16},{32,40},{40,32},{48,56},{56,48},{64,72... | collective-permute-start | bytes 24584 | tf_op jit(solution)/shard_map/ppermute | solution.py:54
  24.8 1.0 collective-permute-done
  25.8 0.7 add.39
  26.5 0.0 collective-permute-start.1
  26.5 2.5 %collective-permute-done.1 = f32[16,128]{1,0:T(8,128)S(1)} collective-permute-done((f32[16,128]{1,0:T(8,128)S(1)}, f32[16,128]{1,0:T(8,128)S(1)}, u32[]{:S(2)}, u32[]{:S(2)}) %collective-permute-start.1) | collective-permute-done | bytes 8224 | tf_op jit(solution)/shard_map/ppermute | solution.py:54
  29.0 1.0 collective-permute-start.2
  30.1 3.0 %collective-permute-done.2 = f32[16,128]{1,0:T(8,128)S(1)} collective-permute-done((f32[16,128]{1,0:T(8,128)S(1)}, f32[16,128]{1,0:T(8,128)S(1)}, u32[]{:S(2)}, u32[]{:S(2)}) %collective-permute-start.2) | collective-permute-done | bytes 8224 | tf_op jit(solution)/shard_map/ppermute | solution.py:54
  33.0 0.0 collective-permute-start.3
  33.1 2.5 %collective-permute-done.3 = f32[16,128]{1,0:T(8,128)S(1)} collective-permute-done((f32[16,128]{1,0:T(8,128)S(1)}, f32[16,128]{1,0:T(8,128)S(1)}, u32[]{:S(2)}, u32[]{:S(2)}) %collective-permute-start.3) | collective-permute-done | bytes 8224 | tf_op jit(solution)/shard_map/ppermute | solution.py:54
  35.6 1.2 collective-permute-start.4
  36.8 2.8 %collective-permute-done.4 = f32[16,128]{1,0:T(8,128)S(1)} collective-permute-done((f32[16,128]{1,0:T(8,128)S(1)}, f32[16,128]{1,0:T(8,128)S(1)}, u32[]{:S(2)}, u32[]{:S(2)}) %collective-permute-start.4) | collective-permute-done | bytes 8224 | tf_op jit(solution)/shard_map/ppermute | solution.py:54
  39.6 0.0 collective-permute-start.5
  39.6 2.5 %collective-permute-done.5 = f32[16,128]{1,0:T(8,128)S(1)} collective-permute-done((f32[16,128]{1,0:T(8,128)S(1)}, f32[16,128]{1,0:T(8,128)S(1)}, u32[]{:S(2)}, u32[]{:S(2)}) %collective-permute-start.5) | collective-permute-done | bytes 8224 | tf_op jit(solution)/shard_map/ppermute | solution.py:54
  42.1 1.5 collective-permute-start.6
  43.5 1.9 collective-permute-done.6
  45.5 5.2 %collective-permute-start.7 = (f32[16,128]{1,0:T(8,128)S(1)}, f32[16,128]{1,0:T(8,128)S(1)}, u32[]{:S(2)}, u32[]{:S(2)}) collective-permute-start(f32[16,128]{1,0:T(8,128)S(1)} %add.45), channel_id=1, source_target_pairs={{0,4},{1,5},{2,6},{3,7},{4,0},{5,1},{6,2},{7,3},{8,12},{9,13},{10,... | collective-permute-start | bytes 24584 | tf_op jit(solution)/shard_map/ppermute | solution.py:54
  50.7 1.2 collective-permute-done.7
  51.9 0.1 add_reduce_fusion
  52.0 0.1 fusion
  52.1 0.7 select_reduce_fusion.2
  52.9 0.0 copy-start
  52.9 1.3 select_reduce_fusion.trust_ref
  54.2 2.4 %shard_map.119 = (f32[656,128]{1,0:T(8,128)}, f32[656,128]{1,0:T(8,128)}, bf16[656,128]{1,0:T(8,128)(2,1)}) custom-call(s32[8]{0:T(128)} %pad_add_fusion.scalars_ref, f32[7]{0:T(128)} %select_reduce_fusion.trust_ref, f32[656,128]{1,0:T(8,128)} %bitcast.13, f32[656,128]{1,0:T(8,128)} %get-tuple-element.14.raw_ref), custom_call_target="tpu_custom_call" | custom-call | tf_op jit(solution)/shard_map/pallas_call | solution.py:153
  56.7 0.0 all-gather.3.cloned.1.call-update
  56.7 1.7 slice.37
  58.4 1.7 slice.38
  60.1 1.7 slice.36
  61.9 1.7 slice.39
  63.6 55.0 %all-gather.3.cloned.1.call-done = bf16[20992,128]{1,0:T(8,128)(2,1)} async-done(((bf16[656,128]{1,0:T(8,128)(2,1)}), bf16[20992,128]{1,0:T(8,128)(2,1)}) %all-gather.3.cloned.1.call-update) | async-done | bytes 5373968 | tf_op jit(solution)/shard_map/all_gather | solution.py:159
  118.6 6.4 %reshape.69 = bf16[32,83968]{1,0:T(8,128)(2,1)} reshape(bf16[20992,128]{1,0:T(8,128)(2,1)} %all-gather.3.cloned.1.call-done) | data formatting | bytes 10747904 | tf_op jit(solution)/shard_map/reshape | solution.py:160
  125.0 0.0 copy-done
  125.0 5.2 %slice.40 = bf16[32,83034]{1,0:T(8,128)(2,1)} slice(bf16[32,83968]{1,0:T(8,128)(2,1)} %reshape.69), slice={[0:32], [0:83034]} | slice | bytes 10628352 | tf_op jit(solution)/shard_map/slice | solution.py:160
  130.2 11.9 %reshape.74 = bf16[2657088]{0:T(1024)(128)(2,1)} reshape(bf16[32,83034]{1,0:T(8,128)(2,1)} %slice.40) | data formatting | bytes 10628352
  142.1 51.9 %reshape.70 = bf16[1,2657088]{1,0:T(2,128)(2,1)} reshape(bf16[2657088]{0:T(1024)(128)(2,1)} %reshape.74) | data formatting | bytes 10628352 | tf_op jit(solution)/shard_map/reshape | solution.py:160
  (8 shorter events, 0.0 us)
Async XLA Ops:
  7.2 111.5 %all-gather.3.cloned.1.call-start = ((), (), s32[]{:S(2)}) async-start(), calls=%async_computation | async-start | bytes 5541888 | tf_op jit(solution)/shard_map/all_gather | solution.py:159
  21.6 4.2 %collective-permute-start = (f32[16,128]{1,0:T(8,128)}, f32[16,128]{1,0:T(8,128)S(1)}, u32[]{:S(2)}, u32[]{:S(2)}) collective-permute-start(f32[16,128]{1,0:T(8,128)} %get-tuple-element.13), channel_id=1, source_target_pairs={{0,8},{8,0},{16,24},{24,16},{32,40},{40,32},{48,56},{56,48},{64,72... | collective-permute-start | bytes 24584 | tf_op jit(solution)/shard_map/ppermute | solution.py:54
  26.5 2.5 %collective-permute-start.1 = (f32[16,128]{1,0:T(8,128)S(1)}, f32[16,128]{1,0:T(8,128)S(1)}, u32[]{:S(2)}, u32[]{:S(2)}) collective-permute-start(f32[16,128]{1,0:T(8,128)S(1)} %add.39), channel_id=1, source_target_pairs={{0,16},{8,24},{16,0},{24,8},{32,48},{40,56},{48,32},{56,40},{64,80... | collective-permute-start | bytes 24584 | tf_op jit(solution)/shard_map/ppermute | solution.py:54
  29.0 4.0 %collective-permute-start.2 = (f32[16,128]{1,0:T(8,128)S(1)}, f32[16,128]{1,0:T(8,128)S(1)}, u32[]{:S(2)}, u32[]{:S(2)}) collective-permute-start(f32[16,128]{1,0:T(8,128)S(1)} %add.40), channel_id=1, source_target_pairs={{0,32},{8,40},{16,48},{24,56},{32,0},{40,8},{48,16},{56,24},{64,96... | collective-permute-start | bytes 24584 | tf_op jit(solution)/shard_map/ppermute | solution.py:54
  33.0 2.5 %collective-permute-start.3 = (f32[16,128]{1,0:T(8,128)S(1)}, f32[16,128]{1,0:T(8,128)S(1)}, u32[]{:S(2)}, u32[]{:S(2)}) collective-permute-start(f32[16,128]{1,0:T(8,128)S(1)} %add.41), channel_id=1, source_target_pairs={{0,64},{8,72},{16,80},{24,88},{32,96},{40,104},{48,112},{56,120},{... | collective-permute-start | bytes 24584 | tf_op jit(solution)/shard_map/ppermute | solution.py:54
  35.6 4.0 %collective-permute-start.4 = (f32[16,128]{1,0:T(8,128)S(1)}, f32[16,128]{1,0:T(8,128)S(1)}, u32[]{:S(2)}, u32[]{:S(2)}) collective-permute-start(f32[16,128]{1,0:T(8,128)S(1)} %add.42), channel_id=1, source_target_pairs={{0,128},{8,136},{16,144},{24,152},{32,160},{40,168},{48,176},{56,1... | collective-permute-start | bytes 24584 | tf_op jit(solution)/shard_map/ppermute | solution.py:54
  39.6 2.5 %collective-permute-start.5 = (f32[16,128]{1,0:T(8,128)S(1)}, f32[16,128]{1,0:T(8,128)S(1)}, u32[]{:S(2)}, u32[]{:S(2)}) collective-permute-start(f32[16,128]{1,0:T(8,128)S(1)} %add.43), channel_id=1, source_target_pairs={{0,1},{1,0},{2,3},{3,2},{4,5},{5,4},{6,7},{7,6},{8,9},{9,8},{10,11... | collective-permute-start | bytes 24584 | tf_op jit(solution)/shard_map/ppermute | solution.py:54
  42.1 3.4 %collective-permute-start.6 = (f32[16,128]{1,0:T(8,128)S(1)}, f32[16,128]{1,0:T(8,128)S(1)}, u32[]{:S(2)}, u32[]{:S(2)}) collective-permute-start(f32[16,128]{1,0:T(8,128)S(1)} %add.44), channel_id=1, source_target_pairs={{0,2},{1,3},{2,0},{3,1},{4,6},{5,7},{6,4},{7,5},{8,10},{9,11},{10,... | collective-permute-start | bytes 24584 | tf_op jit(solution)/shard_map/ppermute | solution.py:54
  45.5 6.4 %collective-permute-start.7 = (f32[16,128]{1,0:T(8,128)S(1)}, f32[16,128]{1,0:T(8,128)S(1)}, u32[]{:S(2)}, u32[]{:S(2)}) collective-permute-start(f32[16,128]{1,0:T(8,128)S(1)} %add.45), channel_id=1, source_target_pairs={{0,4},{1,5},{2,6},{3,7},{4,0},{5,1},{6,2},{7,3},{8,12},{9,13},{10,... | collective-permute-start | bytes 24584 | tf_op jit(solution)/shard_map/ppermute | solution.py:54
  52.9 72.2 %copy-start = (f32[7]{0:T(128)}, f32[7]{0:T(128)S(1)}, u32[]{:S(2)}) copy-start(f32[7]{0:T(128)S(1)} %add_divide_fusion) | copy-start | bytes 88
Sparse Core Ops, SparseCore 0:
  56.8 61.7 all-gather.2

commit v6 on v5

--- a/solution.py
+++ b/solution.py
@@ -1,3 +1,4 @@
+import functools
 import math
 
 import jax
@@ -111,6 +112,38 @@
     su_ref[...] = scaled_update
     nw_ref[...] = new_weights
     tc_ref[...] = new_weights.astype(jnp.bfloat16)
+
+
+def assemble_kernel(width, whole_ref, out_ref):
+    count, rows, _ = whole_ref.shape
+    total = count * width
+    lane = lax.broadcasted_iota(jnp.int32, (rows, 128), 1)
+    for k in range(count):
+        start, shift = divmod(k * width, 128)
+        chunks = -(-(shift + width) // 128)
+        piece = whole_ref[k].astype(jnp.float32)
+        if shift:
+            rolled = pltpu.roll(piece, shift, 1)
+            piece = jnp.where(lane >= shift, rolled, pltpu.roll(rolled, 1, 0))
+        if shift and k:
+            held = out_ref[:, pl.ds(start * 128, 128)].astype(jnp.float32)
+            first = jnp.where(lane[:1] >= shift, piece[:1], held)
+            piece = jnp.concatenate([first, piece[1:]], axis=0)
+        full = min(chunks, total // 128 - start)
+        out_ref[:, pl.ds(start * 128, full * 128)] = piece[:full].reshape(1, full * 128).astype(out_ref.dtype)
+        tail = total - (start + full) * 128
+        if full < chunks and tail:
+            out_ref[:, pl.ds((start + full) * 128, tail)] = piece[full : full + 1, :tail].astype(out_ref.dtype)
+
+
+def assemble(whole, width):
+    count = whole.shape[0]
+    return pl.pallas_call(
+        functools.partial(assemble_kernel, width),
+        out_shape=jax.ShapeDtypeStruct((1, count * width), jnp.bfloat16),
+        in_specs=[pl.BlockSpec(memory_space=pltpu.VMEM)],
+        out_specs=pl.BlockSpec(memory_space=pltpu.VMEM),
+    )(whole)
 
 
 SMEM = pl.BlockSpec(memory_space=pltpu.SMEM)
@@ -157,7 +190,7 @@
         out_specs=(VMEM, VMEM, VMEM),
     )(scalars, trust_slot, w, raw)
     whole = lax.all_gather(piece, "dp", axis=0, tiled=False)
-    training_copy = whole.reshape(whole.shape[0], padded)[:, :width].reshape(1, -1)
+    training_copy = assemble(whole, width)
     return (
         from_dense(new_weights, width),
         from_dense(new_first, width),

time: 202 us -> 142 us (0.70)
  local copies, waits for them, and re-layouts: 90.8 us -> 15.4 us
  Pallas kernels: 5.37 us -> 21.5 us
    reshape x2 -> x0, local copies, waits for them, and re-layouts: 58.3 us -> none  [on_device(): whole.reshape(whole.shape[0], padded)[:, :width].reshape(1, -1)]
    pallas_call x0 -> x1, Pallas kernels: none -> 16.1 us  [assemble(): pl.pallas_call(functools.partial(assemble_kernel, width), out_shape=jax.S...]
    unnamed x3 -> x2, local copies, waits for them, and re-layouts: 11.9 us -> 0.01 us
    slice x1 -> x0, local copies, waits for them, and re-layouts: 5.16 us -> none  [on_device(): whole.reshape(whole.shape[0], padded)[:, :width].reshape(1, -1)]
  transfers between devices with their start and end apart: 9 -> 9, of which waited for: 9 -> 9; matrix products, arithmetic and copies ran while one was open for 3% -> 5% of each run, Pallas kernels for 0% -> 0%
where the time goes in v6:
time: 142 us
  waiting for transfers between devices  72.5 us (51%)
  Pallas kernels  21.5 us (15%)
  local copies, waits for them, and re-layouts  15.4 us (11%)
  between operations  14.1 us (10%)
  starting transfers between devices  12.1 us (9%)
  other arithmetic  5.93 us (4%)
    all_gather x1, waiting for transfers between devices, on_device(): whole = lax.all_gather(piece, 'dp', axis=0, tiled=False)  55 us
    ppermute x8, waiting for transfers between devices, tree_sum(): x = x + lax.ppermute(x, axis, pairs)  17.5 us
    pallas_call x1, Pallas kernels, assemble(): pl.pallas_call(functools.partial(assemble_kernel, width), out_shape=jax.S...  16.1 us
    ppermute x8, starting transfers between devices, tree_sum(): x = x + lax.ppermute(x, axis, pairs)  12.1 us
    pad x4, local copies, waits for them, and re-layouts, to_dense(): jnp.pad(row, ((0, 0), (0, padded - row.shape[1])))  8.44 us
    slice x4, local copies, waits for them, and re-layouts, from_dense(): return block.reshape(1, -1)[:, :width]  6.89 us
    pallas_call x1, Pallas kernels, on_device(): pl.pallas_call(moments_kernel, out_shape=(dense, dense, dense, jax.ShapeD...  2.94 us
  transfers between devices with their start and end apart: 9, of which 9 were waited for; matrix products, arithmetic and copies ran while one was open for 5% of the time, Pallas kernels for 0%

profile of v6, /device:TPU:1, one launch (start us, length us, event | category | flops | bytes accessed | tf_op | source)
XLA Modules:
  0.0 141.6 jit_solution(5547327318622372105)
XLA Ops:
  7.2 0.0 all-gather.3.cloned.1.call-start
  7.2 0.9 select_reduce_fusion.4
  8.1 0.2 reduce-window.4
  8.3 1.4 select_reduce_fusion.3.decay_ref
  9.6 2.6 %pad_reduce_fusion = bf16[83968]{0:T(1024)(128)(2,1)} fusion(bf16[1,83034]{1,0:T(2,128)(2,1)} %param.10), kind=kLoop, calls=%fused_computation | loop fusion | bytes 334004 | tf_op jit(solution)/shard_map/jit(_pad)/pad | solution.py:61
  12.3 1.9 %pad.14 = f32[1,83968]{1,0:T(1,128)} pad(f32[1,83034]{1,0:T(1,128)} %param.7, f32[]{:T(128)} %constant.23.clone.1), padding=0_0x0_934 | pad | bytes 668012 | tf_op jit(solution)/shard_map/jit(_pad)/pad | solution.py:61
  14.2 1.9 %pad.15 = f32[1,83968]{1,0:T(1,128)} pad(f32[1,83034]{1,0:T(1,128)} %param.8, f32[]{:T(128)} %constant.23.clone.1), padding=0_0x0_934 | pad | bytes 668012 | tf_op jit(solution)/shard_map/jit(_pad)/pad | solution.py:61
  16.1 1.9 %pad.16 = f32[1,83968]{1,0:T(1,128)} pad(f32[1,83034]{1,0:T(1,128)} %param.9, f32[]{:T(128)} %constant.23.clone.1), padding=0_0x0_934 | pad | bytes 668012 | tf_op jit(solution)/shard_map/jit(_pad)/pad | solution.py:61
  18.1 0.6 pad_add_fusion.scalars_ref
  18.7 2.9 %shard_map.118 = (f32[656,128]{1,0:T(8,128)}, f32[656,128]{1,0:T(8,128)}, f32[656,128]{1,0:T(8,128)}, f32[16,128]{1,0:T(8,128)}) custom-call(s32[8]{0:T(128)} %pad_add_fusion.scalars_ref, f32[7]{0:T(128)} %select_reduce_fusion.3.decay_ref, f32[656,128]{1,0:T(8,128)} %bitcast.14, f32[656,128]{1,0:T(8,128)} %bitcast.16, f32[656,128]{1,0:T(8,128)} %bitcast.17, ...), custom_call_target="tpu_custom_call" | custom-call | tf_op jit(solution)/shard_map/pallas_call | solution.py:174
  21.6 3.2 %collective-permute-start = (f32[16,128]{1,0:T(8,128)}, f32[16,128]{1,0:T(8,128)S(1)}, u32[]{:S(2)}, u32[]{:S(2)}) collective-permute-start(f32[16,128]{1,0:T(8,128)} %get-tuple-element.13), channel_id=1, source_target_pairs={{0,8},{8,0},{16,24},{24,16},{32,40},{40,32},{48,56},{56,48},{64,72... | collective-permute-start | bytes 24584 | tf_op jit(solution)/shard_map/ppermute | solution.py:55
  24.8 1.0 collective-permute-done
  25.8 0.7 add.39
  26.5 0.0 collective-permute-start.1
  26.5 2.5 %collective-permute-done.1 = f32[16,128]{1,0:T(8,128)S(1)} collective-permute-done((f32[16,128]{1,0:T(8,128)S(1)}, f32[16,128]{1,0:T(8,128)S(1)}, u32[]{:S(2)}, u32[]{:S(2)}) %collective-permute-start.1) | collective-permute-done | bytes 8224 | tf_op jit(solution)/shard_map/ppermute | solution.py:55
  29.0 1.0 collective-permute-start.2
  30.1 3.0 %collective-permute-done.2 = f32[16,128]{1,0:T(8,128)S(1)} collective-permute-done((f32[16,128]{1,0:T(8,128)S(1)}, f32[16,128]{1,0:T(8,128)S(1)}, u32[]{:S(2)}, u32[]{:S(2)}) %collective-permute-start.2) | collective-permute-done | bytes 8224 | tf_op jit(solution)/shard_map/ppermute | solution.py:55
  33.0 0.0 collective-permute-start.3
  33.1 2.5 %collective-permute-done.3 = f32[16,128]{1,0:T(8,128)S(1)} collective-permute-done((f32[16,128]{1,0:T(8,128)S(1)}, f32[16,128]{1,0:T(8,128)S(1)}, u32[]{:S(2)}, u32[]{:S(2)}) %collective-permute-start.3) | collective-permute-done | bytes 8224 | tf_op jit(solution)/shard_map/ppermute | solution.py:55
  35.6 1.2 collective-permute-start.4
  36.8 2.8 %collective-permute-done.4 = f32[16,128]{1,0:T(8,128)S(1)} collective-permute-done((f32[16,128]{1,0:T(8,128)S(1)}, f32[16,128]{1,0:T(8,128)S(1)}, u32[]{:S(2)}, u32[]{:S(2)}) %collective-permute-start.4) | collective-permute-done | bytes 8224 | tf_op jit(solution)/shard_map/ppermute | solution.py:55
  39.6 0.0 collective-permute-start.5
  39.6 2.5 %collective-permute-done.5 = f32[16,128]{1,0:T(8,128)S(1)} collective-permute-done((f32[16,128]{1,0:T(8,128)S(1)}, f32[16,128]{1,0:T(8,128)S(1)}, u32[]{:S(2)}, u32[]{:S(2)}) %collective-permute-start.5) | collective-permute-done | bytes 8224 | tf_op jit(solution)/shard_map/ppermute | solution.py:55
  42.1 1.5 %collective-permute-start.6 = (f32[16,128]{1,0:T(8,128)S(1)}, f32[16,128]{1,0:T(8,128)S(1)}, u32[]{:S(2)}, u32[]{:S(2)}) collective-permute-start(f32[16,128]{1,0:T(8,128)S(1)} %add.44), channel_id=1, source_target_pairs={{0,2},{1,3},{2,0},{3,1},{4,6},{5,7},{6,4},{7,5},{8,10},{9,11},{10,... | collective-permute-start | bytes 24584 | tf_op jit(solution)/shard_map/ppermute | solution.py:55
  43.5 1.9 %collective-permute-done.6 = f32[16,128]{1,0:T(8,128)S(1)} collective-permute-done((f32[16,128]{1,0:T(8,128)S(1)}, f32[16,128]{1,0:T(8,128)S(1)}, u32[]{:S(2)}, u32[]{:S(2)}) %collective-permute-start.6) | collective-permute-done | bytes 8224 | tf_op jit(solution)/shard_map/ppermute | solution.py:55
  45.5 5.2 %collective-permute-start.7 = (f32[16,128]{1,0:T(8,128)S(1)}, f32[16,128]{1,0:T(8,128)S(1)}, u32[]{:S(2)}, u32[]{:S(2)}) collective-permute-start(f32[16,128]{1,0:T(8,128)S(1)} %add.45), channel_id=1, source_target_pairs={{0,4},{1,5},{2,6},{3,7},{4,0},{5,1},{6,2},{7,3},{8,12},{9,13},{10,... | collective-permute-start | bytes 24584 | tf_op jit(solution)/shard_map/ppermute | solution.py:55
  50.7 1.2 collective-permute-done.7
  51.9 0.1 add_reduce_fusion
  52.0 0.1 fusion
  52.1 0.7 select_reduce_fusion.2
  52.9 0.0 copy-start
  52.9 1.3 select_reduce_fusion.trust_ref
  54.2 2.4 %shard_map.119 = (f32[656,128]{1,0:T(8,128)}, f32[656,128]{1,0:T(8,128)}, bf16[656,128]{1,0:T(8,128)(2,1)}) custom-call(s32[8]{0:T(128)} %pad_add_fusion.scalars_ref, f32[7]{0:T(128)} %select_reduce_fusion.trust_ref, f32[656,128]{1,0:T(8,128)} %bitcast.15, f32[656,128]{1,0:T(8,128)} %get-tuple-element.14.raw_ref), custom_call_target="tpu_custom_call" | custom-call | tf_op jit(solution)/shard_map/pallas_call | solution.py:186
  56.7 0.0 all-gather.3.cloned.1.call-update
  56.7 1.7 %slice.33 = f32[1,83034]{1,0:T(1,128)} slice(f32[1,83968]{1,0:T(1,128)} %bitcast.20), slice={[0:1], [0:83034]} | slice | bytes 664272 | tf_op jit(solution)/shard_map/slice | solution.py:65
  58.4 1.7 %slice.34 = f32[1,83034]{1,0:T(1,128)} slice(f32[1,83968]{1,0:T(1,128)} %bitcast.19), slice={[0:1], [0:83034]} | slice | bytes 664272 | tf_op jit(solution)/shard_map/slice | solution.py:65
  60.1 1.7 %slice.32 = f32[1,83034]{1,0:T(1,128)} slice(f32[1,83968]{1,0:T(1,128)} %bitcast.22), slice={[0:1], [0:83034]} | slice | bytes 664272 | tf_op jit(solution)/shard_map/slice | solution.py:65
  61.9 1.7 %slice.35 = f32[1,83034]{1,0:T(1,128)} slice(f32[1,83968]{1,0:T(1,128)} %bitcast.21), slice={[0:1], [0:83034]} | slice | bytes 664272 | tf_op jit(solution)/shard_map/slice | solution.py:65
  63.6 55.0 %all-gather.3.cloned.1.call-done = bf16[20992,128]{1,0:T(8,128)(2,1)} async-done(((bf16[656,128]{1,0:T(8,128)(2,1)}), bf16[20992,128]{1,0:T(8,128)(2,1)}) %all-gather.3.cloned.1.call-update) | async-done | bytes 5373968 | tf_op jit(solution)/shard_map/all_gather | solution.py:192
  118.6 16.1 %shard_map.120 = bf16[1,2657088]{1,0:T(2,128)(2,1)} custom-call(bf16[32,656,128]{2,1,0:T(8,128)(2,1)} %bitcast.13), custom_call_target="tpu_custom_call" | custom-call | tf_op jit(solution)/shard_map/pallas_call | solution.py:141
  134.8 0.0 copy-done
  (8 shorter events, 0.0 us)
Async XLA Ops:
  7.2 111.5 %all-gather.3.cloned.1.call-start = ((), (), s32[]{:S(2)}) async-start(), calls=%async_computation | async-start | bytes 5541888 | tf_op jit(solution)/shard_map/all_gather | solution.py:192
  21.6 4.2 %collective-permute-start = (f32[16,128]{1,0:T(8,128)}, f32[16,128]{1,0:T(8,128)S(1)}, u32[]{:S(2)}, u32[]{:S(2)}) collective-permute-start(f32[16,128]{1,0:T(8,128)} %get-tuple-element.13), channel_id=1, source_target_pairs={{0,8},{8,0},{16,24},{24,16},{32,40},{40,32},{48,56},{56,48},{64,72... | collective-permute-start | bytes 24584 | tf_op jit(solution)/shard_map/ppermute | solution.py:55
  26.5 2.5 %collective-permute-start.1 = (f32[16,128]{1,0:T(8,128)S(1)}, f32[16,128]{1,0:T(8,128)S(1)}, u32[]{:S(2)}, u32[]{:S(2)}) collective-permute-start(f32[16,128]{1,0:T(8,128)S(1)} %add.39), channel_id=1, source_target_pairs={{0,16},{8,24},{16,0},{24,8},{32,48},{40,56},{48,32},{56,40},{64,80... | collective-permute-start | bytes 24584 | tf_op jit(solution)/shard_map/ppermute | solution.py:55
  29.0 4.0 %collective-permute-start.2 = (f32[16,128]{1,0:T(8,128)S(1)}, f32[16,128]{1,0:T(8,128)S(1)}, u32[]{:S(2)}, u32[]{:S(2)}) collective-permute-start(f32[16,128]{1,0:T(8,128)S(1)} %add.40), channel_id=1, source_target_pairs={{0,32},{8,40},{16,48},{24,56},{32,0},{40,8},{48,16},{56,24},{64,96... | collective-permute-start | bytes 24584 | tf_op jit(solution)/shard_map/ppermute | solution.py:55
  33.0 2.5 %collective-permute-start.3 = (f32[16,128]{1,0:T(8,128)S(1)}, f32[16,128]{1,0:T(8,128)S(1)}, u32[]{:S(2)}, u32[]{:S(2)}) collective-permute-start(f32[16,128]{1,0:T(8,128)S(1)} %add.41), channel_id=1, source_target_pairs={{0,64},{8,72},{16,80},{24,88},{32,96},{40,104},{48,112},{56,120},{... | collective-permute-start | bytes 24584 | tf_op jit(solution)/shard_map/ppermute | solution.py:55
  35.6 4.0 %collective-permute-start.4 = (f32[16,128]{1,0:T(8,128)S(1)}, f32[16,128]{1,0:T(8,128)S(1)}, u32[]{:S(2)}, u32[]{:S(2)}) collective-permute-start(f32[16,128]{1,0:T(8,128)S(1)} %add.42), channel_id=1, source_target_pairs={{0,128},{8,136},{16,144},{24,152},{32,160},{40,168},{48,176},{56,1... | collective-permute-start | bytes 24584 | tf_op jit(solution)/shard_map/ppermute | solution.py:55
  39.6 2.5 %collective-permute-start.5 = (f32[16,128]{1,0:T(8,128)S(1)}, f32[16,128]{1,0:T(8,128)S(1)}, u32[]{:S(2)}, u32[]{:S(2)}) collective-permute-start(f32[16,128]{1,0:T(8,128)S(1)} %add.43), channel_id=1, source_target_pairs={{0,1},{1,0},{2,3},{3,2},{4,5},{5,4},{6,7},{7,6},{8,9},{9,8},{10,11... | collective-permute-start | bytes 24584 | tf_op jit(solution)/shard_map/ppermute | solution.py:55
  42.1 3.4 %collective-permute-start.6 = (f32[16,128]{1,0:T(8,128)S(1)}, f32[16,128]{1,0:T(8,128)S(1)}, u32[]{:S(2)}, u32[]{:S(2)}) collective-permute-start(f32[16,128]{1,0:T(8,128)S(1)} %add.44), channel_id=1, source_target_pairs={{0,2},{1,3},{2,0},{3,1},{4,6},{5,7},{6,4},{7,5},{8,10},{9,11},{10,... | collective-permute-start | bytes 24584 | tf_op jit(solution)/shard_map/ppermute | solution.py:55
  45.5 6.4 %collective-permute-start.7 = (f32[16,128]{1,0:T(8,128)S(1)}, f32[16,128]{1,0:T(8,128)S(1)}, u32[]{:S(2)}, u32[]{:S(2)}) collective-permute-start(f32[16,128]{1,0:T(8,128)S(1)} %add.45), channel_id=1, source_target_pairs={{0,4},{1,5},{2,6},{3,7},{4,0},{5,1},{6,2},{7,3},{8,12},{9,13},{10,... | collective-permute-start | bytes 24584 | tf_op jit(solution)/shard_map/ppermute | solution.py:55
  52.9 81.9 %copy-start = (f32[7]{0:T(128)}, f32[7]{0:T(128)S(1)}, u32[]{:S(2)}) copy-start(f32[7]{0:T(128)S(1)} %add_divide_fusion) | copy-start | bytes 88
Sparse Core Ops, SparseCore 0:
  56.8 61.7 all-gather.2

commit v7 on v6

--- a/solution.py
+++ b/solution.py
@@ -84,16 +84,29 @@
     return result
 
 
-def moments_kernel(scalars_ref, decay_ref, w_ref, m1_ref, m2_ref, g_ref, nf_ref, ns_ref, raw_ref, sums_ref):
-    rows = w_ref.shape[0]
+def load_dense(row_ref, rows, width):
+    block = row_ref[...].astype(jnp.float32).reshape(rows, 128)
+    inside = (
+        lax.broadcasted_iota(jnp.int32, (rows, 128), 0) * 128
+        + lax.broadcasted_iota(jnp.int32, (rows, 128), 1)
+    ) < width
+    return jnp.where(inside, block, 0.0)
+
+
+def store_row(row_ref, block):
+    row_ref[...] = block.reshape(row_ref.shape).astype(row_ref.dtype)
+
+
+def moments_kernel(width, scalars_ref, decay_ref, w_ref, m1_ref, m2_ref, g_ref, nf_ref, ns_ref, raw_ref, sums_ref):
+    rows = raw_ref.shape[0]
     slot = slot_of(scalars_ref, rows)
-    grads = g_ref[...].astype(jnp.float32)
-    new_first = 0.9 * m1_ref[...] + 0.1 * grads
-    new_second = 0.999 * m2_ref[...] + 0.001 * grads * grads
-    w = w_ref[...]
+    grads = load_dense(g_ref, rows, width)
+    new_first = 0.9 * load_dense(m1_ref, rows, width) + 0.1 * grads
+    new_second = 0.999 * load_dense(m2_ref, rows, width) + 0.001 * grads * grads
+    w = load_dense(w_ref, rows, width)
     raw = new_first / fix_first / (jnp.sqrt(new_second / fix_second) + 1e-06) + per_slot(slot, decay_ref) * w
-    nf_ref[...] = new_first
-    ns_ref[...] = new_second
+    store_row(nf_ref, new_first)
+    store_row(ns_ref, new_second)
     raw_ref[...] = raw
     wsq = w * w
     usq = raw * raw
@@ -104,13 +117,13 @@
         sums_ref[pl.ds(8 + number, 1), :] = jnp.sum(jnp.where(mask, usq, 0.0), axis=0, keepdims=True)
 
 
-def update_kernel(scalars_ref, trust_ref, w_ref, raw_ref, su_ref, nw_ref, tc_ref):
-    rows = w_ref.shape[0]
+def update_kernel(width, scalars_ref, trust_ref, w_ref, raw_ref, su_ref, nw_ref, tc_ref):
+    rows = raw_ref.shape[0]
     slot = slot_of(scalars_ref, rows)
     scaled_update = per_slot(slot, trust_ref) * raw_ref[...]
-    new_weights = w_ref[...] - step_rate * scaled_update
-    su_ref[...] = scaled_update
-    nw_ref[...] = new_weights
+    new_weights = load_dense(w_ref, rows, width) - step_rate * scaled_update
+    store_row(su_ref, scaled_update)
+    store_row(nw_ref, new_weights)
     tc_ref[...] = new_weights.astype(jnp.bfloat16)
 
 
@@ -146,19 +159,11 @@
     )(whole)
 
 
-SMEM = pl.BlockSpec(memory_space=pltpu.SMEM)
-VMEM = pl.BlockSpec(memory_space=pltpu.VMEM)
-
-
 def on_device(weights, moment_first, moment_second, gradients, tensor_order):
     parts = lax.axis_size("mp")
     width = weights.shape[1]
     padded = -(-width // 2048) * 2048
     rows = padded // 128
-    w = to_dense(weights, padded)
-    m1 = to_dense(moment_first, padded)
-    m2 = to_dense(moment_second, padded)
-    g = to_dense(gradients, padded)
     lengths = jnp.array(
         [D * D // parts] * 4 + [EXPERTS * D // parts, D // parts, D // parts], jnp.int32
     )
@@ -171,12 +176,17 @@
     ).astype(jnp.int32)
     decay_slot = jnp.sum(jnp.where(matches, jnp.array(decay_values, jnp.float32)[None, :], 0.0), axis=1)
     dense = jax.ShapeDtypeStruct((rows, 128), jnp.float32)
+    row = jax.ShapeDtypeStruct((1, width), jnp.float32)
+    row_block = pl.BlockSpec((1, padded), lambda i: (0, 0))
+    whole_block = lambda shape: pl.BlockSpec(shape, lambda i: (0, 0))
+    scalar_block = pl.BlockSpec(memory_space=pltpu.SMEM)
     new_first, new_second, raw, sums = pl.pallas_call(
-        moments_kernel,
-        out_shape=(dense, dense, dense, jax.ShapeDtypeStruct((16, 128), jnp.float32)),
-        in_specs=[SMEM, SMEM, VMEM, VMEM, VMEM, VMEM],
-        out_specs=(VMEM, VMEM, VMEM, VMEM),
-    )(scalars, decay_slot, w, m1, m2, g)
+        functools.partial(moments_kernel, width),
+        grid=(1,),
+        out_shape=(row, row, dense, jax.ShapeDtypeStruct((16, 128), jnp.float32)),
+        in_specs=[scalar_block, scalar_block, row_block, row_block, row_block, row_block],
+        out_specs=(row_block, row_block, whole_block((rows, 128)), whole_block((16, 128))),
+    )(scalars, decay_slot, weights, moment_first, moment_second, gradients)
     total = jnp.sum(tree_sum(tree_sum(sums, "dp"), "mp"), axis=1)
     wsq_slot, usq_slot = total[:SLOTS], total[8 : 8 + SLOTS]
     wsq = jnp.sum(jnp.where(matches, wsq_slot[:, None], 0.0), axis=0)
@@ -184,21 +194,15 @@
     trust = jnp.sqrt(wsq) / (jnp.sqrt(usq) + 1e-06)
     trust_slot = jnp.sum(jnp.where(matches, trust[None, :], 0.0), axis=1)
     scaled_update, new_weights, piece = pl.pallas_call(
-        update_kernel,
-        out_shape=(dense, dense, jax.ShapeDtypeStruct((rows, 128), jnp.bfloat16)),
-        in_specs=[SMEM, SMEM, VMEM, VMEM],
-        out_specs=(VMEM, VMEM, VMEM),
-    )(scalars, trust_slot, w, raw)
+        functools.partial(update_kernel, width),
+        grid=(1,),
+        out_shape=(row, row, jax.ShapeDtypeStruct((rows, 128), jnp.bfloat16)),
+        in_specs=[scalar_block, scalar_block, row_block, whole_block((rows, 128))],
+        out_specs=(row_block, row_block, whole_block((rows, 128))),
+    )(scalars, trust_slot, weights, raw)
     whole = lax.all_gather(piece, "dp", axis=0, tiled=False)
     training_copy = assemble(whole, width)
-    return (
-        from_dense(new_weights, width),
-        from_dense(new_first, width),
-        from_dense(new_second, width),
-        from_dense(scaled_update, width),
-        training_copy,
-        trust,
-    )
+    return (new_weights, new_first, new_second, scaled_update, training_copy, trust)
 
 
 def solution(mesh):

time: 142 us -> 134 us (0.944)
  local copies, waits for them, and re-layouts: 15.4 us -> 0.09 us
  waiting for transfers between devices: 72.5 us -> 79.4 us
    pad x4 -> x0, local copies, waits for them, and re-layouts: 8.44 us -> none  [to_dense(): jnp.pad(row, ((0, 0), (0, padded - row.shape[1])))]
    all_gather x1, waiting for transfers between devices: 55 us -> 61.9 us  [on_device(): whole = lax.all_gather(piece, 'dp', axis=0, tiled=False)]
    slice x4 -> x0, local copies, waits for them, and re-layouts: 6.89 us -> none  [from_dense(): return block.reshape(1, -1)[:, :width]]
  transfers between devices with their start and end apart: 9 -> 9, of which waited for: 9 -> 9; matrix products, arithmetic and copies ran while one was open for 5% -> 0% of each run, Pallas kernels for 0% -> 0%
where the time goes in v7:
time: 134 us
  waiting for transfers between devices  79.4 us (59%)
  Pallas kernels  22 us (16%)
  between operations  14.1 us (11%)
  starting transfers between devices  12.1 us (9%)
  other arithmetic  6 us (4%)
    all_gather x1, waiting for transfers between devices, on_device(): whole = lax.all_gather(piece, 'dp', axis=0, tiled=False)  61.9 us
    ppermute x8, waiting for transfers between devices, tree_sum(): x = x + lax.ppermute(x, axis, pairs)  17.5 us
    pallas_call x1, Pallas kernels, assemble(): pl.pallas_call(functools.partial(assemble_kernel, width), out_shape=jax.S...  16.1 us
    ppermute x8, starting transfers between devices, tree_sum(): x = x + lax.ppermute(x, axis, pairs)  12.1 us
    pallas_call x1, Pallas kernels, on_device(): pl.pallas_call(functools.partial(moments_kernel, width), grid=(1,), out_s...  3.38 us
  transfers between devices with their start and end apart: 9, of which 9 were waited for; matrix products, arithmetic and copies ran while one was open for 0% of the time, Pallas kernels for 0%

profile of v7, /device:TPU:1, one launch (start us, length us, event | category | flops | bytes accessed | tf_op | source)
XLA Modules:
  0.0 133.7 jit_solution(6761794584292757607)
XLA Ops:
  7.2 0.0 all-gather.3.cloned.1.call-start
  7.2 0.9 select_reduce_fusion.4
  8.1 0.2 reduce-window.4
  8.3 1.4 %select_reduce_fusion.3.decay_ref = f32[7]{0:T(128)} fusion(f32[7]{0:T(128)} %constant.24.clone, s32[7]{0:T(128)} %param.11), kind=kLoop, calls=%fused_computation.4 | loop fusion | flops 140 | bytes 84 | tf_op jit(solution)/shard_map/reduce_sum | solution.py:177
  9.6 0.7 pad_add_fusion.scalars_ref
  10.3 3.4 %shard_map.118 = (f32[1,83034]{1,0:T(1,128)}, f32[1,83034]{1,0:T(1,128)}, f32[656,128]{1,0:T(8,128)}, f32[16,128]{1,0:T(8,128)}) custom-call(s32[8]{0:T(128)} %pad_add_fusion.scalars_ref, f32[7]{0:T(128)} %select_reduce_fusion.3.decay_ref, f32[1,83034]{1,0:T(1,128)} %w_ref.3, f32[1,83034]{1,0:T(1,128)} %m1_ref.1, f32[1,83034]{1,0:T(1,128)} %m2_ref.1, ...), custom_call_target="tpu_custom_call" | custom-call | tf_op jit(solution)/shard_map/pallas_call | solution.py:183
  13.7 3.2 %collective-permute-start = (f32[16,128]{1,0:T(8,128)}, f32[16,128]{1,0:T(8,128)S(1)}, u32[]{:S(2)}, u32[]{:S(2)}) collective-permute-start(f32[16,128]{1,0:T(8,128)} %get-tuple-element.13), channel_id=1, source_target_pairs={{0,8},{8,0},{16,24},{24,16},{32,40},{40,32},{48,56},{56,48},{64,72... | collective-permute-start | bytes 24584 | tf_op jit(solution)/shard_map/ppermute | solution.py:55
  16.9 1.0 collective-permute-done
  17.9 0.7 add.31
  18.6 0.0 collective-permute-start.1
  18.6 2.5 %collective-permute-done.1 = f32[16,128]{1,0:T(8,128)S(1)} collective-permute-done((f32[16,128]{1,0:T(8,128)S(1)}, f32[16,128]{1,0:T(8,128)S(1)}, u32[]{:S(2)}, u32[]{:S(2)}) %collective-permute-start.1) | collective-permute-done | bytes 8224 | tf_op jit(solution)/shard_map/ppermute | solution.py:55
  21.1 1.0 collective-permute-start.2
  22.2 3.0 %collective-permute-done.2 = f32[16,128]{1,0:T(8,128)S(1)} collective-permute-done((f32[16,128]{1,0:T(8,128)S(1)}, f32[16,128]{1,0:T(8,128)S(1)}, u32[]{:S(2)}, u32[]{:S(2)}) %collective-permute-start.2) | collective-permute-done | bytes 8224 | tf_op jit(solution)/shard_map/ppermute | solution.py:55
  25.1 0.0 collective-permute-start.3
  25.1 2.5 %collective-permute-done.3 = f32[16,128]{1,0:T(8,128)S(1)} collective-permute-done((f32[16,128]{1,0:T(8,128)S(1)}, f32[16,128]{1,0:T(8,128)S(1)}, u32[]{:S(2)}, u32[]{:S(2)}) %collective-permute-start.3) | collective-permute-done | bytes 8224 | tf_op jit(solution)/shard_map/ppermute | solution.py:55
  27.6 1.2 collective-permute-start.4
  28.8 2.8 %collective-permute-done.4 = f32[16,128]{1,0:T(8,128)S(1)} collective-permute-done((f32[16,128]{1,0:T(8,128)S(1)}, f32[16,128]{1,0:T(8,128)S(1)}, u32[]{:S(2)}, u32[]{:S(2)}) %collective-permute-start.4) | collective-permute-done | bytes 8224 | tf_op jit(solution)/shard_map/ppermute | solution.py:55
  31.6 0.0 collective-permute-start.5
  31.7 2.5 %collective-permute-done.5 = f32[16,128]{1,0:T(8,128)S(1)} collective-permute-done((f32[16,128]{1,0:T(8,128)S(1)}, f32[16,128]{1,0:T(8,128)S(1)}, u32[]{:S(2)}, u32[]{:S(2)}) %collective-permute-start.5) | collective-permute-done | bytes 8224 | tf_op jit(solution)/shard_map/ppermute | solution.py:55
  34.2 1.5 %collective-permute-start.6 = (f32[16,128]{1,0:T(8,128)S(1)}, f32[16,128]{1,0:T(8,128)S(1)}, u32[]{:S(2)}, u32[]{:S(2)}) collective-permute-start(f32[16,128]{1,0:T(8,128)S(1)} %add.36), channel_id=1, source_target_pairs={{0,2},{1,3},{2,0},{3,1},{4,6},{5,7},{6,4},{7,5},{8,10},{9,11},{10,... | collective-permute-start | bytes 24584 | tf_op jit(solution)/shard_map/ppermute | solution.py:55
  35.6 1.9 %collective-permute-done.6 = f32[16,128]{1,0:T(8,128)S(1)} collective-permute-done((f32[16,128]{1,0:T(8,128)S(1)}, f32[16,128]{1,0:T(8,128)S(1)}, u32[]{:S(2)}, u32[]{:S(2)}) %collective-permute-start.6) | collective-permute-done | bytes 8224 | tf_op jit(solution)/shard_map/ppermute | solution.py:55
  37.6 5.2 %collective-permute-start.7 = (f32[16,128]{1,0:T(8,128)S(1)}, f32[16,128]{1,0:T(8,128)S(1)}, u32[]{:S(2)}, u32[]{:S(2)}) collective-permute-start(f32[16,128]{1,0:T(8,128)S(1)} %add.37), channel_id=1, source_target_pairs={{0,4},{1,5},{2,6},{3,7},{4,0},{5,1},{6,2},{7,3},{8,12},{9,13},{10,... | collective-permute-start | bytes 24584 | tf_op jit(solution)/shard_map/ppermute | solution.py:55
  42.8 1.2 collective-permute-done.7
  44.0 0.1 add_reduce_fusion
  44.1 0.1 fusion
  44.2 0.7 select_reduce_fusion.2
  44.9 0.0 copy-start
  45.0 1.3 %select_reduce_fusion.trust_ref = f32[7]{0:T(128)} fusion(f32[7]{0:T(128)S(1)} %add_divide_fusion, s32[7]{0:T(128)} %param.11), kind=kLoop, calls=%fused_computation.1 | loop fusion | flops 140 | bytes 84 | tf_op jit(solution)/shard_map/reduce_sum | solution.py:195
  46.3 2.4 %shard_map.119 = (f32[1,83034]{1,0:T(1,128)}, f32[1,83034]{1,0:T(1,128)}, bf16[656,128]{1,0:T(8,128)(2,1)}) custom-call(s32[8]{0:T(128)} %pad_add_fusion.scalars_ref, f32[7]{0:T(128)} %select_reduce_fusion.trust_ref, f32[1,83034]{1,0:T(1,128)} %w_ref.3, f32[656,128]{1,0:T(8,128)} %get-tuple-element.14.raw_ref), custom_call_target="tpu_custom_call" | custom-call | tf_op jit(solution)/shard_map/pallas_call | solution.py:196
  48.7 0.0 all-gather.3.cloned.1.call-update
  48.8 61.9 %all-gather.3.cloned.1.call-done = bf16[20992,128]{1,0:T(8,128)(2,1)} async-done(((bf16[656,128]{1,0:T(8,128)(2,1)}), bf16[20992,128]{1,0:T(8,128)(2,1)}) %all-gather.3.cloned.1.call-update) | async-done | bytes 5373968 | tf_op jit(solution)/shard_map/all_gather | solution.py:203
  110.7 16.1 %shard_map.120 = bf16[1,2657088]{1,0:T(2,128)(2,1)} custom-call(bf16[32,656,128]{2,1,0:T(8,128)(2,1)} %bitcast.5), custom_call_target="tpu_custom_call" | custom-call | tf_op jit(solution)/shard_map/pallas_call | solution.py:154
  126.8 0.0 copy-done
  (8 shorter events, 0.0 us)
Async XLA Ops:
  7.2 103.5 %all-gather.3.cloned.1.call-start = ((), (), s32[]{:S(2)}) async-start(), calls=%async_computation | async-start | bytes 5541888 | tf_op jit(solution)/shard_map/all_gather | solution.py:203
  13.7 4.2 %collective-permute-start = (f32[16,128]{1,0:T(8,128)}, f32[16,128]{1,0:T(8,128)S(1)}, u32[]{:S(2)}, u32[]{:S(2)}) collective-permute-start(f32[16,128]{1,0:T(8,128)} %get-tuple-element.13), channel_id=1, source_target_pairs={{0,8},{8,0},{16,24},{24,16},{32,40},{40,32},{48,56},{56,48},{64,72... | collective-permute-start | bytes 24584 | tf_op jit(solution)/shard_map/ppermute | solution.py:55
  18.6 2.5 %collective-permute-start.1 = (f32[16,128]{1,0:T(8,128)S(1)}, f32[16,128]{1,0:T(8,128)S(1)}, u32[]{:S(2)}, u32[]{:S(2)}) collective-permute-start(f32[16,128]{1,0:T(8,128)S(1)} %add.31), channel_id=1, source_target_pairs={{0,16},{8,24},{16,0},{24,8},{32,48},{40,56},{48,32},{56,40},{64,80... | collective-permute-start | bytes 24584 | tf_op jit(solution)/shard_map/ppermute | solution.py:55
  21.1 4.0 %collective-permute-start.2 = (f32[16,128]{1,0:T(8,128)S(1)}, f32[16,128]{1,0:T(8,128)S(1)}, u32[]{:S(2)}, u32[]{:S(2)}) collective-permute-start(f32[16,128]{1,0:T(8,128)S(1)} %add.32), channel_id=1, source_target_pairs={{0,32},{8,40},{16,48},{24,56},{32,0},{40,8},{48,16},{56,24},{64,96... | collective-permute-start | bytes 24584 | tf_op jit(solution)/shard_map/ppermute | solution.py:55
  25.1 2.5 %collective-permute-start.3 = (f32[16,128]{1,0:T(8,128)S(1)}, f32[16,128]{1,0:T(8,128)S(1)}, u32[]{:S(2)}, u32[]{:S(2)}) collective-permute-start(f32[16,128]{1,0:T(8,128)S(1)} %add.33), channel_id=1, source_target_pairs={{0,64},{8,72},{16,80},{24,88},{32,96},{40,104},{48,112},{56,120},{... | collective-permute-start | bytes 24584 | tf_op jit(solution)/shard_map/ppermute | solution.py:55
  27.6 4.0 %collective-permute-start.4 = (f32[16,128]{1,0:T(8,128)S(1)}, f32[16,128]{1,0:T(8,128)S(1)}, u32[]{:S(2)}, u32[]{:S(2)}) collective-permute-start(f32[16,128]{1,0:T(8,128)S(1)} %add.34), channel_id=1, source_target_pairs={{0,128},{8,136},{16,144},{24,152},{32,160},{40,168},{48,176},{56,1... | collective-permute-start | bytes 24584 | tf_op jit(solution)/shard_map/ppermute | solution.py:55
  31.6 2.5 %collective-permute-start.5 = (f32[16,128]{1,0:T(8,128)S(1)}, f32[16,128]{1,0:T(8,128)S(1)}, u32[]{:S(2)}, u32[]{:S(2)}) collective-permute-start(f32[16,128]{1,0:T(8,128)S(1)} %add.35), channel_id=1, source_target_pairs={{0,1},{1,0},{2,3},{3,2},{4,5},{5,4},{6,7},{7,6},{8,9},{9,8},{10,11... | collective-permute-start | bytes 24584 | tf_op jit(solution)/shard_map/ppermute | solution.py:55
  34.2 3.4 %collective-permute-start.6 = (f32[16,128]{1,0:T(8,128)S(1)}, f32[16,128]{1,0:T(8,128)S(1)}, u32[]{:S(2)}, u32[]{:S(2)}) collective-permute-start(f32[16,128]{1,0:T(8,128)S(1)} %add.36), channel_id=1, source_target_pairs={{0,2},{1,3},{2,0},{3,1},{4,6},{5,7},{6,4},{7,5},{8,10},{9,11},{10,... | collective-permute-start | bytes 24584 | tf_op jit(solution)/shard_map/ppermute | solution.py:55
  37.6 6.4 %collective-permute-start.7 = (f32[16,128]{1,0:T(8,128)S(1)}, f32[16,128]{1,0:T(8,128)S(1)}, u32[]{:S(2)}, u32[]{:S(2)}) collective-permute-start(f32[16,128]{1,0:T(8,128)S(1)} %add.37), channel_id=1, source_target_pairs={{0,4},{1,5},{2,6},{3,7},{4,0},{5,1},{6,2},{7,3},{8,12},{9,13},{10,... | collective-permute-start | bytes 24584 | tf_op jit(solution)/shard_map/ppermute | solution.py:55
  44.9 81.9 %copy-start = (f32[7]{0:T(128)}, f32[7]{0:T(128)S(1)}, u32[]{:S(2)}) copy-start(f32[7]{0:T(128)S(1)} %add_divide_fusion) | copy-start | bytes 88
Sparse Core Ops, SparseCore 0:
  48.9 61.7 all-gather.2

commit v8 on v7

--- a/solution.py
+++ b/solution.py
@@ -65,22 +65,33 @@
     return block.reshape(1, -1)[:, :width]
 
 
-def slot_of(scalars_ref, rows):
+def slot_of(order_ref, width, parts, rows):
+    lengths = [D * D // parts] * 4 + [EXPERTS * D // parts, D // parts, D // parts]
     places = (
-        scalars_ref[SLOTS - 1]
+        lax.axis_index("dp") * width
         + lax.broadcasted_iota(jnp.int32, (rows, 128), 0) * 128
         + lax.broadcasted_iota(jnp.int32, (rows, 128), 1)
     )
     slot = jnp.zeros((rows, 128), jnp.int32)
+    boundary = jnp.int32(0)
     for number in range(SLOTS - 1):
-        slot = slot + (places >= scalars_ref[number]).astype(jnp.int32)
+        kind = order_ref[number]
+        length = jnp.int32(lengths[SLOTS - 1])
+        for other in range(SLOTS - 1):
+            length = jnp.where(kind == other, jnp.int32(lengths[other]), length)
+        boundary = boundary + length
+        slot = slot + (places >= boundary).astype(jnp.int32)
     return slot
 
 
-def per_slot(slot, table_ref):
+def decay_of(order_ref, slot):
     result = jnp.zeros(slot.shape, jnp.float32)
     for number in range(SLOTS):
-        result = jnp.where(slot == number, table_ref[number], result)
+        kind = order_ref[number]
+        value = jnp.float32(0.0)
+        for other in range(SLOTS):
+            value = jnp.where(kind == other, jnp.float32(decay_values[other]), value)
+        result = jnp.where(slot == number, value, result)
     return result
 
 
@@ -97,14 +108,14 @@
     row_ref[...] = block.reshape(row_ref.shape).astype(row_ref.dtype)
 
 
-def moments_kernel(width, scalars_ref, decay_ref, w_ref, m1_ref, m2_ref, g_ref, nf_ref, ns_ref, raw_ref, sums_ref):
+def moments_kernel(width, parts, order_ref, w_ref, m1_ref, m2_ref, g_ref, nf_ref, ns_ref, raw_ref, sums_ref):
     rows = raw_ref.shape[0]
-    slot = slot_of(scalars_ref, rows)
+    slot = slot_of(order_ref, width, parts, rows)
     grads = load_dense(g_ref, rows, width)
     new_first = 0.9 * load_dense(m1_ref, rows, width) + 0.1 * grads
     new_second = 0.999 * load_dense(m2_ref, rows, width) + 0.001 * grads * grads
     w = load_dense(w_ref, rows, width)
-    raw = new_first / fix_first / (jnp.sqrt(new_second / fix_second) + 1e-06) + per_slot(slot, decay_ref) * w
+    raw = new_first / fix_first / (jnp.sqrt(new_second / fix_second) + 1e-06) + decay_of(order_ref, slot) * w
     store_row(nf_ref, new_first)
     store_row(ns_ref, new_second)
     raw_ref[...] = raw
@@ -117,10 +128,15 @@
         sums_ref[pl.ds(8 + number, 1), :] = jnp.sum(jnp.where(mask, usq, 0.0), axis=0, keepdims=True)
 
 
-def update_kernel(width, scalars_ref, trust_ref, w_ref, raw_ref, su_ref, nw_ref, tc_ref):
+def update_kernel(width, parts, order_ref, total_ref, w_ref, raw_ref, su_ref, nw_ref, tc_ref):
     rows = raw_ref.shape[0]
-    slot = slot_of(scalars_ref, rows)
-    scaled_update = per_slot(slot, trust_ref) * raw_ref[...]
+    slot = slot_of(order_ref, width, parts, rows)
+    sums = jnp.sum(total_ref[...], axis=1, keepdims=True)
+    trust = jnp.sqrt(sums[:8]) / (jnp.sqrt(sums[8:]) + 1e-06)
+    factor = jnp.zeros((rows, 128), jnp.float32)
+    for number in range(SLOTS):
+        factor = jnp.where(slot == number, trust[number : number + 1, :], factor)
+    scaled_update = factor * raw_ref[...]
     new_weights = load_dense(w_ref, rows, width) - step_rate * scaled_update
     store_row(su_ref, scaled_update)
     store_row(nw_ref, new_weights)
@@ -164,44 +180,33 @@
     width = weights.shape[1]
     padded = -(-width // 2048) * 2048
     rows = padded // 128
-    lengths = jnp.array(
-        [D * D // parts] * 4 + [EXPERTS * D // parts, D // parts, D // parts], jnp.int32
-    )
-    kinds = jnp.arange(SLOTS, dtype=jnp.int32)
-    matches = tensor_order[:, None] == kinds[None, :]
-    slot_lengths = jnp.sum(jnp.where(matches, lengths[None, :], 0), axis=1)
-    boundary = jnp.cumsum(slot_lengths)
-    scalars = jnp.concatenate(
-        [boundary[: SLOTS - 1], (lax.axis_index("dp") * width)[None], jnp.zeros((1,), jnp.int32)]
-    ).astype(jnp.int32)
-    decay_slot = jnp.sum(jnp.where(matches, jnp.array(decay_values, jnp.float32)[None, :], 0.0), axis=1)
     dense = jax.ShapeDtypeStruct((rows, 128), jnp.float32)
     row = jax.ShapeDtypeStruct((1, width), jnp.float32)
     row_block = pl.BlockSpec((1, padded), lambda i: (0, 0))
     whole_block = lambda shape: pl.BlockSpec(shape, lambda i: (0, 0))
     scalar_block = pl.BlockSpec(memory_space=pltpu.SMEM)
     new_first, new_second, raw, sums = pl.pallas_call(
-        functools.partial(moments_kernel, width),
+        functools.partial(moments_kernel, width, parts),
         grid=(1,),
         out_shape=(row, row, dense, jax.ShapeDtypeStruct((16, 128), jnp.float32)),
-        in_specs=[scalar_block, scalar_block, row_block, row_block, row_block, row_block],
+        in_specs=[scalar_block, row_block, row_block, row_block, row_block],
         out_specs=(row_block, row_block, whole_block((rows, 128)), whole_block((16, 128))),
-    )(scalars, decay_slot, weights, moment_first, moment_second, gradients)
-    total = jnp.sum(tree_sum(tree_sum(sums, "dp"), "mp"), axis=1)
-    wsq_slot, usq_slot = total[:SLOTS], total[8 : 8 + SLOTS]
-    wsq = jnp.sum(jnp.where(matches, wsq_slot[:, None], 0.0), axis=0)
-    usq = jnp.sum(jnp.where(matches, usq_slot[:, None], 0.0), axis=0)
-    trust = jnp.sqrt(wsq) / (jnp.sqrt(usq) + 1e-06)
-    trust_slot = jnp.sum(jnp.where(matches, trust[None, :], 0.0), axis=1)
+    )(tensor_order, weights, moment_first, moment_second, gradients)
+    total = tree_sum(tree_sum(sums, "dp"), "mp")
     scaled_update, new_weights, piece = pl.pallas_call(
-        functools.partial(update_kernel, width),
+        functools.partial(update_kernel, width, parts),
         grid=(1,),
         out_shape=(row, row, jax.ShapeDtypeStruct((rows, 128), jnp.bfloat16)),
-        in_specs=[scalar_block, scalar_block, row_block, whole_block((rows, 128))],
+        in_specs=[scalar_block, whole_block((16, 128)), row_block, whole_block((rows, 128))],
         out_specs=(row_block, row_block, whole_block((rows, 128))),
-    )(scalars, trust_slot, weights, raw)
+    )(tensor_order, total, weights, raw)
     whole = lax.all_gather(piece, "dp", axis=0, tiled=False)
     training_copy = assemble(whole, width)
+    sums_by_slot = jnp.sum(total, axis=1)
+    matches = tensor_order[:, None] == jnp.arange(SLOTS, dtype=jnp.int32)[None, :]
+    wsq = jnp.sum(jnp.where(matches, sums_by_slot[:SLOTS, None], 0.0), axis=0)
+    usq = jnp.sum(jnp.where(matches, sums_by_slot[8 : 8 + SLOTS, None], 0.0), axis=0)
+    trust = jnp.sqrt(wsq) / (jnp.sqrt(usq) + 1e-06)
     return (new_weights, new_first, new_second, scaled_update, training_copy, trust)
 
 

time: 134 us -> 129 us (0.963)
  other arithmetic: 6 us -> 2.69 us
    reduce_sum x5 -> x2, other arithmetic: 4.42 us -> 1.45 us  [the longest x1 0.74 us: on_device(): wsq = jnp.sum(jnp.where(matches, sums_by_slot[:SLOTS, None], 0.0), axis=0)]
    all_gather x1, waiting for transfers between devices: 61.9 us -> 60.6 us  [on_device(): whole = lax.all_gather(piece, 'dp', axis=0, tiled=False)]
  transfers between devices with their start and end apart: 9 -> 9, of which waited for: 9 -> 9; matrix products, arithmetic and copies ran while one was open for 0% -> 1% of each run, Pallas kernels for 0% -> 0%
where the time goes in v8:
time: 129 us
  waiting for transfers between devices  78.1 us (61%)
  Pallas kernels  22.2 us (17%)
  between operations  14 us (11%)
  starting transfers between devices  12.1 us (9%)
  other arithmetic  2.69 us (2%)
    all_gather x1, waiting for transfers between devices, on_device(): whole = lax.all_gather(piece, 'dp', axis=0, tiled=False)  60.6 us
    ppermute x8, waiting for transfers between devices, tree_sum(): x = x + lax.ppermute(x, axis, pairs)  17.5 us
    pallas_call x1, Pallas kernels, assemble(): pl.pallas_call(functools.partial(assemble_kernel, width), out_shape=jax.S...  16.1 us
    ppermute x8, starting transfers between devices, tree_sum(): x = x + lax.ppermute(x, axis, pairs)  12.1 us
    pallas_call x1, Pallas kernels, on_device(): pl.pallas_call(functools.partial(moments_kernel, width, parts), grid=(1,)...  3.39 us
    pallas_call x1, Pallas kernels, on_device(): pl.pallas_call(functools.partial(update_kernel, width, parts), grid=(1,),...  2.68 us
  transfers between devices with their start and end apart: 9, of which 9 were waited for; matrix products, arithmetic and copies ran while one was open for 1% of the time, Pallas kernels for 0%

profile of v8, /device:TPU:1, one launch (start us, length us, event | category | flops | bytes accessed | tf_op | source)
XLA Modules:
  0.0 129.2 jit_solution(516356121906637914)
XLA Ops:
  7.2 0.0 all-gather.3.cloned.1.call-start
  7.2 3.4 %shard_map.100 = (f32[1,83034]{1,0:T(1,128)}, f32[1,83034]{1,0:T(1,128)}, f32[656,128]{1,0:T(8,128)}, f32[16,128]{1,0:T(8,128)}) custom-call(s32[7]{0:T(128)} %order_ref.3, f32[1,83034]{1,0:T(1,128)} %w_ref.3, f32[1,83034]{1,0:T(1,128)} %m1_ref.1, f32[1,83034]{1,0:T(1,128)} %m2_ref.1, bf16[1,83034]{1,0:T(2,128)(2,1)} %g_ref.1), custom_call_target="tpu_custom_call" | custom-call | tf_op jit(solution)/shard_map/pallas_call | solution.py:188
  10.6 3.2 %collective-permute-start = (f32[16,128]{1,0:T(8,128)}, f32[16,128]{1,0:T(8,128)S(1)}, u32[]{:S(2)}, u32[]{:S(2)}) collective-permute-start(f32[16,128]{1,0:T(8,128)} %get-tuple-element.13), channel_id=1, source_target_pairs={{0,8},{8,0},{16,24},{24,16},{32,40},{40,32},{48,56},{56,48},{64,72... | collective-permute-start | bytes 24584 | tf_op jit(solution)/shard_map/ppermute | solution.py:55
  13.8 1.0 collective-permute-done
  14.8 0.7 add.27
  15.5 0.0 collective-permute-start.1
  15.5 2.5 %collective-permute-done.1 = f32[16,128]{1,0:T(8,128)S(1)} collective-permute-done((f32[16,128]{1,0:T(8,128)S(1)}, f32[16,128]{1,0:T(8,128)S(1)}, u32[]{:S(2)}, u32[]{:S(2)}) %collective-permute-start.1) | collective-permute-done | bytes 8224 | tf_op jit(solution)/shard_map/ppermute | solution.py:55
  18.0 1.0 collective-permute-start.2
  19.1 3.0 %collective-permute-done.2 = f32[16,128]{1,0:T(8,128)S(1)} collective-permute-done((f32[16,128]{1,0:T(8,128)S(1)}, f32[16,128]{1,0:T(8,128)S(1)}, u32[]{:S(2)}, u32[]{:S(2)}) %collective-permute-start.2) | collective-permute-done | bytes 8224 | tf_op jit(solution)/shard_map/ppermute | solution.py:55
  22.1 0.0 collective-permute-start.3
  22.1 2.5 %collective-permute-done.3 = f32[16,128]{1,0:T(8,128)S(1)} collective-permute-done((f32[16,128]{1,0:T(8,128)S(1)}, f32[16,128]{1,0:T(8,128)S(1)}, u32[]{:S(2)}, u32[]{:S(2)}) %collective-permute-start.3) | collective-permute-done | bytes 8224 | tf_op jit(solution)/shard_map/ppermute | solution.py:55
  24.6 1.2 collective-permute-start.4
  25.8 2.8 %collective-permute-done.4 = f32[16,128]{1,0:T(8,128)S(1)} collective-permute-done((f32[16,128]{1,0:T(8,128)S(1)}, f32[16,128]{1,0:T(8,128)S(1)}, u32[]{:S(2)}, u32[]{:S(2)}) %collective-permute-start.4) | collective-permute-done | bytes 8224 | tf_op jit(solution)/shard_map/ppermute | solution.py:55
  28.6 0.0 collective-permute-start.5
  28.6 2.5 %collective-permute-done.5 = f32[16,128]{1,0:T(8,128)S(1)} collective-permute-done((f32[16,128]{1,0:T(8,128)S(1)}, f32[16,128]{1,0:T(8,128)S(1)}, u32[]{:S(2)}, u32[]{:S(2)}) %collective-permute-start.5) | collective-permute-done | bytes 8224 | tf_op jit(solution)/shard_map/ppermute | solution.py:55
  31.1 1.5 %collective-permute-start.6 = (f32[16,128]{1,0:T(8,128)S(1)}, f32[16,128]{1,0:T(8,128)S(1)}, u32[]{:S(2)}, u32[]{:S(2)}) collective-permute-start(f32[16,128]{1,0:T(8,128)S(1)} %add.32), channel_id=1, source_target_pairs={{0,2},{1,3},{2,0},{3,1},{4,6},{5,7},{6,4},{7,5},{8,10},{9,11},{10,... | collective-permute-start | bytes 24584 | tf_op jit(solution)/shard_map/ppermute | solution.py:55
  32.5 1.9 %collective-permute-done.6 = f32[16,128]{1,0:T(8,128)S(1)} collective-permute-done((f32[16,128]{1,0:T(8,128)S(1)}, f32[16,128]{1,0:T(8,128)S(1)}, u32[]{:S(2)}, u32[]{:S(2)}) %collective-permute-start.6) | collective-permute-done | bytes 8224 | tf_op jit(solution)/shard_map/ppermute | solution.py:55
  34.5 5.2 %collective-permute-start.7 = (f32[16,128]{1,0:T(8,128)S(1)}, f32[16,128]{1,0:T(8,128)S(1)}, u32[]{:S(2)}, u32[]{:S(2)}) collective-permute-start(f32[16,128]{1,0:T(8,128)S(1)} %add.33), channel_id=1, source_target_pairs={{0,4},{1,5},{2,6},{3,7},{4,0},{5,1},{6,2},{7,3},{8,12},{9,13},{10,... | collective-permute-start | bytes 24584 | tf_op jit(solution)/shard_map/ppermute | solution.py:55
  39.7 1.2 collective-permute-done.7
  40.9 0.7 fusion
  41.6 2.7 %shard_map.101 = (f32[1,83034]{1,0:T(1,128)}, f32[1,83034]{1,0:T(1,128)}, bf16[656,128]{1,0:T(8,128)(2,1)}) custom-call(s32[7]{0:T(128)} %order_ref.3, f32[16,128]{1,0:T(8,128)} %get-tuple-element.23.total_ref, f32[1,83034]{1,0:T(1,128)} %w_ref.3, f32[656,128]{1,0:T(8,128)} %get-tuple-element.14.raw_ref), custom_call_target="tpu_custom_call" | custom-call | tf_op jit(solution)/shard_map/pallas_call | solution.py:196
  44.3 0.0 all-gather.3.cloned.1.call-update
  44.3 0.1 fusion.1
  44.4 0.7 select_reduce_fusion.1
  45.1 0.5 add_divide_fusion
  45.7 60.6 %all-gather.3.cloned.1.call-done = bf16[20992,128]{1,0:T(8,128)(2,1)} async-done(((bf16[656,128]{1,0:T(8,128)(2,1)}), bf16[20992,128]{1,0:T(8,128)(2,1)}) %all-gather.3.cloned.1.call-update) | async-done | bytes 5373968 | tf_op jit(solution)/shard_map/all_gather | solution.py:203
  106.3 16.1 %shard_map.102 = bf16[1,2657088]{1,0:T(2,128)(2,1)} custom-call(bf16[32,656,128]{2,1,0:T(8,128)(2,1)} %bitcast.1), custom_call_target="tpu_custom_call" | custom-call | tf_op jit(solution)/shard_map/pallas_call | solution.py:170
  (6 shorter events, 0.0 us)
Async XLA Ops:
  7.2 99.1 %all-gather.3.cloned.1.call-start = ((), (), s32[]{:S(2)}) async-start(), calls=%async_computation | async-start | bytes 5541888 | tf_op jit(solution)/shard_map/all_gather | solution.py:203
  10.6 4.2 %collective-permute-start = (f32[16,128]{1,0:T(8,128)}, f32[16,128]{1,0:T(8,128)S(1)}, u32[]{:S(2)}, u32[]{:S(2)}) collective-permute-start(f32[16,128]{1,0:T(8,128)} %get-tuple-element.13), channel_id=1, source_target_pairs={{0,8},{8,0},{16,24},{24,16},{32,40},{40,32},{48,56},{56,48},{64,72... | collective-permute-start | bytes 24584 | tf_op jit(solution)/shard_map/ppermute | solution.py:55
  15.5 2.5 %collective-permute-start.1 = (f32[16,128]{1,0:T(8,128)S(1)}, f32[16,128]{1,0:T(8,128)S(1)}, u32[]{:S(2)}, u32[]{:S(2)}) collective-permute-start(f32[16,128]{1,0:T(8,128)S(1)} %add.27), channel_id=1, source_target_pairs={{0,16},{8,24},{16,0},{24,8},{32,48},{40,56},{48,32},{56,40},{64,80... | collective-permute-start | bytes 24584 | tf_op jit(solution)/shard_map/ppermute | solution.py:55
  18.0 4.0 %collective-permute-start.2 = (f32[16,128]{1,0:T(8,128)S(1)}, f32[16,128]{1,0:T(8,128)S(1)}, u32[]{:S(2)}, u32[]{:S(2)}) collective-permute-start(f32[16,128]{1,0:T(8,128)S(1)} %add.28), channel_id=1, source_target_pairs={{0,32},{8,40},{16,48},{24,56},{32,0},{40,8},{48,16},{56,24},{64,96... | collective-permute-start | bytes 24584 | tf_op jit(solution)/shard_map/ppermute | solution.py:55
  22.1 2.5 %collective-permute-start.3 = (f32[16,128]{1,0:T(8,128)S(1)}, f32[16,128]{1,0:T(8,128)S(1)}, u32[]{:S(2)}, u32[]{:S(2)}) collective-permute-start(f32[16,128]{1,0:T(8,128)S(1)} %add.29), channel_id=1, source_target_pairs={{0,64},{8,72},{16,80},{24,88},{32,96},{40,104},{48,112},{56,120},{... | collective-permute-start | bytes 24584 | tf_op jit(solution)/shard_map/ppermute | solution.py:55
  24.6 4.0 %collective-permute-start.4 = (f32[16,128]{1,0:T(8,128)S(1)}, f32[16,128]{1,0:T(8,128)S(1)}, u32[]{:S(2)}, u32[]{:S(2)}) collective-permute-start(f32[16,128]{1,0:T(8,128)S(1)} %add.30), channel_id=1, source_target_pairs={{0,128},{8,136},{16,144},{24,152},{32,160},{40,168},{48,176},{56,1... | collective-permute-start | bytes 24584 | tf_op jit(solution)/shard_map/ppermute | solution.py:55
  28.6 2.5 %collective-permute-start.5 = (f32[16,128]{1,0:T(8,128)S(1)}, f32[16,128]{1,0:T(8,128)S(1)}, u32[]{:S(2)}, u32[]{:S(2)}) collective-permute-start(f32[16,128]{1,0:T(8,128)S(1)} %add.31), channel_id=1, source_target_pairs={{0,1},{1,0},{2,3},{3,2},{4,5},{5,4},{6,7},{7,6},{8,9},{9,8},{10,11... | collective-permute-start | bytes 24584 | tf_op jit(solution)/shard_map/ppermute | solution.py:55
  31.1 3.4 %collective-permute-start.6 = (f32[16,128]{1,0:T(8,128)S(1)}, f32[16,128]{1,0:T(8,128)S(1)}, u32[]{:S(2)}, u32[]{:S(2)}) collective-permute-start(f32[16,128]{1,0:T(8,128)S(1)} %add.32), channel_id=1, source_target_pairs={{0,2},{1,3},{2,0},{3,1},{4,6},{5,7},{6,4},{7,5},{8,10},{9,11},{10,... | collective-permute-start | bytes 24584 | tf_op jit(solution)/shard_map/ppermute | solution.py:55
  34.5 6.4 %collective-permute-start.7 = (f32[16,128]{1,0:T(8,128)S(1)}, f32[16,128]{1,0:T(8,128)S(1)}, u32[]{:S(2)}, u32[]{:S(2)}) collective-permute-start(f32[16,128]{1,0:T(8,128)S(1)} %add.33), channel_id=1, source_target_pairs={{0,4},{1,5},{2,6},{3,7},{4,0},{5,1},{6,2},{7,3},{8,12},{9,13},{10,... | collective-permute-start | bytes 24584 | tf_op jit(solution)/shard_map/ppermute | solution.py:55
Sparse Core Ops, SparseCore 0:
  44.4 61.7 all-gather.2

commit v9 on v8

--- a/solution.py
+++ b/solution.py
@@ -65,10 +65,14 @@
     return block.reshape(1, -1)[:, :width]
 
 
+def position():
+    return lax.axis_index("chips") * lax.axis_size("core") + lax.axis_index("core")
+
+
 def slot_of(order_ref, width, parts, rows):
     lengths = [D * D // parts] * 4 + [EXPERTS * D // parts, D // parts, D // parts]
     places = (
-        lax.axis_index("dp") * width
+        position() * width
         + lax.broadcasted_iota(jnp.int32, (rows, 128), 0) * 128
         + lax.broadcasted_iota(jnp.int32, (rows, 128), 1)
     )
@@ -143,14 +147,16 @@
     tc_ref[...] = new_weights.astype(jnp.bfloat16)
 
 
-def assemble_kernel(width, whole_ref, out_ref):
-    count, rows, _ = whole_ref.shape
+def assemble_kernel(width, mine_ref, other_ref, out_ref):
+    half, rows, _ = mine_ref.shape
+    count = 2 * half
     total = count * width
+    core = lax.axis_index("core")
     lane = lax.broadcasted_iota(jnp.int32, (rows, 128), 1)
     for k in range(count):
         start, shift = divmod(k * width, 128)
         chunks = -(-(shift + width) // 128)
-        piece = whole_ref[k].astype(jnp.float32)
+        piece = jnp.where(core == k % 2, mine_ref[k // 2], other_ref[k // 2]).astype(jnp.float32)
         if shift:
             rolled = pltpu.roll(piece, shift, 1)
             piece = jnp.where(lane >= shift, rolled, pltpu.roll(rolled, 1, 0))
@@ -165,14 +171,14 @@
             out_ref[:, pl.ds((start + full) * 128, tail)] = piece[full : full + 1, :tail].astype(out_ref.dtype)
 
 
-def assemble(whole, width):
-    count = whole.shape[0]
+def assemble(mine, other, width):
+    count = 2 * mine.shape[0]
     return pl.pallas_call(
         functools.partial(assemble_kernel, width),
         out_shape=jax.ShapeDtypeStruct((1, count * width), jnp.bfloat16),
-        in_specs=[pl.BlockSpec(memory_space=pltpu.VMEM)],
+        in_specs=[pl.BlockSpec(memory_space=pltpu.VMEM)] * 2,
         out_specs=pl.BlockSpec(memory_space=pltpu.VMEM),
-    )(whole)
+    )(mine, other)
 
 
 def on_device(weights, moment_first, moment_second, gradients, tensor_order):
@@ -192,7 +198,7 @@
         in_specs=[scalar_block, row_block, row_block, row_block, row_block],
         out_specs=(row_block, row_block, whole_block((rows, 128)), whole_block((16, 128))),
     )(tensor_order, weights, moment_first, moment_second, gradients)
-    total = tree_sum(tree_sum(sums, "dp"), "mp")
+    total = tree_sum(tree_sum(tree_sum(sums, "core"), "chips"), "mp")
     scaled_update, new_weights, piece = pl.pallas_call(
         functools.partial(update_kernel, width, parts),
         grid=(1,),
@@ -200,8 +206,9 @@
         in_specs=[scalar_block, whole_block((16, 128)), row_block, whole_block((rows, 128))],
         out_specs=(row_block, row_block, whole_block((rows, 128))),
     )(tensor_order, total, weights, raw)
-    whole = lax.all_gather(piece, "dp", axis=0, tiled=False)
-    training_copy = assemble(whole, width)
+    mine = lax.all_gather(piece, "chips", axis=0, tiled=False)
+    other = lax.ppermute(mine, "core", [(0, 1), (1, 0)])
+    training_copy = assemble(mine, other, width)
     sums_by_slot = jnp.sum(total, axis=1)
     matches = tensor_order[:, None] == jnp.arange(SLOTS, dtype=jnp.int32)[None, :]
     wsq = jnp.sum(jnp.where(matches, sums_by_slot[:SLOTS, None], 0.0), axis=0)
@@ -211,10 +218,13 @@
 
 
 def solution(mesh):
+    rows, columns = mesh.devices.shape
+    fine = jax.sharding.Mesh(mesh.devices.reshape(rows // 2, 2, columns), ("chips", "core", "mp"))
+    shard = P("mp", ("chips", "core"))
     return jax.shard_map(
         on_device,
-        mesh=mesh,
-        in_specs=(P("mp", "dp"), P("mp", "dp"), P("mp", "dp"), P("mp", "dp"), P()),
-        out_specs=(P("mp", "dp"), P("mp", "dp"), P("mp", "dp"), P("mp", "dp"), P("mp", None), P()),
+        mesh=fine,
+        in_specs=(shard, shard, shard, shard, P()),
+        out_specs=(shard, shard, shard, shard, P("mp", None), P()),
         check_vma=False,
     )

time: 129 us -> 135 us (1.047)
  waiting for transfers between devices: 78.1 us -> 80.6 us
  local copies, waits for them, and re-layouts: 0.07 us -> 1.6 us
  starting transfers between devices: 12.1 us -> 13.6 us
    ppermute x0 -> x1, waiting for transfers between devices: none -> 3.5 us  [on_device(): other = lax.ppermute(mine, 'core', [(0, 1), (1, 0)])]
    unnamed x0 -> x2, local copies, waits for them, and re-layouts: none -> 1.53 us
    ppermute x0 -> x1, starting transfers between devices: none -> 1.46 us  [on_device(): other = lax.ppermute(mine, 'core', [(0, 1), (1, 0)])]
  transfers between devices with their start and end apart: 9 -> 10, of which waited for: 9 -> 10; matrix products, arithmetic and copies ran while one was open for 1% -> 1% of each run, Pallas kernels for 0% -> 0%
where the time goes in v9:
time: 135 us
  waiting for transfers between devices  80.6 us (60%)
  Pallas kernels  22.7 us (17%)
  between operations  14 us (10%)
  starting transfers between devices  13.6 us (10%)
  other arithmetic  2.7 us (2%)
  local copies, waits for them, and re-layouts  1.6 us (1%)
    all_gather x1, waiting for transfers between devices, on_device(): mine = lax.all_gather(piece, 'chips', axis=0, tiled=False)  59.6 us
    ppermute x8, waiting for transfers between devices, tree_sum(): x = x + lax.ppermute(x, axis, pairs)  17.5 us
    pallas_call x1, Pallas kernels, assemble(): pl.pallas_call(functools.partial(assemble_kernel, width), out_shape=jax.S...  16.6 us
    ppermute x8, starting transfers between devices, tree_sum(): x = x + lax.ppermute(x, axis, pairs)  12.1 us
    ppermute x1, waiting for transfers between devices, on_device(): other = lax.ppermute(mine, 'core', [(0, 1), (1, 0)])  3.5 us
    pallas_call x1, Pallas kernels, on_device(): pl.pallas_call(functools.partial(moments_kernel, width, parts), grid=(1,)...  3.38 us
  transfers between devices with their start and end apart: 10, of which 10 were waited for; matrix products, arithmetic and copies ran while one was open for 1% of the time, Pallas kernels for 0%

profile of v9, /device:TPU:1, one launch (start us, length us, event | category | flops | bytes accessed | tf_op | source)
XLA Modules:
  0.0 135.2 jit_solution(16977562212521884237)
XLA Ops:
  7.2 0.0 all-gather.3.cloned.1.call-start
  7.2 3.4 %shard_map.100 = (f32[1,83034]{1,0:T(1,128)}, f32[1,83034]{1,0:T(1,128)}, f32[656,128]{1,0:T(8,128)}, f32[16,128]{1,0:T(8,128)}) custom-call(s32[7]{0:T(128)} %order_ref.3, f32[1,83034]{1,0:T(1,128)} %w_ref.3, f32[1,83034]{1,0:T(1,128)} %m1_ref.1, f32[1,83034]{1,0:T(1,128)} %m2_ref.1, bf16[1,83034]{1,0:T(2,128)(2,1)} %g_ref.1), custom_call_target="tpu_custom_call" | custom-call | tf_op jit(solution)/shard_map/pallas_call | solution.py:194
  10.6 3.2 %collective-permute-start = (f32[16,128]{1,0:T(8,128)}, f32[16,128]{1,0:T(8,128)S(1)}, u32[]{:S(2)}, u32[]{:S(2)}) collective-permute-start(f32[16,128]{1,0:T(8,128)} %get-tuple-element.13), channel_id=1, source_target_pairs={{0,8},{8,0},{1,9},{9,1},{2,10},{10,2},{3,11},{11,3},{4,12},{12,4},... | collective-permute-start | bytes 24584 | tf_op jit(solution)/shard_map/ppermute | solution.py:55
  13.8 1.0 collective-permute-done
  14.8 0.7 add.27
  15.5 0.0 collective-permute-start.1
  15.5 2.5 %collective-permute-done.1 = f32[16,128]{1,0:T(8,128)S(1)} collective-permute-done((f32[16,128]{1,0:T(8,128)S(1)}, f32[16,128]{1,0:T(8,128)S(1)}, u32[]{:S(2)}, u32[]{:S(2)}) %collective-permute-start.1) | collective-permute-done | bytes 8224 | tf_op jit(solution)/shard_map/ppermute | solution.py:55
  18.0 1.0 collective-permute-start.2
  19.1 3.0 %collective-permute-done.2 = f32[16,128]{1,0:T(8,128)S(1)} collective-permute-done((f32[16,128]{1,0:T(8,128)S(1)}, f32[16,128]{1,0:T(8,128)S(1)}, u32[]{:S(2)}, u32[]{:S(2)}) %collective-permute-start.2) | collective-permute-done | bytes 8224 | tf_op jit(solution)/shard_map/ppermute | solution.py:55
  22.1 0.0 collective-permute-start.3
  22.1 2.5 %collective-permute-done.3 = f32[16,128]{1,0:T(8,128)S(1)} collective-permute-done((f32[16,128]{1,0:T(8,128)S(1)}, f32[16,128]{1,0:T(8,128)S(1)}, u32[]{:S(2)}, u32[]{:S(2)}) %collective-permute-start.3) | collective-permute-done | bytes 8224 | tf_op jit(solution)/shard_map/ppermute | solution.py:55
  24.6 1.2 collective-permute-start.4
  25.8 2.8 %collective-permute-done.4 = f32[16,128]{1,0:T(8,128)S(1)} collective-permute-done((f32[16,128]{1,0:T(8,128)S(1)}, f32[16,128]{1,0:T(8,128)S(1)}, u32[]{:S(2)}, u32[]{:S(2)}) %collective-permute-start.4) | collective-permute-done | bytes 8224 | tf_op jit(solution)/shard_map/ppermute | solution.py:55
  28.6 0.0 collective-permute-start.5
  28.6 2.5 %collective-permute-done.5 = f32[16,128]{1,0:T(8,128)S(1)} collective-permute-done((f32[16,128]{1,0:T(8,128)S(1)}, f32[16,128]{1,0:T(8,128)S(1)}, u32[]{:S(2)}, u32[]{:S(2)}) %collective-permute-start.5) | collective-permute-done | bytes 8224 | tf_op jit(solution)/shard_map/ppermute | solution.py:55
  31.1 1.5 %collective-permute-start.6 = (f32[16,128]{1,0:T(8,128)S(1)}, f32[16,128]{1,0:T(8,128)S(1)}, u32[]{:S(2)}, u32[]{:S(2)}) collective-permute-start(f32[16,128]{1,0:T(8,128)S(1)} %add.32), channel_id=1, source_target_pairs={{0,2},{1,3},{2,0},{3,1},{4,6},{5,7},{6,4},{7,5},{8,10},{9,11},{10,... | collective-permute-start | bytes 24584 | tf_op jit(solution)/shard_map/ppermute | solution.py:55
  32.5 1.9 %collective-permute-done.6 = f32[16,128]{1,0:T(8,128)S(1)} collective-permute-done((f32[16,128]{1,0:T(8,128)S(1)}, f32[16,128]{1,0:T(8,128)S(1)}, u32[]{:S(2)}, u32[]{:S(2)}) %collective-permute-start.6) | collective-permute-done | bytes 8224 | tf_op jit(solution)/shard_map/ppermute | solution.py:55
  34.5 5.2 %collective-permute-start.7 = (f32[16,128]{1,0:T(8,128)S(1)}, f32[16,128]{1,0:T(8,128)S(1)}, u32[]{:S(2)}, u32[]{:S(2)}) collective-permute-start(f32[16,128]{1,0:T(8,128)S(1)} %add.33), channel_id=1, source_target_pairs={{0,4},{1,5},{2,6},{3,7},{4,0},{5,1},{6,2},{7,3},{8,12},{9,13},{10,... | collective-permute-start | bytes 24584 | tf_op jit(solution)/shard_map/ppermute | solution.py:55
  39.7 1.2 collective-permute-done.7
  40.9 0.7 fusion
  41.6 2.7 %shard_map.101 = (f32[1,83034]{1,0:T(1,128)}, f32[1,83034]{1,0:T(1,128)}, bf16[656,128]{1,0:T(8,128)(2,1)}) custom-call(s32[7]{0:T(128)} %order_ref.3, f32[16,128]{1,0:T(8,128)} %get-tuple-element.23.total_ref, f32[1,83034]{1,0:T(1,128)} %w_ref.3, f32[656,128]{1,0:T(8,128)} %get-tuple-element.14.raw_ref), custom_call_target="tpu_custom_call" | custom-call | tf_op jit(solution)/shard_map/pallas_call | solution.py:202
  44.3 0.0 all-gather.3.cloned.1.call-update
  44.3 59.6 %all-gather.3.cloned.1.call-done = bf16[10496,128]{1,0:T(8,128)(2,1)} async-done(((bf16[656,128]{1,0:T(8,128)(2,1)}), bf16[10496,128]{1,0:T(8,128)(2,1)}) %all-gather.3.cloned.1.call-update) | async-done | bytes 2686992 | tf_op jit(solution)/shard_map/all_gather | solution.py:209
  103.9 1.5 %collective-permute-start.8 = (bf16[16,656,128]{2,1,0:T(8,128)(2,1)}, bf16[16,656,128]{2,1,0:T(8,128)(2,1)S(1)}, u32[]{:S(2)}, u32[]{:S(2)}) collective-permute-start(bf16[16,656,128]{2,1,0:T(8,128)(2,1)} %bitcast.1), channel_id=1, source_target_pairs={{0,8},{8,0},{1,9},{9,1},{2,10},{10,2},{3,11},{11,3},{4,12},{12,4},... | collective-permute-start | bytes 8060936 | tf_op jit(solution)/shard_map/ppermute | solution.py:210
  105.4 0.1 fusion.1
  105.4 0.7 select_reduce_fusion.1
  106.2 0.5 add_divide_fusion
  106.7 3.5 %collective-permute-done.8.other_ref = bf16[16,656,128]{2,1,0:T(8,128)(2,1)S(1)} collective-permute-done((bf16[16,656,128]{2,1,0:T(8,128)(2,1)}, bf16[16,656,128]{2,1,0:T(8,128)(2,1)S(1)}, u32[]{:S(2)}, u32[]{:S(2)}) %collective-permute-start.8) | collective-permute-done | bytes 2687008 | tf_op jit(solution)/shard_map/ppermute | solution.py:210
  110.2 0.0 copy-start
  110.2 1.5 %copy-done = bf16[16,656,128]{2,1,0:T(8,128)(2,1)} copy-done((bf16[16,656,128]{2,1,0:T(8,128)(2,1)}, bf16[16,656,128]{2,1,0:T(8,128)(2,1)S(1)}, u32[]{:S(2)}) %copy-start) | copy-done | bytes 2687000
  111.7 16.6 %shard_map.102 = bf16[1,2657088]{1,0:T(2,128)(2,1)} custom-call(bf16[16,656,128]{2,1,0:T(8,128)(2,1)} %bitcast.2, bf16[16,656,128]{2,1,0:T(8,128)(2,1)} %copy-done), custom_call_target="tpu_custom_call" | custom-call | tf_op jit(solution)/shard_map/pallas_call | solution.py:176
  (6 shorter events, 0.0 us)
Async XLA Ops:
  7.2 96.7 %all-gather.3.cloned.1.call-start = ((), (), s32[]{:S(2)}) async-start(), calls=%async_computation | async-start | bytes 2854912 | tf_op jit(solution)/shard_map/all_gather | solution.py:209
  10.6 4.2 %collective-permute-start = (f32[16,128]{1,0:T(8,128)}, f32[16,128]{1,0:T(8,128)S(1)}, u32[]{:S(2)}, u32[]{:S(2)}) collective-permute-start(f32[16,128]{1,0:T(8,128)} %get-tuple-element.13), channel_id=1, source_target_pairs={{0,8},{8,0},{1,9},{9,1},{2,10},{10,2},{3,11},{11,3},{4,12},{12,4},... | collective-permute-start | bytes 24584 | tf_op jit(solution)/shard_map/ppermute | solution.py:55
  15.5 2.5 %collective-permute-start.1 = (f32[16,128]{1,0:T(8,128)S(1)}, f32[16,128]{1,0:T(8,128)S(1)}, u32[]{:S(2)}, u32[]{:S(2)}) collective-permute-start(f32[16,128]{1,0:T(8,128)S(1)} %add.27), channel_id=1, source_target_pairs={{0,16},{16,0},{32,48},{48,32},{64,80},{80,64},{96,112},{112,96},{1... | collective-permute-start | bytes 24584 | tf_op jit(solution)/shard_map/ppermute | solution.py:55
  18.0 4.0 %collective-permute-start.2 = (f32[16,128]{1,0:T(8,128)S(1)}, f32[16,128]{1,0:T(8,128)S(1)}, u32[]{:S(2)}, u32[]{:S(2)}) collective-permute-start(f32[16,128]{1,0:T(8,128)S(1)} %add.28), channel_id=1, source_target_pairs={{0,32},{16,48},{32,0},{48,16},{64,96},{80,112},{96,64},{112,80},{1... | collective-permute-start | bytes 24584 | tf_op jit(solution)/shard_map/ppermute | solution.py:55
  22.1 2.5 %collective-permute-start.3 = (f32[16,128]{1,0:T(8,128)S(1)}, f32[16,128]{1,0:T(8,128)S(1)}, u32[]{:S(2)}, u32[]{:S(2)}) collective-permute-start(f32[16,128]{1,0:T(8,128)S(1)} %add.29), channel_id=1, source_target_pairs={{0,64},{16,80},{32,96},{48,112},{64,0},{80,16},{96,32},{112,48},{1... | collective-permute-start | bytes 24584 | tf_op jit(solution)/shard_map/ppermute | solution.py:55
  24.6 4.0 %collective-permute-start.4 = (f32[16,128]{1,0:T(8,128)S(1)}, f32[16,128]{1,0:T(8,128)S(1)}, u32[]{:S(2)}, u32[]{:S(2)}) collective-permute-start(f32[16,128]{1,0:T(8,128)S(1)} %add.30), channel_id=1, source_target_pairs={{0,128},{16,144},{32,160},{48,176},{64,192},{80,208},{96,224},{112... | collective-permute-start | bytes 24584 | tf_op jit(solution)/shard_map/ppermute | solution.py:55
  28.6 2.5 %collective-permute-start.5 = (f32[16,128]{1,0:T(8,128)S(1)}, f32[16,128]{1,0:T(8,128)S(1)}, u32[]{:S(2)}, u32[]{:S(2)}) collective-permute-start(f32[16,128]{1,0:T(8,128)S(1)} %add.31), channel_id=1, source_target_pairs={{0,1},{1,0},{2,3},{3,2},{4,5},{5,4},{6,7},{7,6},{8,9},{9,8},{10,11... | collective-permute-start | bytes 24584 | tf_op jit(solution)/shard_map/ppermute | solution.py:55
  31.1 3.4 %collective-permute-start.6 = (f32[16,128]{1,0:T(8,128)S(1)}, f32[16,128]{1,0:T(8,128)S(1)}, u32[]{:S(2)}, u32[]{:S(2)}) collective-permute-start(f32[16,128]{1,0:T(8,128)S(1)} %add.32), channel_id=1, source_target_pairs={{0,2},{1,3},{2,0},{3,1},{4,6},{5,7},{6,4},{7,5},{8,10},{9,11},{10,... | collective-permute-start | bytes 24584 | tf_op jit(solution)/shard_map/ppermute | solution.py:55
  34.5 6.4 %collective-permute-start.7 = (f32[16,128]{1,0:T(8,128)S(1)}, f32[16,128]{1,0:T(8,128)S(1)}, u32[]{:S(2)}, u32[]{:S(2)}) collective-permute-start(f32[16,128]{1,0:T(8,128)S(1)} %add.33), channel_id=1, source_target_pairs={{0,4},{1,5},{2,6},{3,7},{4,0},{5,1},{6,2},{7,3},{8,12},{9,13},{10,... | collective-permute-start | bytes 24584 | tf_op jit(solution)/shard_map/ppermute | solution.py:55
  103.9 6.3 %collective-permute-start.8 = (bf16[16,656,128]{2,1,0:T(8,128)(2,1)}, bf16[16,656,128]{2,1,0:T(8,128)(2,1)S(1)}, u32[]{:S(2)}, u32[]{:S(2)}) collective-permute-start(bf16[16,656,128]{2,1,0:T(8,128)(2,1)} %bitcast.1), channel_id=1, source_target_pairs={{0,8},{8,0},{1,9},{9,1},{2,10},{10,2},{3,11},{11,3},{4,12},{12,4},... | collective-permute-start | bytes 8060936 | tf_op jit(solution)/shard_map/ppermute | solution.py:210
  110.2 1.5 %copy-start = (bf16[16,656,128]{2,1,0:T(8,128)(2,1)}, bf16[16,656,128]{2,1,0:T(8,128)(2,1)S(1)}, u32[]{:S(2)}) copy-start(bf16[16,656,128]{2,1,0:T(8,128)(2,1)S(1)} %collective-permute-done.8.other_ref) | copy-start | bytes 8060932
Sparse Core Ops, SparseCore 0:
  44.4 59.4 all-gather.2

commit v10 on v8

--- a/solution.py
+++ b/solution.py
@@ -65,10 +65,15 @@
     return block.reshape(1, -1)[:, :width]
 
 
+def position():
+    index = lax.axis_index("y") * lax.axis_size("x") + lax.axis_index("x")
+    return index * lax.axis_size("core") + lax.axis_index("core")
+
+
 def slot_of(order_ref, width, parts, rows):
     lengths = [D * D // parts] * 4 + [EXPERTS * D // parts, D // parts, D // parts]
     places = (
-        lax.axis_index("dp") * width
+        position() * width
         + lax.broadcasted_iota(jnp.int32, (rows, 128), 0) * 128
         + lax.broadcasted_iota(jnp.int32, (rows, 128), 1)
     )
@@ -192,7 +197,9 @@
         in_specs=[scalar_block, row_block, row_block, row_block, row_block],
         out_specs=(row_block, row_block, whole_block((rows, 128)), whole_block((16, 128))),
     )(tensor_order, weights, moment_first, moment_second, gradients)
-    total = tree_sum(tree_sum(sums, "dp"), "mp")
+    total = sums
+    for axis in ("core", "x", "y", "mp"):
+        total = tree_sum(total, axis)
     scaled_update, new_weights, piece = pl.pallas_call(
         functools.partial(update_kernel, width, parts),
         grid=(1,),
@@ -200,7 +207,10 @@
         in_specs=[scalar_block, whole_block((16, 128)), row_block, whole_block((rows, 128))],
         out_specs=(row_block, row_block, whole_block((rows, 128))),
     )(tensor_order, total, weights, raw)
-    whole = lax.all_gather(piece, "dp", axis=0, tiled=False)
+    whole = piece
+    for axis in ("core", "x", "y"):
+        whole = lax.all_gather(whole, axis, axis=0, tiled=False)
+    whole = whole.reshape(-1, rows, 128)
     training_copy = assemble(whole, width)
     sums_by_slot = jnp.sum(total, axis=1)
     matches = tensor_order[:, None] == jnp.arange(SLOTS, dtype=jnp.int32)[None, :]
@@ -211,10 +221,16 @@
 
 
 def solution(mesh):
+    ys, xs = 4, 4
+    rows, columns = mesh.devices.shape
+    fine = jax.sharding.Mesh(
+        mesh.devices.reshape(ys, xs, rows // (ys * xs), columns), ("y", "x", "core", "mp")
+    )
+    shard = P("mp", ("y", "x", "core"))
     return jax.shard_map(
         on_device,
-        mesh=mesh,
-        in_specs=(P("mp", "dp"), P("mp", "dp"), P("mp", "dp"), P("mp", "dp"), P()),
-        out_specs=(P("mp", "dp"), P("mp", "dp"), P("mp", "dp"), P("mp", "dp"), P("mp", None), P()),
+        mesh=fine,
+        in_specs=(shard, shard, shard, shard, P()),
+        out_specs=(shard, shard, shard, shard, P("mp", None), P()),
         check_vma=False,
     )

time: 129 us -> 170 us (1.32)
  waiting for transfers between devices: 78.1 us -> 107 us
  blocking collectives: 0 us -> 12 us
    all_gather x1 -> x2, waiting for transfers between devices: 60.6 us -> 89.3 us  [on_device(): whole = lax.all_gather(whole, axis, axis=0, tiled=False)]
    all_gather x0 -> x1, blocking collectives: none -> 12 us  [on_device(): whole = lax.all_gather(whole, axis, axis=0, tiled=False)]
  transfers between devices with their start and end apart: 9 -> 10, of which waited for: 9 -> 10; matrix products, arithmetic and copies ran while one was open for 1% -> 1% of each run, Pallas kernels for 0% -> 0%
where the time goes in v10:
time: 170 us
  waiting for transfers between devices  107 us (63%)
  Pallas kernels  22.2 us (13%)
  between operations  14.1 us (8%)
  starting transfers between devices  12.4 us (7%)
  blocking collectives  12 us (7%)
  other arithmetic  2.69 us (2%)
    all_gather x2, waiting for transfers between devices, on_device(): whole = lax.all_gather(whole, axis, axis=0, tiled=False)  89.3 us
    ppermute x8, waiting for transfers between devices, tree_sum(): x = x + lax.ppermute(x, axis, pairs)  17.5 us
    pallas_call x1, Pallas kernels, assemble(): pl.pallas_call(functools.partial(assemble_kernel, width), out_shape=jax.S...  16.1 us
    ppermute x8, starting transfers between devices, tree_sum(): x = x + lax.ppermute(x, axis, pairs)  12.1 us
    all_gather x1, blocking collectives, on_device(): whole = lax.all_gather(whole, axis, axis=0, tiled=False)  12 us
  transfers between devices with their start and end apart: 10, of which 10 were waited for; matrix products, arithmetic and copies ran while one was open for 1% of the time, Pallas kernels for 0%

profile of v10, /device:TPU:1, one launch (start us, length us, event | category | flops | bytes accessed | tf_op | source)
XLA Modules:
  0.0 170.1 jit_solution(8101292889304205877)
XLA Ops:
  7.2 0.0 all-gather.6.cloned.1.call-start
  7.2 3.4 %shard_map.100 = (f32[1,83034]{1,0:T(1,128)}, f32[1,83034]{1,0:T(1,128)}, f32[656,128]{1,0:T(8,128)}, f32[16,128]{1,0:T(8,128)}) custom-call(s32[7]{0:T(128)} %order_ref.3, f32[1,83034]{1,0:T(1,128)} %w_ref.3, f32[1,83034]{1,0:T(1,128)} %m1_ref.1, f32[1,83034]{1,0:T(1,128)} %m2_ref.1, bf16[1,83034]{1,0:T(2,128)(2,1)} %g_ref.1), custom_call_target="tpu_custom_call" | custom-call | tf_op jit(solution)/shard_map/pallas_call | solution.py:193
  10.6 3.2 %collective-permute-start = (f32[16,128]{1,0:T(8,128)}, f32[16,128]{1,0:T(8,128)S(1)}, u32[]{:S(2)}, u32[]{:S(2)}) collective-permute-start(f32[16,128]{1,0:T(8,128)} %get-tuple-element.13), channel_id=1, source_target_pairs={{0,8},{8,0},{1,9},{9,1},{2,10},{10,2},{3,11},{11,3},{4,12},{12,4},... | collective-permute-start | bytes 24584 | tf_op jit(solution)/shard_map/ppermute | solution.py:55
  13.8 1.0 collective-permute-done
  14.8 0.7 add.27
  15.5 0.0 collective-permute-start.1
  15.5 2.5 %collective-permute-done.1 = f32[16,128]{1,0:T(8,128)S(1)} collective-permute-done((f32[16,128]{1,0:T(8,128)S(1)}, f32[16,128]{1,0:T(8,128)S(1)}, u32[]{:S(2)}, u32[]{:S(2)}) %collective-permute-start.1) | collective-permute-done | bytes 8224 | tf_op jit(solution)/shard_map/ppermute | solution.py:55
  18.0 1.0 collective-permute-start.2
  19.1 3.0 %collective-permute-done.2 = f32[16,128]{1,0:T(8,128)S(1)} collective-permute-done((f32[16,128]{1,0:T(8,128)S(1)}, f32[16,128]{1,0:T(8,128)S(1)}, u32[]{:S(2)}, u32[]{:S(2)}) %collective-permute-start.2) | collective-permute-done | bytes 8224 | tf_op jit(solution)/shard_map/ppermute | solution.py:55
  22.1 0.0 collective-permute-start.3
  22.1 2.5 %collective-permute-done.3 = f32[16,128]{1,0:T(8,128)S(1)} collective-permute-done((f32[16,128]{1,0:T(8,128)S(1)}, f32[16,128]{1,0:T(8,128)S(1)}, u32[]{:S(2)}, u32[]{:S(2)}) %collective-permute-start.3) | collective-permute-done | bytes 8224 | tf_op jit(solution)/shard_map/ppermute | solution.py:55
  24.6 1.2 collective-permute-start.4
  25.8 2.8 %collective-permute-done.4 = f32[16,128]{1,0:T(8,128)S(1)} collective-permute-done((f32[16,128]{1,0:T(8,128)S(1)}, f32[16,128]{1,0:T(8,128)S(1)}, u32[]{:S(2)}, u32[]{:S(2)}) %collective-permute-start.4) | collective-permute-done | bytes 8224 | tf_op jit(solution)/shard_map/ppermute | solution.py:55
  28.6 0.0 collective-permute-start.5
  28.6 2.5 %collective-permute-done.5 = f32[16,128]{1,0:T(8,128)S(1)} collective-permute-done((f32[16,128]{1,0:T(8,128)S(1)}, f32[16,128]{1,0:T(8,128)S(1)}, u32[]{:S(2)}, u32[]{:S(2)}) %collective-permute-start.5) | collective-permute-done | bytes 8224 | tf_op jit(solution)/shard_map/ppermute | solution.py:55
  31.1 1.5 collective-permute-start.6
  32.5 1.9 %collective-permute-done.6 = f32[16,128]{1,0:T(8,128)S(1)} collective-permute-done((f32[16,128]{1,0:T(8,128)S(1)}, f32[16,128]{1,0:T(8,128)S(1)}, u32[]{:S(2)}, u32[]{:S(2)}) %collective-permute-start.6) | collective-permute-done | bytes 8224 | tf_op jit(solution)/shard_map/ppermute | solution.py:55
  34.5 5.2 %collective-permute-start.7 = (f32[16,128]{1,0:T(8,128)S(1)}, f32[16,128]{1,0:T(8,128)S(1)}, u32[]{:S(2)}, u32[]{:S(2)}) collective-permute-start(f32[16,128]{1,0:T(8,128)S(1)} %add.33), channel_id=1, source_target_pairs={{0,4},{1,5},{2,6},{3,7},{4,0},{5,1},{6,2},{7,3},{8,12},{9,13},{10,... | collective-permute-start | bytes 24584 | tf_op jit(solution)/shard_map/ppermute | solution.py:55
  39.7 1.2 collective-permute-done.7
  40.9 0.7 fusion
  41.6 2.7 %shard_map.101 = (f32[1,83034]{1,0:T(1,128)}, f32[1,83034]{1,0:T(1,128)}, bf16[656,128]{1,0:T(8,128)(2,1)}) custom-call(s32[7]{0:T(128)} %order_ref.3, f32[16,128]{1,0:T(8,128)} %get-tuple-element.23.total_ref, f32[1,83034]{1,0:T(1,128)} %w_ref.3, f32[656,128]{1,0:T(8,128)} %get-tuple-element.14.raw_ref), custom_call_target="tpu_custom_call" | custom-call | tf_op jit(solution)/shard_map/pallas_call | solution.py:203
  44.3 12.0 %all-gather = bf16[1312,128]{1,0:T(8,128)(2,1)} all-gather(bf16[656,128]{1,0:T(8,128)(2,1)} %get-tuple-element.19), channel_id=2, replica_groups=mesh['y'=4,'x'=4,'core'=2,'mp'=8] {'core'}, dimensions={0}, use_global_device_ids=true | all-gather | bytes 503808 | tf_op jit(solution)/shard_map/all_gather | solution.py:212
  56.3 0.0 all-gather.6.cloned.1.call-update
  56.3 0.2 all-gather.8.cloned.1.call-start
  56.5 27.1 %all-gather.6.cloned.1.call-done = bf16[8,656,128]{2,1,0:T(8,128)(2,1)} async-done(((bf16[2,656,128]{2,1,0:T(8,128)(2,1)}), bf16[8,656,128]{2,1,0:T(8,128)(2,1)}) %all-gather.6.cloned.1.call-update) | async-done | bytes 1343504 | tf_op jit(solution)/shard_map/all_gather | solution.py:212
  83.6 0.0 all-gather.8.cloned.1.call-update
  83.7 0.1 fusion.1
  83.7 0.7 select_reduce_fusion.1
  84.5 0.5 add_divide_fusion
  85.0 62.2 %all-gather.8.cloned.1.call-done = bf16[16,2,656,128]{3,2,1,0:T(8,128)(2,1)} async-done(((bf16[4,2,656,128]{3,2,1,0:T(8,128)(2,1)}), bf16[16,2,656,128]{3,2,1,0:T(8,128)(2,1)}) %all-gather.8.cloned.1.call-update) | async-done | bytes 5373968 | tf_op jit(solution)/shard_map/all_gather | solution.py:212
  147.2 16.1 %shard_map.102 = bf16[1,2657088]{1,0:T(2,128)(2,1)} custom-call(bf16[32,656,128]{2,1,0:T(8,128)(2,1)} %bitcast.3), custom_call_target="tpu_custom_call" | custom-call | tf_op jit(solution)/shard_map/pallas_call | solution.py:175
  (6 shorter events, 0.0 us)
Async XLA Ops:
  7.2 76.5 %all-gather.6.cloned.1.call-start = ((), (), s32[]{:S(2)}) async-start(), calls=%async_computation | async-start | bytes 1679360 | tf_op jit(solution)/shard_map/all_gather | solution.py:212
  10.6 4.2 %collective-permute-start = (f32[16,128]{1,0:T(8,128)}, f32[16,128]{1,0:T(8,128)S(1)}, u32[]{:S(2)}, u32[]{:S(2)}) collective-permute-start(f32[16,128]{1,0:T(8,128)} %get-tuple-element.13), channel_id=1, source_target_pairs={{0,8},{8,0},{1,9},{9,1},{2,10},{10,2},{3,11},{11,3},{4,12},{12,4},... | collective-permute-start | bytes 24584 | tf_op jit(solution)/shard_map/ppermute | solution.py:55
  15.5 2.5 %collective-permute-start.1 = (f32[16,128]{1,0:T(8,128)S(1)}, f32[16,128]{1,0:T(8,128)S(1)}, u32[]{:S(2)}, u32[]{:S(2)}) collective-permute-start(f32[16,128]{1,0:T(8,128)S(1)} %add.27), channel_id=1, source_target_pairs={{0,16},{16,0},{32,48},{48,32},{1,17},{17,1},{33,49},{49,33},{2,18}... | collective-permute-start | bytes 24584 | tf_op jit(solution)/shard_map/ppermute | solution.py:55
  18.0 4.0 %collective-permute-start.2 = (f32[16,128]{1,0:T(8,128)S(1)}, f32[16,128]{1,0:T(8,128)S(1)}, u32[]{:S(2)}, u32[]{:S(2)}) collective-permute-start(f32[16,128]{1,0:T(8,128)S(1)} %add.28), channel_id=1, source_target_pairs={{0,32},{16,48},{32,0},{48,16},{1,33},{17,49},{33,1},{49,17},{2,34}... | collective-permute-start | bytes 24584 | tf_op jit(solution)/shard_map/ppermute | solution.py:55
  22.1 2.5 %collective-permute-start.3 = (f32[16,128]{1,0:T(8,128)S(1)}, f32[16,128]{1,0:T(8,128)S(1)}, u32[]{:S(2)}, u32[]{:S(2)}) collective-permute-start(f32[16,128]{1,0:T(8,128)S(1)} %add.29), channel_id=1, source_target_pairs={{0,64},{64,0},{128,192},{192,128},{1,65},{65,1},{129,193},{193,129... | collective-permute-start | bytes 24584 | tf_op jit(solution)/shard_map/ppermute | solution.py:55
  24.6 4.0 %collective-permute-start.4 = (f32[16,128]{1,0:T(8,128)S(1)}, f32[16,128]{1,0:T(8,128)S(1)}, u32[]{:S(2)}, u32[]{:S(2)}) collective-permute-start(f32[16,128]{1,0:T(8,128)S(1)} %add.30), channel_id=1, source_target_pairs={{0,128},{64,192},{128,0},{192,64},{1,129},{65,193},{129,1},{193,65... | collective-permute-start | bytes 24584 | tf_op jit(solution)/shard_map/ppermute | solution.py:55
  28.6 2.5 %collective-permute-start.5 = (f32[16,128]{1,0:T(8,128)S(1)}, f32[16,128]{1,0:T(8,128)S(1)}, u32[]{:S(2)}, u32[]{:S(2)}) collective-permute-start(f32[16,128]{1,0:T(8,128)S(1)} %add.31), channel_id=1, source_target_pairs={{0,1},{1,0},{2,3},{3,2},{4,5},{5,4},{6,7},{7,6},{8,9},{9,8},{10,11... | collective-permute-start | bytes 24584 | tf_op jit(solution)/shard_map/ppermute | solution.py:55
  31.1 3.4 %collective-permute-start.6 = (f32[16,128]{1,0:T(8,128)S(1)}, f32[16,128]{1,0:T(8,128)S(1)}, u32[]{:S(2)}, u32[]{:S(2)}) collective-permute-start(f32[16,128]{1,0:T(8,128)S(1)} %add.32), channel_id=1, source_target_pairs={{0,2},{1,3},{2,0},{3,1},{4,6},{5,7},{6,4},{7,5},{8,10},{9,11},{10,... | collective-permute-start | bytes 24584 | tf_op jit(solution)/shard_map/ppermute | solution.py:55
  34.5 6.4 %collective-permute-start.7 = (f32[16,128]{1,0:T(8,128)S(1)}, f32[16,128]{1,0:T(8,128)S(1)}, u32[]{:S(2)}, u32[]{:S(2)}) collective-permute-start(f32[16,128]{1,0:T(8,128)S(1)} %add.33), channel_id=1, source_target_pairs={{0,4},{1,5},{2,6},{3,7},{4,0},{5,1},{6,2},{7,3},{8,12},{9,13},{10,... | collective-permute-start | bytes 24584 | tf_op jit(solution)/shard_map/ppermute | solution.py:55
  56.3 90.9 %all-gather.8.cloned.1.call-start = ((), (), s32[]{:S(2)}) async-start(), calls=%async_computation.1 | async-start | bytes 6717440 | tf_op jit(solution)/shard_map/all_gather | solution.py:212
Sparse Core Ops, SparseCore 0:
  56.4 27.1 all-gather.5
  85.4 61.6 all-gather.7

commit v11 on v8

--- a/solution.py
+++ b/solution.py
@@ -143,10 +143,11 @@
     tc_ref[...] = new_weights.astype(jnp.bfloat16)
 
 
-def assemble_kernel(width, whole_ref, out_ref):
+def assemble_kernel(width, whole_ref, out_ref, stage_ref, sems):
     count, rows, _ = whole_ref.shape
     total = count * width
     lane = lax.broadcasted_iota(jnp.int32, (rows, 128), 1)
+    copies = []
     for k in range(count):
         start, shift = divmod(k * width, 128)
         chunks = -(-(shift + width) // 128)
@@ -155,14 +156,27 @@
             rolled = pltpu.roll(piece, shift, 1)
             piece = jnp.where(lane >= shift, rolled, pltpu.roll(rolled, 1, 0))
         if shift and k:
-            held = out_ref[:, pl.ds(start * 128, 128)].astype(jnp.float32)
+            held = stage_ref[:, pl.ds(start * 128, 128)].astype(jnp.float32)
             first = jnp.where(lane[:1] >= shift, piece[:1], held)
             piece = jnp.concatenate([first, piece[1:]], axis=0)
         full = min(chunks, total // 128 - start)
-        out_ref[:, pl.ds(start * 128, full * 128)] = piece[:full].reshape(1, full * 128).astype(out_ref.dtype)
+        stage_ref[:, pl.ds(start * 128, full * 128)] = piece[:full].reshape(1, full * 128).astype(stage_ref.dtype)
         tail = total - (start + full) * 128
         if full < chunks and tail:
-            out_ref[:, pl.ds((start + full) * 128, tail)] = piece[full : full + 1, :tail].astype(out_ref.dtype)
+            stage_ref[:, pl.ds((start + full) * 128, tail)] = piece[full : full + 1, :tail].astype(stage_ref.dtype)
+        if k + 1 < count:
+            end = ((k + 1) * width) // 128 * 128
+        else:
+            end = total
+        begin = 0 if k == 0 else copies_end
+        copy = pltpu.make_async_copy(
+            stage_ref.at[:, pl.ds(begin, end - begin)], out_ref.at[:, pl.ds(begin, end - begin)], sems.at[k]
+        )
+        copy.start()
+        copies.append(copy)
+        copies_end = end
+    for copy in copies:
+        copy.wait()
 
 
 def assemble(whole, width):
@@ -171,7 +185,8 @@
         functools.partial(assemble_kernel, width),
         out_shape=jax.ShapeDtypeStruct((1, count * width), jnp.bfloat16),
         in_specs=[pl.BlockSpec(memory_space=pltpu.VMEM)],
-        out_specs=pl.BlockSpec(memory_space=pltpu.VMEM),
+        out_specs=pl.BlockSpec(memory_space=pl.ANY),
+        scratch_shapes=[pltpu.VMEM((1, count * width), jnp.bfloat16), pltpu.SemaphoreType.DMA((count,))],
     )(whole)
 
 

time: 129 us -> 126 us (0.977)
  Pallas kernels: 22.2 us -> 19.1 us
    pallas_call x1, Pallas kernels: 16.1 us -> 13 us  [assemble(): pl.pallas_call(functools.partial(assemble_kernel, width), out_shape=jax.S...]
where the time goes in v11:
time: 126 us
  waiting for transfers between devices  78.1 us (62%)
  Pallas kernels  19.1 us (15%)
  between operations  14.1 us (11%)
  starting transfers between devices  12.1 us (10%)
  other arithmetic  2.69 us (2%)
    all_gather x1, waiting for transfers between devices, on_device(): whole = lax.all_gather(piece, 'dp', axis=0, tiled=False)  60.6 us
    ppermute x8, waiting for transfers between devices, tree_sum(): x = x + lax.ppermute(x, axis, pairs)  17.5 us
    pallas_call x1, Pallas kernels, assemble(): pl.pallas_call(functools.partial(assemble_kernel, width), out_shape=jax.S...  13 us
    ppermute x8, starting transfers between devices, tree_sum(): x = x + lax.ppermute(x, axis, pairs)  12.1 us
    pallas_call x1, Pallas kernels, on_device(): pl.pallas_call(functools.partial(moments_kernel, width, parts), grid=(1,)...  3.39 us
    pallas_call x1, Pallas kernels, on_device(): pl.pallas_call(functools.partial(update_kernel, width, parts), grid=(1,),...  2.68 us
  transfers between devices with their start and end apart: 9, of which 9 were waited for; matrix products, arithmetic and copies ran while one was open for 1% of the time, Pallas kernels for 0%

profile of v11, /device:TPU:1, one launch (start us, length us, event | category | flops | bytes accessed | tf_op | source)
XLA Modules:
  0.0 126.1 jit_solution(925787130044966300)
XLA Ops:
  7.2 0.0 all-gather.3.cloned.1.call-start
  7.2 3.4 %shard_map.100 = (f32[1,83034]{1,0:T(1,128)}, f32[1,83034]{1,0:T(1,128)}, f32[656,128]{1,0:T(8,128)}, f32[16,128]{1,0:T(8,128)}) custom-call(s32[7]{0:T(128)} %order_ref.3, f32[1,83034]{1,0:T(1,128)} %w_ref.3, f32[1,83034]{1,0:T(1,128)} %m1_ref.1, f32[1,83034]{1,0:T(1,128)} %m2_ref.1, bf16[1,83034]{1,0:T(2,128)(2,1)} %g_ref.1), custom_call_target="tpu_custom_call" | custom-call | tf_op jit(solution)/shard_map/pallas_call | solution.py:203
  10.6 3.2 %collective-permute-start = (f32[16,128]{1,0:T(8,128)}, f32[16,128]{1,0:T(8,128)S(1)}, u32[]{:S(2)}, u32[]{:S(2)}) collective-permute-start(f32[16,128]{1,0:T(8,128)} %get-tuple-element.13), channel_id=1, source_target_pairs={{0,8},{8,0},{16,24},{24,16},{32,40},{40,32},{48,56},{56,48},{64,72... | collective-permute-start | bytes 24584 | tf_op jit(solution)/shard_map/ppermute | solution.py:55
  13.8 1.0 collective-permute-done
  14.8 0.7 add.27
  15.5 0.0 collective-permute-start.1
  15.5 2.5 %collective-permute-done.1 = f32[16,128]{1,0:T(8,128)S(1)} collective-permute-done((f32[16,128]{1,0:T(8,128)S(1)}, f32[16,128]{1,0:T(8,128)S(1)}, u32[]{:S(2)}, u32[]{:S(2)}) %collective-permute-start.1) | collective-permute-done | bytes 8224 | tf_op jit(solution)/shard_map/ppermute | solution.py:55
  18.0 1.0 collective-permute-start.2
  19.1 3.0 %collective-permute-done.2 = f32[16,128]{1,0:T(8,128)S(1)} collective-permute-done((f32[16,128]{1,0:T(8,128)S(1)}, f32[16,128]{1,0:T(8,128)S(1)}, u32[]{:S(2)}, u32[]{:S(2)}) %collective-permute-start.2) | collective-permute-done | bytes 8224 | tf_op jit(solution)/shard_map/ppermute | solution.py:55
  22.1 0.0 collective-permute-start.3
  22.1 2.5 %collective-permute-done.3 = f32[16,128]{1,0:T(8,128)S(1)} collective-permute-done((f32[16,128]{1,0:T(8,128)S(1)}, f32[16,128]{1,0:T(8,128)S(1)}, u32[]{:S(2)}, u32[]{:S(2)}) %collective-permute-start.3) | collective-permute-done | bytes 8224 | tf_op jit(solution)/shard_map/ppermute | solution.py:55
  24.6 1.2 collective-permute-start.4
  25.8 2.8 %collective-permute-done.4 = f32[16,128]{1,0:T(8,128)S(1)} collective-permute-done((f32[16,128]{1,0:T(8,128)S(1)}, f32[16,128]{1,0:T(8,128)S(1)}, u32[]{:S(2)}, u32[]{:S(2)}) %collective-permute-start.4) | collective-permute-done | bytes 8224 | tf_op jit(solution)/shard_map/ppermute | solution.py:55
  28.6 0.0 collective-permute-start.5
  28.6 2.5 %collective-permute-done.5 = f32[16,128]{1,0:T(8,128)S(1)} collective-permute-done((f32[16,128]{1,0:T(8,128)S(1)}, f32[16,128]{1,0:T(8,128)S(1)}, u32[]{:S(2)}, u32[]{:S(2)}) %collective-permute-start.5) | collective-permute-done | bytes 8224 | tf_op jit(solution)/shard_map/ppermute | solution.py:55
  31.1 1.5 %collective-permute-start.6 = (f32[16,128]{1,0:T(8,128)S(1)}, f32[16,128]{1,0:T(8,128)S(1)}, u32[]{:S(2)}, u32[]{:S(2)}) collective-permute-start(f32[16,128]{1,0:T(8,128)S(1)} %add.32), channel_id=1, source_target_pairs={{0,2},{1,3},{2,0},{3,1},{4,6},{5,7},{6,4},{7,5},{8,10},{9,11},{10,... | collective-permute-start | bytes 24584 | tf_op jit(solution)/shard_map/ppermute | solution.py:55
  32.5 1.9 %collective-permute-done.6 = f32[16,128]{1,0:T(8,128)S(1)} collective-permute-done((f32[16,128]{1,0:T(8,128)S(1)}, f32[16,128]{1,0:T(8,128)S(1)}, u32[]{:S(2)}, u32[]{:S(2)}) %collective-permute-start.6) | collective-permute-done | bytes 8224 | tf_op jit(solution)/shard_map/ppermute | solution.py:55
  34.5 5.2 %collective-permute-start.7 = (f32[16,128]{1,0:T(8,128)S(1)}, f32[16,128]{1,0:T(8,128)S(1)}, u32[]{:S(2)}, u32[]{:S(2)}) collective-permute-start(f32[16,128]{1,0:T(8,128)S(1)} %add.33), channel_id=1, source_target_pairs={{0,4},{1,5},{2,6},{3,7},{4,0},{5,1},{6,2},{7,3},{8,12},{9,13},{10,... | collective-permute-start | bytes 24584 | tf_op jit(solution)/shard_map/ppermute | solution.py:55
  39.7 1.2 collective-permute-done.7
  40.9 0.7 fusion
  41.6 2.7 %shard_map.101 = (f32[1,83034]{1,0:T(1,128)}, f32[1,83034]{1,0:T(1,128)}, bf16[656,128]{1,0:T(8,128)(2,1)}) custom-call(s32[7]{0:T(128)} %order_ref.3, f32[16,128]{1,0:T(8,128)} %get-tuple-element.23.total_ref, f32[1,83034]{1,0:T(1,128)} %w_ref.3, f32[656,128]{1,0:T(8,128)} %get-tuple-element.14.raw_ref), custom_call_target="tpu_custom_call" | custom-call | tf_op jit(solution)/shard_map/pallas_call | solution.py:211
  44.3 0.0 all-gather.3.cloned.1.call-update
  44.3 0.1 fusion.1
  44.4 0.7 select_reduce_fusion.1
  45.1 0.5 add_divide_fusion
  45.7 60.6 %all-gather.3.cloned.1.call-done = bf16[20992,128]{1,0:T(8,128)(2,1)} async-done(((bf16[656,128]{1,0:T(8,128)(2,1)}), bf16[20992,128]{1,0:T(8,128)(2,1)}) %all-gather.3.cloned.1.call-update) | async-done | bytes 5373968 | tf_op jit(solution)/shard_map/all_gather | solution.py:218
  106.3 13.0 %shard_map.102 = bf16[1,2657088]{1,0:T(2,128)(2,1)} custom-call(bf16[32,656,128]{2,1,0:T(8,128)(2,1)} %bitcast.1), custom_call_target="tpu_custom_call" | custom-call | tf_op jit(solution)/shard_map/pallas_call | solution.py:184
  (6 shorter events, 0.0 us)
Async XLA Ops:
  7.2 99.1 %all-gather.3.cloned.1.call-start = ((), (), s32[]{:S(2)}) async-start(), calls=%async_computation | async-start | bytes 5541888 | tf_op jit(solution)/shard_map/all_gather | solution.py:218
  10.6 4.2 %collective-permute-start = (f32[16,128]{1,0:T(8,128)}, f32[16,128]{1,0:T(8,128)S(1)}, u32[]{:S(2)}, u32[]{:S(2)}) collective-permute-start(f32[16,128]{1,0:T(8,128)} %get-tuple-element.13), channel_id=1, source_target_pairs={{0,8},{8,0},{16,24},{24,16},{32,40},{40,32},{48,56},{56,48},{64,72... | collective-permute-start | bytes 24584 | tf_op jit(solution)/shard_map/ppermute | solution.py:55
  15.5 2.5 %collective-permute-start.1 = (f32[16,128]{1,0:T(8,128)S(1)}, f32[16,128]{1,0:T(8,128)S(1)}, u32[]{:S(2)}, u32[]{:S(2)}) collective-permute-start(f32[16,128]{1,0:T(8,128)S(1)} %add.27), channel_id=1, source_target_pairs={{0,16},{8,24},{16,0},{24,8},{32,48},{40,56},{48,32},{56,40},{64,80... | collective-permute-start | bytes 24584 | tf_op jit(solution)/shard_map/ppermute | solution.py:55
  18.0 4.0 %collective-permute-start.2 = (f32[16,128]{1,0:T(8,128)S(1)}, f32[16,128]{1,0:T(8,128)S(1)}, u32[]{:S(2)}, u32[]{:S(2)}) collective-permute-start(f32[16,128]{1,0:T(8,128)S(1)} %add.28), channel_id=1, source_target_pairs={{0,32},{8,40},{16,48},{24,56},{32,0},{40,8},{48,16},{56,24},{64,96... | collective-permute-start | bytes 24584 | tf_op jit(solution)/shard_map/ppermute | solution.py:55
  22.1 2.5 %collective-permute-start.3 = (f32[16,128]{1,0:T(8,128)S(1)}, f32[16,128]{1,0:T(8,128)S(1)}, u32[]{:S(2)}, u32[]{:S(2)}) collective-permute-start(f32[16,128]{1,0:T(8,128)S(1)} %add.29), channel_id=1, source_target_pairs={{0,64},{8,72},{16,80},{24,88},{32,96},{40,104},{48,112},{56,120},{... | collective-permute-start | bytes 24584 | tf_op jit(solution)/shard_map/ppermute | solution.py:55
  24.6 4.0 %collective-permute-start.4 = (f32[16,128]{1,0:T(8,128)S(1)}, f32[16,128]{1,0:T(8,128)S(1)}, u32[]{:S(2)}, u32[]{:S(2)}) collective-permute-start(f32[16,128]{1,0:T(8,128)S(1)} %add.30), channel_id=1, source_target_pairs={{0,128},{8,136},{16,144},{24,152},{32,160},{40,168},{48,176},{56,1... | collective-permute-start | bytes 24584 | tf_op jit(solution)/shard_map/ppermute | solution.py:55
  28.6 2.5 %collective-permute-start.5 = (f32[16,128]{1,0:T(8,128)S(1)}, f32[16,128]{1,0:T(8,128)S(1)}, u32[]{:S(2)}, u32[]{:S(2)}) collective-permute-start(f32[16,128]{1,0:T(8,128)S(1)} %add.31), channel_id=1, source_target_pairs={{0,1},{1,0},{2,3},{3,2},{4,5},{5,4},{6,7},{7,6},{8,9},{9,8},{10,11... | collective-permute-start | bytes 24584 | tf_op jit(solution)/shard_map/ppermute | solution.py:55
  31.1 3.4 %collective-permute-start.6 = (f32[16,128]{1,0:T(8,128)S(1)}, f32[16,128]{1,0:T(8,128)S(1)}, u32[]{:S(2)}, u32[]{:S(2)}) collective-permute-start(f32[16,128]{1,0:T(8,128)S(1)} %add.32), channel_id=1, source_target_pairs={{0,2},{1,3},{2,0},{3,1},{4,6},{5,7},{6,4},{7,5},{8,10},{9,11},{10,... | collective-permute-start | bytes 24584 | tf_op jit(solution)/shard_map/ppermute | solution.py:55
  34.5 6.4 %collective-permute-start.7 = (f32[16,128]{1,0:T(8,128)S(1)}, f32[16,128]{1,0:T(8,128)S(1)}, u32[]{:S(2)}, u32[]{:S(2)}) collective-permute-start(f32[16,128]{1,0:T(8,128)S(1)} %add.33), channel_id=1, source_target_pairs={{0,4},{1,5},{2,6},{3,7},{4,0},{5,1},{6,2},{7,3},{8,12},{9,13},{10,... | collective-permute-start | bytes 24584 | tf_op jit(solution)/shard_map/ppermute | solution.py:55
Sparse Core Ops, SparseCore 0:
  44.4 61.7 all-gather.2

commit v12 on v11

--- a/solution.py
+++ b/solution.py
@@ -143,15 +143,22 @@
     tc_ref[...] = new_weights.astype(jnp.bfloat16)
 
 
-def assemble_kernel(width, whole_ref, out_ref, stage_ref, sems):
+def assemble_kernel(width, whole_ref, out_ref, slots, stage_ref, fetch_sems, sems):
     count, rows, _ = whole_ref.shape
     total = count * width
     lane = lax.broadcasted_iota(jnp.int32, (rows, 128), 1)
+    fetches = [
+        pltpu.make_async_copy(whole_ref.at[k], slots.at[k % 2], fetch_sems.at[k % 2]) for k in range(count)
+    ]
+    fetches[0].start()
     copies = []
     for k in range(count):
         start, shift = divmod(k * width, 128)
         chunks = -(-(shift + width) // 128)
-        piece = whole_ref[k].astype(jnp.float32)
+        if k + 1 < count:
+            fetches[k + 1].start()
+        fetches[k].wait()
+        piece = slots[k % 2].astype(jnp.float32)
         if shift:
             rolled = pltpu.roll(piece, shift, 1)
             piece = jnp.where(lane >= shift, rolled, pltpu.roll(rolled, 1, 0))
@@ -184,9 +191,14 @@
     return pl.pallas_call(
         functools.partial(assemble_kernel, width),
         out_shape=jax.ShapeDtypeStruct((1, count * width), jnp.bfloat16),
-        in_specs=[pl.BlockSpec(memory_space=pltpu.VMEM)],
+        in_specs=[pl.BlockSpec(memory_space=pl.ANY)],
         out_specs=pl.BlockSpec(memory_space=pl.ANY),
-        scratch_shapes=[pltpu.VMEM((1, count * width), jnp.bfloat16), pltpu.SemaphoreType.DMA((count,))],
+        scratch_shapes=[
+            pltpu.VMEM((2,) + whole.shape[1:], whole.dtype),
+            pltpu.VMEM((1, count * width), jnp.bfloat16),
+            pltpu.SemaphoreType.DMA((2,)),
+            pltpu.SemaphoreType.DMA((count,)),
+        ],
     )(whole)
 
 

time: 126 us -> 131 us (1.040)
  Pallas kernels: 19.1 us -> 23.2 us
    pallas_call x1, Pallas kernels: 13 us -> 17.1 us  [assemble(): pl.pallas_call(functools.partial(assemble_kernel, width), out_shape=jax.S...]
where the time goes in v12:
time: 131 us; the launch traced here: 130 us
  waiting for transfers between devices  78.1 us (60%)
  Pallas kernels  23.2 us (18%)
  between operations  14.1 us (11%)
  starting transfers between devices  12.1 us (9%)
  other arithmetic  2.69 us (2%)
    all_gather x1, waiting for transfers between devices, on_device(): whole = lax.all_gather(piece, 'dp', axis=0, tiled=False)  60.6 us
    ppermute x8, waiting for transfers between devices, tree_sum(): x = x + lax.ppermute(x, axis, pairs)  17.5 us
    pallas_call x1, Pallas kernels, assemble(): pl.pallas_call(functools.partial(assemble_kernel, width), out_shape=jax.S...  17.1 us
    ppermute x8, starting transfers between devices, tree_sum(): x = x + lax.ppermute(x, axis, pairs)  12.1 us
    pallas_call x1, Pallas kernels, on_device(): pl.pallas_call(functools.partial(moments_kernel, width, parts), grid=(1,)...  3.39 us
    pallas_call x1, Pallas kernels, on_device(): pl.pallas_call(functools.partial(update_kernel, width, parts), grid=(1,),...  2.68 us
  transfers between devices with their start and end apart: 9, of which 9 were waited for; matrix products, arithmetic and copies ran while one was open for 1% of the time, Pallas kernels for 0%

profile of v12, /device:TPU:1, one launch (start us, length us, event | category | flops | bytes accessed | tf_op | source)
XLA Modules:
  0.0 130.2 jit_solution(17197166027770223390)
XLA Ops:
  7.2 0.0 all-gather.3.cloned.1.call-start
  7.2 3.4 %shard_map.100 = (f32[1,83034]{1,0:T(1,128)}, f32[1,83034]{1,0:T(1,128)}, f32[656,128]{1,0:T(8,128)}, f32[16,128]{1,0:T(8,128)}) custom-call(s32[7]{0:T(128)} %order_ref.3, f32[1,83034]{1,0:T(1,128)} %w_ref.3, f32[1,83034]{1,0:T(1,128)} %m1_ref.1, f32[1,83034]{1,0:T(1,128)} %m2_ref.1, bf16[1,83034]{1,0:T(2,128)(2,1)} %g_ref.1), custom_call_target="tpu_custom_call" | custom-call | tf_op jit(solution)/shard_map/pallas_call | solution.py:215
  10.6 3.2 %collective-permute-start = (f32[16,128]{1,0:T(8,128)}, f32[16,128]{1,0:T(8,128)S(1)}, u32[]{:S(2)}, u32[]{:S(2)}) collective-permute-start(f32[16,128]{1,0:T(8,128)} %get-tuple-element.13), channel_id=1, source_target_pairs={{0,8},{8,0},{16,24},{24,16},{32,40},{40,32},{48,56},{56,48},{64,72... | collective-permute-start | bytes 24584 | tf_op jit(solution)/shard_map/ppermute | solution.py:55
  13.8 1.0 collective-permute-done
  14.8 0.7 add.27
  15.5 0.0 collective-permute-start.1
  15.5 2.5 %collective-permute-done.1 = f32[16,128]{1,0:T(8,128)S(1)} collective-permute-done((f32[16,128]{1,0:T(8,128)S(1)}, f32[16,128]{1,0:T(8,128)S(1)}, u32[]{:S(2)}, u32[]{:S(2)}) %collective-permute-start.1) | collective-permute-done | bytes 8224 | tf_op jit(solution)/shard_map/ppermute | solution.py:55
  18.0 1.0 collective-permute-start.2
  19.1 3.0 %collective-permute-done.2 = f32[16,128]{1,0:T(8,128)S(1)} collective-permute-done((f32[16,128]{1,0:T(8,128)S(1)}, f32[16,128]{1,0:T(8,128)S(1)}, u32[]{:S(2)}, u32[]{:S(2)}) %collective-permute-start.2) | collective-permute-done | bytes 8224 | tf_op jit(solution)/shard_map/ppermute | solution.py:55
  22.1 0.0 collective-permute-start.3
  22.1 2.5 %collective-permute-done.3 = f32[16,128]{1,0:T(8,128)S(1)} collective-permute-done((f32[16,128]{1,0:T(8,128)S(1)}, f32[16,128]{1,0:T(8,128)S(1)}, u32[]{:S(2)}, u32[]{:S(2)}) %collective-permute-start.3) | collective-permute-done | bytes 8224 | tf_op jit(solution)/shard_map/ppermute | solution.py:55
  24.6 1.2 collective-permute-start.4
  25.8 2.8 %collective-permute-done.4 = f32[16,128]{1,0:T(8,128)S(1)} collective-permute-done((f32[16,128]{1,0:T(8,128)S(1)}, f32[16,128]{1,0:T(8,128)S(1)}, u32[]{:S(2)}, u32[]{:S(2)}) %collective-permute-start.4) | collective-permute-done | bytes 8224 | tf_op jit(solution)/shard_map/ppermute | solution.py:55
  28.6 0.0 collective-permute-start.5
  28.6 2.5 %collective-permute-done.5 = f32[16,128]{1,0:T(8,128)S(1)} collective-permute-done((f32[16,128]{1,0:T(8,128)S(1)}, f32[16,128]{1,0:T(8,128)S(1)}, u32[]{:S(2)}, u32[]{:S(2)}) %collective-permute-start.5) | collective-permute-done | bytes 8224 | tf_op jit(solution)/shard_map/ppermute | solution.py:55
  31.1 1.5 %collective-permute-start.6 = (f32[16,128]{1,0:T(8,128)S(1)}, f32[16,128]{1,0:T(8,128)S(1)}, u32[]{:S(2)}, u32[]{:S(2)}) collective-permute-start(f32[16,128]{1,0:T(8,128)S(1)} %add.32), channel_id=1, source_target_pairs={{0,2},{1,3},{2,0},{3,1},{4,6},{5,7},{6,4},{7,5},{8,10},{9,11},{10,... | collective-permute-start | bytes 24584 | tf_op jit(solution)/shard_map/ppermute | solution.py:55
  32.5 1.9 %collective-permute-done.6 = f32[16,128]{1,0:T(8,128)S(1)} collective-permute-done((f32[16,128]{1,0:T(8,128)S(1)}, f32[16,128]{1,0:T(8,128)S(1)}, u32[]{:S(2)}, u32[]{:S(2)}) %collective-permute-start.6) | collective-permute-done | bytes 8224 | tf_op jit(solution)/shard_map/ppermute | solution.py:55
  34.5 5.2 %collective-permute-start.7 = (f32[16,128]{1,0:T(8,128)S(1)}, f32[16,128]{1,0:T(8,128)S(1)}, u32[]{:S(2)}, u32[]{:S(2)}) collective-permute-start(f32[16,128]{1,0:T(8,128)S(1)} %add.33), channel_id=1, source_target_pairs={{0,4},{1,5},{2,6},{3,7},{4,0},{5,1},{6,2},{7,3},{8,12},{9,13},{10,... | collective-permute-start | bytes 24584 | tf_op jit(solution)/shard_map/ppermute | solution.py:55
  39.7 1.2 collective-permute-done.7
  40.9 0.7 fusion
  41.6 2.7 %shard_map.101 = (f32[1,83034]{1,0:T(1,128)}, f32[1,83034]{1,0:T(1,128)}, bf16[656,128]{1,0:T(8,128)(2,1)}) custom-call(s32[7]{0:T(128)} %order_ref.3, f32[16,128]{1,0:T(8,128)} %get-tuple-element.23.total_ref, f32[1,83034]{1,0:T(1,128)} %w_ref.3, f32[656,128]{1,0:T(8,128)} %get-tuple-element.14.raw_ref), custom_call_target="tpu_custom_call" | custom-call | tf_op jit(solution)/shard_map/pallas_call | solution.py:223
  44.3 0.0 all-gather.3.cloned.1.call-update
  44.3 0.1 fusion.1
  44.4 0.7 select_reduce_fusion.1
  45.1 0.5 add_divide_fusion
  45.7 60.6 %all-gather.3.cloned.1.call-done = bf16[20992,128]{1,0:T(8,128)(2,1)} async-done(((bf16[656,128]{1,0:T(8,128)(2,1)}), bf16[20992,128]{1,0:T(8,128)(2,1)}) %all-gather.3.cloned.1.call-update) | async-done | bytes 5373968 | tf_op jit(solution)/shard_map/all_gather | solution.py:230
  106.3 17.1 %shard_map.102 = bf16[1,2657088]{1,0:T(2,128)(2,1)} custom-call(bf16[32,656,128]{2,1,0:T(8,128)(2,1)} %bitcast.1), custom_call_target="tpu_custom_call" | custom-call | tf_op jit(solution)/shard_map/pallas_call | solution.py:191
  (6 shorter events, 0.0 us)
Async XLA Ops:
  7.2 99.1 %all-gather.3.cloned.1.call-start = ((), (), s32[]{:S(2)}) async-start(), calls=%async_computation | async-start | bytes 5541888 | tf_op jit(solution)/shard_map/all_gather | solution.py:230
  10.6 4.2 %collective-permute-start = (f32[16,128]{1,0:T(8,128)}, f32[16,128]{1,0:T(8,128)S(1)}, u32[]{:S(2)}, u32[]{:S(2)}) collective-permute-start(f32[16,128]{1,0:T(8,128)} %get-tuple-element.13), channel_id=1, source_target_pairs={{0,8},{8,0},{16,24},{24,16},{32,40},{40,32},{48,56},{56,48},{64,72... | collective-permute-start | bytes 24584 | tf_op jit(solution)/shard_map/ppermute | solution.py:55
  15.5 2.5 %collective-permute-start.1 = (f32[16,128]{1,0:T(8,128)S(1)}, f32[16,128]{1,0:T(8,128)S(1)}, u32[]{:S(2)}, u32[]{:S(2)}) collective-permute-start(f32[16,128]{1,0:T(8,128)S(1)} %add.27), channel_id=1, source_target_pairs={{0,16},{8,24},{16,0},{24,8},{32,48},{40,56},{48,32},{56,40},{64,80... | collective-permute-start | bytes 24584 | tf_op jit(solution)/shard_map/ppermute | solution.py:55
  18.0 4.0 %collective-permute-start.2 = (f32[16,128]{1,0:T(8,128)S(1)}, f32[16,128]{1,0:T(8,128)S(1)}, u32[]{:S(2)}, u32[]{:S(2)}) collective-permute-start(f32[16,128]{1,0:T(8,128)S(1)} %add.28), channel_id=1, source_target_pairs={{0,32},{8,40},{16,48},{24,56},{32,0},{40,8},{48,16},{56,24},{64,96... | collective-permute-start | bytes 24584 | tf_op jit(solution)/shard_map/ppermute | solution.py:55
  22.1 2.5 %collective-permute-start.3 = (f32[16,128]{1,0:T(8,128)S(1)}, f32[16,128]{1,0:T(8,128)S(1)}, u32[]{:S(2)}, u32[]{:S(2)}) collective-permute-start(f32[16,128]{1,0:T(8,128)S(1)} %add.29), channel_id=1, source_target_pairs={{0,64},{8,72},{16,80},{24,88},{32,96},{40,104},{48,112},{56,120},{... | collective-permute-start | bytes 24584 | tf_op jit(solution)/shard_map/ppermute | solution.py:55
  24.6 4.0 %collective-permute-start.4 = (f32[16,128]{1,0:T(8,128)S(1)}, f32[16,128]{1,0:T(8,128)S(1)}, u32[]{:S(2)}, u32[]{:S(2)}) collective-permute-start(f32[16,128]{1,0:T(8,128)S(1)} %add.30), channel_id=1, source_target_pairs={{0,128},{8,136},{16,144},{24,152},{32,160},{40,168},{48,176},{56,1... | collective-permute-start | bytes 24584 | tf_op jit(solution)/shard_map/ppermute | solution.py:55
  28.6 2.5 %collective-permute-start.5 = (f32[16,128]{1,0:T(8,128)S(1)}, f32[16,128]{1,0:T(8,128)S(1)}, u32[]{:S(2)}, u32[]{:S(2)}) collective-permute-start(f32[16,128]{1,0:T(8,128)S(1)} %add.31), channel_id=1, source_target_pairs={{0,1},{1,0},{2,3},{3,2},{4,5},{5,4},{6,7},{7,6},{8,9},{9,8},{10,11... | collective-permute-start | bytes 24584 | tf_op jit(solution)/shard_map/ppermute | solution.py:55
  31.1 3.4 %collective-permute-start.6 = (f32[16,128]{1,0:T(8,128)S(1)}, f32[16,128]{1,0:T(8,128)S(1)}, u32[]{:S(2)}, u32[]{:S(2)}) collective-permute-start(f32[16,128]{1,0:T(8,128)S(1)} %add.32), channel_id=1, source_target_pairs={{0,2},{1,3},{2,0},{3,1},{4,6},{5,7},{6,4},{7,5},{8,10},{9,11},{10,... | collective-permute-start | bytes 24584 | tf_op jit(solution)/shard_map/ppermute | solution.py:55
  34.5 6.4 %collective-permute-start.7 = (f32[16,128]{1,0:T(8,128)S(1)}, f32[16,128]{1,0:T(8,128)S(1)}, u32[]{:S(2)}, u32[]{:S(2)}) collective-permute-start(f32[16,128]{1,0:T(8,128)S(1)} %add.33), channel_id=1, source_target_pairs={{0,4},{1,5},{2,6},{3,7},{4,0},{5,1},{6,2},{7,3},{8,12},{9,13},{10,... | collective-permute-start | bytes 24584 | tf_op jit(solution)/shard_map/ppermute | solution.py:55
Sparse Core Ops, SparseCore 0:
  44.4 61.7 all-gather.2

commit v13 on v11

--- a/solution.py
+++ b/solution.py
@@ -47,11 +47,27 @@
     return jnp.sum(jnp.where(kind[None] == kinds, values[None], 0.0), axis=1)
 
 
+GRAY = (0, 1, 3, 2)
+
+
+def partner(index, step, size):
+    if size != 32:
+        return index ^ step
+    core, x, y = index % 2, (index // 2) % 4, index // 8
+    if step == 1:
+        core ^= 1
+    elif step < 8:
+        x = GRAY[GRAY[x] ^ (step // 2)]
+    else:
+        y = GRAY[GRAY[y] ^ (step // 8)]
+    return (y * 4 + x) * 2 + core
+
+
 def tree_sum(x, axis):
     size = lax.axis_size(axis)
     step = 1
     while step < size:
-        pairs = [(i, i ^ step) for i in range(size)]
+        pairs = [(i, partner(i, step, size) if axis == "dp" else i ^ step) for i in range(size)]
         x = x + lax.ppermute(x, axis, pairs)
         step *= 2
     return x

time: 126 us -> 125 us (level)
  no operation moved by 1% of the time
where the time goes in v13:
time: 125 us
  waiting for transfers between devices  77.4 us (62%)
  Pallas kernels  19.1 us (15%)
  between operations  14.1 us (11%)
  starting transfers between devices  11.8 us (9%)
  other arithmetic  2.69 us (2%)
    all_gather x1, waiting for transfers between devices, on_device(): whole = lax.all_gather(piece, 'dp', axis=0, tiled=False)  60.1 us
    ppermute x8, waiting for transfers between devices, tree_sum(): x = x + lax.ppermute(x, axis, pairs)  17.2 us
    pallas_call x1, Pallas kernels, assemble(): pl.pallas_call(functools.partial(assemble_kernel, width), out_shape=jax.S...  13 us
    ppermute x8, starting transfers between devices, tree_sum(): x = x + lax.ppermute(x, axis, pairs)  11.8 us
    pallas_call x1, Pallas kernels, on_device(): pl.pallas_call(functools.partial(moments_kernel, width, parts), grid=(1,)...  3.39 us
    pallas_call x1, Pallas kernels, on_device(): pl.pallas_call(functools.partial(update_kernel, width, parts), grid=(1,),...  2.68 us
  transfers between devices with their start and end apart: 9, of which 9 were waited for; matrix products, arithmetic and copies ran while one was open for 1% of the time, Pallas kernels for 0%

profile of v13, /device:TPU:1, one launch (start us, length us, event | category | flops | bytes accessed | tf_op | source)
XLA Modules:
  0.0 125.1 jit_solution(9431974509239709405)
XLA Ops:
  7.2 0.0 all-gather.3.cloned.1.call-start
  7.2 3.4 %shard_map.100 = (f32[1,83034]{1,0:T(1,128)}, f32[1,83034]{1,0:T(1,128)}, f32[656,128]{1,0:T(8,128)}, f32[16,128]{1,0:T(8,128)}) custom-call(s32[7]{0:T(128)} %order_ref.3, f32[1,83034]{1,0:T(1,128)} %w_ref.3, f32[1,83034]{1,0:T(1,128)} %m1_ref.1, f32[1,83034]{1,0:T(1,128)} %m2_ref.1, bf16[1,83034]{1,0:T(2,128)(2,1)} %g_ref.1), custom_call_target="tpu_custom_call" | custom-call | tf_op jit(solution)/shard_map/pallas_call | solution.py:219
  10.6 3.2 %collective-permute-start = (f32[16,128]{1,0:T(8,128)}, f32[16,128]{1,0:T(8,128)S(1)}, u32[]{:S(2)}, u32[]{:S(2)}) collective-permute-start(f32[16,128]{1,0:T(8,128)} %get-tuple-element.13), channel_id=1, source_target_pairs={{0,8},{8,0},{16,24},{24,16},{32,40},{40,32},{48,56},{56,48},{64,72... | collective-permute-start | bytes 24584 | tf_op jit(solution)/shard_map/ppermute | solution.py:71
  13.8 1.0 collective-permute-done
  14.8 0.7 add.27
  15.5 0.0 collective-permute-start.1
  15.5 2.5 %collective-permute-done.1 = f32[16,128]{1,0:T(8,128)S(1)} collective-permute-done((f32[16,128]{1,0:T(8,128)S(1)}, f32[16,128]{1,0:T(8,128)S(1)}, u32[]{:S(2)}, u32[]{:S(2)}) %collective-permute-start.1) | collective-permute-done | bytes 8224 | tf_op jit(solution)/shard_map/ppermute | solution.py:71
  18.0 0.8 collective-permute-start.2
  18.8 2.9 %collective-permute-done.2 = f32[16,128]{1,0:T(8,128)S(1)} collective-permute-done((f32[16,128]{1,0:T(8,128)S(1)}, f32[16,128]{1,0:T(8,128)S(1)}, u32[]{:S(2)}, u32[]{:S(2)}) %collective-permute-start.2) | collective-permute-done | bytes 8224 | tf_op jit(solution)/shard_map/ppermute | solution.py:71
  21.8 0.0 collective-permute-start.3
  21.8 2.5 %collective-permute-done.3 = f32[16,128]{1,0:T(8,128)S(1)} collective-permute-done((f32[16,128]{1,0:T(8,128)S(1)}, f32[16,128]{1,0:T(8,128)S(1)}, u32[]{:S(2)}, u32[]{:S(2)}) %collective-permute-start.3) | collective-permute-done | bytes 8224 | tf_op jit(solution)/shard_map/ppermute | solution.py:71
  24.3 1.0 collective-permute-start.4
  25.3 2.7 %collective-permute-done.4 = f32[16,128]{1,0:T(8,128)S(1)} collective-permute-done((f32[16,128]{1,0:T(8,128)S(1)}, f32[16,128]{1,0:T(8,128)S(1)}, u32[]{:S(2)}, u32[]{:S(2)}) %collective-permute-start.4) | collective-permute-done | bytes 8224 | tf_op jit(solution)/shard_map/ppermute | solution.py:71
  28.0 0.0 collective-permute-start.5
  28.0 2.5 %collective-permute-done.5 = f32[16,128]{1,0:T(8,128)S(1)} collective-permute-done((f32[16,128]{1,0:T(8,128)S(1)}, f32[16,128]{1,0:T(8,128)S(1)}, u32[]{:S(2)}, u32[]{:S(2)}) %collective-permute-start.5) | collective-permute-done | bytes 8224 | tf_op jit(solution)/shard_map/ppermute | solution.py:71
  30.5 1.5 %collective-permute-start.6 = (f32[16,128]{1,0:T(8,128)S(1)}, f32[16,128]{1,0:T(8,128)S(1)}, u32[]{:S(2)}, u32[]{:S(2)}) collective-permute-start(f32[16,128]{1,0:T(8,128)S(1)} %add.32), channel_id=1, source_target_pairs={{0,2},{1,3},{2,0},{3,1},{4,6},{5,7},{6,4},{7,5},{8,10},{9,11},{10,... | collective-permute-start | bytes 24584 | tf_op jit(solution)/shard_map/ppermute | solution.py:71
  32.0 1.9 %collective-permute-done.6 = f32[16,128]{1,0:T(8,128)S(1)} collective-permute-done((f32[16,128]{1,0:T(8,128)S(1)}, f32[16,128]{1,0:T(8,128)S(1)}, u32[]{:S(2)}, u32[]{:S(2)}) %collective-permute-start.6) | collective-permute-done | bytes 8224 | tf_op jit(solution)/shard_map/ppermute | solution.py:71
  33.9 5.3 %collective-permute-start.7 = (f32[16,128]{1,0:T(8,128)S(1)}, f32[16,128]{1,0:T(8,128)S(1)}, u32[]{:S(2)}, u32[]{:S(2)}) collective-permute-start(f32[16,128]{1,0:T(8,128)S(1)} %add.33), channel_id=1, source_target_pairs={{0,4},{1,5},{2,6},{3,7},{4,0},{5,1},{6,2},{7,3},{8,12},{9,13},{10,... | collective-permute-start | bytes 24584 | tf_op jit(solution)/shard_map/ppermute | solution.py:71
  39.2 1.2 collective-permute-done.7
  40.3 0.7 fusion
  41.0 2.7 %shard_map.101 = (f32[1,83034]{1,0:T(1,128)}, f32[1,83034]{1,0:T(1,128)}, bf16[656,128]{1,0:T(8,128)(2,1)}) custom-call(s32[7]{0:T(128)} %order_ref.3, f32[16,128]{1,0:T(8,128)} %get-tuple-element.23.total_ref, f32[1,83034]{1,0:T(1,128)} %w_ref.3, f32[656,128]{1,0:T(8,128)} %get-tuple-element.14.raw_ref), custom_call_target="tpu_custom_call" | custom-call | tf_op jit(solution)/shard_map/pallas_call | solution.py:227
  43.7 0.0 all-gather.3.cloned.1.call-update
  43.7 0.1 fusion.1
  43.8 0.7 select_reduce_fusion.1
  44.6 0.5 add_divide_fusion
  45.1 60.1 %all-gather.3.cloned.1.call-done = bf16[20992,128]{1,0:T(8,128)(2,1)} async-done(((bf16[656,128]{1,0:T(8,128)(2,1)}), bf16[20992,128]{1,0:T(8,128)(2,1)}) %all-gather.3.cloned.1.call-update) | async-done | bytes 5373968 | tf_op jit(solution)/shard_map/all_gather | solution.py:234
  105.2 13.0 %shard_map.102 = bf16[1,2657088]{1,0:T(2,128)(2,1)} custom-call(bf16[32,656,128]{2,1,0:T(8,128)(2,1)} %bitcast.1), custom_call_target="tpu_custom_call" | custom-call | tf_op jit(solution)/shard_map/pallas_call | solution.py:200
  (6 shorter events, 0.0 us)
Async XLA Ops:
  7.2 98.1 %all-gather.3.cloned.1.call-start = ((), (), s32[]{:S(2)}) async-start(), calls=%async_computation | async-start | bytes 5541888 | tf_op jit(solution)/shard_map/all_gather | solution.py:234
  10.6 4.2 %collective-permute-start = (f32[16,128]{1,0:T(8,128)}, f32[16,128]{1,0:T(8,128)S(1)}, u32[]{:S(2)}, u32[]{:S(2)}) collective-permute-start(f32[16,128]{1,0:T(8,128)} %get-tuple-element.13), channel_id=1, source_target_pairs={{0,8},{8,0},{16,24},{24,16},{32,40},{40,32},{48,56},{56,48},{64,72... | collective-permute-start | bytes 24584 | tf_op jit(solution)/shard_map/ppermute | solution.py:71
  15.5 2.5 %collective-permute-start.1 = (f32[16,128]{1,0:T(8,128)S(1)}, f32[16,128]{1,0:T(8,128)S(1)}, u32[]{:S(2)}, u32[]{:S(2)}) collective-permute-start(f32[16,128]{1,0:T(8,128)S(1)} %add.27), channel_id=1, source_target_pairs={{0,16},{8,24},{16,0},{24,8},{32,48},{40,56},{48,32},{56,40},{64,80... | collective-permute-start | bytes 24584 | tf_op jit(solution)/shard_map/ppermute | solution.py:71
  18.0 3.7 %collective-permute-start.2 = (f32[16,128]{1,0:T(8,128)S(1)}, f32[16,128]{1,0:T(8,128)S(1)}, u32[]{:S(2)}, u32[]{:S(2)}) collective-permute-start(f32[16,128]{1,0:T(8,128)S(1)} %add.28), channel_id=1, source_target_pairs={{0,48},{8,56},{16,32},{24,40},{32,16},{40,24},{48,0},{56,8},{64,11... | collective-permute-start | bytes 24584 | tf_op jit(solution)/shard_map/ppermute | solution.py:71
  21.8 2.5 %collective-permute-start.3 = (f32[16,128]{1,0:T(8,128)S(1)}, f32[16,128]{1,0:T(8,128)S(1)}, u32[]{:S(2)}, u32[]{:S(2)}) collective-permute-start(f32[16,128]{1,0:T(8,128)S(1)} %add.29), channel_id=1, source_target_pairs={{0,64},{8,72},{16,80},{24,88},{32,96},{40,104},{48,112},{56,120},{... | collective-permute-start | bytes 24584 | tf_op jit(solution)/shard_map/ppermute | solution.py:71
  24.3 3.7 %collective-permute-start.4 = (f32[16,128]{1,0:T(8,128)S(1)}, f32[16,128]{1,0:T(8,128)S(1)}, u32[]{:S(2)}, u32[]{:S(2)}) collective-permute-start(f32[16,128]{1,0:T(8,128)S(1)} %add.30), channel_id=1, source_target_pairs={{0,192},{8,200},{16,208},{24,216},{32,224},{40,232},{48,240},{56,2... | collective-permute-start | bytes 24584 | tf_op jit(solution)/shard_map/ppermute | solution.py:71
  28.0 2.5 %collective-permute-start.5 = (f32[16,128]{1,0:T(8,128)S(1)}, f32[16,128]{1,0:T(8,128)S(1)}, u32[]{:S(2)}, u32[]{:S(2)}) collective-permute-start(f32[16,128]{1,0:T(8,128)S(1)} %add.31), channel_id=1, source_target_pairs={{0,1},{1,0},{2,3},{3,2},{4,5},{5,4},{6,7},{7,6},{8,9},{9,8},{10,11... | collective-permute-start | bytes 24584 | tf_op jit(solution)/shard_map/ppermute | solution.py:71
  30.5 3.4 %collective-permute-start.6 = (f32[16,128]{1,0:T(8,128)S(1)}, f32[16,128]{1,0:T(8,128)S(1)}, u32[]{:S(2)}, u32[]{:S(2)}) collective-permute-start(f32[16,128]{1,0:T(8,128)S(1)} %add.32), channel_id=1, source_target_pairs={{0,2},{1,3},{2,0},{3,1},{4,6},{5,7},{6,4},{7,5},{8,10},{9,11},{10,... | collective-permute-start | bytes 24584 | tf_op jit(solution)/shard_map/ppermute | solution.py:71
  33.9 6.4 %collective-permute-start.7 = (f32[16,128]{1,0:T(8,128)S(1)}, f32[16,128]{1,0:T(8,128)S(1)}, u32[]{:S(2)}, u32[]{:S(2)}) collective-permute-start(f32[16,128]{1,0:T(8,128)S(1)} %add.33), channel_id=1, source_target_pairs={{0,4},{1,5},{2,6},{3,7},{4,0},{5,1},{6,2},{7,3},{8,12},{9,13},{10,... | collective-permute-start | bytes 24584 | tf_op jit(solution)/shard_map/ppermute | solution.py:71
Sparse Core Ops, SparseCore 0:
  43.9 61.3 all-gather.2

commit v14 on v13

--- a/solution.py
+++ b/solution.py
@@ -48,6 +48,7 @@
 
 
 GRAY = (0, 1, 3, 2)
+RING8 = (0, 1, 2, 3, 6, 7, 4, 5)
 
 
 def partner(index, step, size):
@@ -67,7 +68,12 @@
     size = lax.axis_size(axis)
     step = 1
     while step < size:
-        pairs = [(i, partner(i, step, size) if axis == "dp" else i ^ step) for i in range(size)]
+        if axis == "dp":
+            pairs = [(i, partner(i, step, size)) for i in range(size)]
+        elif size == 8:
+            pairs = [(i, RING8.index(RING8[i] ^ step)) for i in range(size)]
+        else:
+            pairs = [(i, i ^ step) for i in range(size)]
         x = x + lax.ppermute(x, axis, pairs)
         step *= 2
     return x

time: 125 us -> 124 us (level)
  no operation moved by 1% of the time
where the time goes in v14:
time: 124 us; the launch traced here: 123 us
  waiting for transfers between devices  76.5 us (62%)
  Pallas kernels  19.1 us (15%)
  between operations  14.1 us (11%)
  starting transfers between devices  10.9 us (9%)
  other arithmetic  2.69 us (2%)
    all_gather x1, waiting for transfers between devices, on_device(): whole = lax.all_gather(piece, 'dp', axis=0, tiled=False)  59.4 us
    ppermute x8, waiting for transfers between devices, tree_sum(): x = x + lax.ppermute(x, axis, pairs)  17.1 us
    pallas_call x1, Pallas kernels, assemble(): pl.pallas_call(functools.partial(assemble_kernel, width), out_shape=jax.S...  13 us
    ppermute x8, starting transfers between devices, tree_sum(): x = x + lax.ppermute(x, axis, pairs)  10.9 us
    pallas_call x1, Pallas kernels, on_device(): pl.pallas_call(functools.partial(moments_kernel, width, parts), grid=(1,)...  3.39 us
    pallas_call x1, Pallas kernels, on_device(): pl.pallas_call(functools.partial(update_kernel, width, parts), grid=(1,),...  2.68 us
  transfers between devices with their start and end apart: 9, of which 9 were waited for; matrix products, arithmetic and copies ran while one was open for 1% of the time, Pallas kernels for 0%

profile of v14, /device:TPU:1, one launch (start us, length us, event | category | flops | bytes accessed | tf_op | source)
XLA Modules:
  0.0 123.3 jit_solution(5011756872604027867)
XLA Ops:
  7.2 0.0 all-gather.3.cloned.1.call-start
  7.2 3.4 %shard_map.100 = (f32[1,83034]{1,0:T(1,128)}, f32[1,83034]{1,0:T(1,128)}, f32[656,128]{1,0:T(8,128)}, f32[16,128]{1,0:T(8,128)}) custom-call(s32[7]{0:T(128)} %order_ref.3, f32[1,83034]{1,0:T(1,128)} %w_ref.3, f32[1,83034]{1,0:T(1,128)} %m1_ref.1, f32[1,83034]{1,0:T(1,128)} %m2_ref.1, bf16[1,83034]{1,0:T(2,128)(2,1)} %g_ref.1), custom_call_target="tpu_custom_call" | custom-call | tf_op jit(solution)/shard_map/pallas_call | solution.py:225
  10.6 3.2 %collective-permute-start = (f32[16,128]{1,0:T(8,128)}, f32[16,128]{1,0:T(8,128)S(1)}, u32[]{:S(2)}, u32[]{:S(2)}) collective-permute-start(f32[16,128]{1,0:T(8,128)} %get-tuple-element.13), channel_id=1, source_target_pairs={{0,8},{8,0},{16,24},{24,16},{32,40},{40,32},{48,56},{56,48},{64,72... | collective-permute-start | bytes 24584 | tf_op jit(solution)/shard_map/ppermute | solution.py:77
  13.8 1.0 collective-permute-done
  14.8 0.7 add.27
  15.5 0.0 collective-permute-start.1
  15.5 2.5 %collective-permute-done.1 = f32[16,128]{1,0:T(8,128)S(1)} collective-permute-done((f32[16,128]{1,0:T(8,128)S(1)}, f32[16,128]{1,0:T(8,128)S(1)}, u32[]{:S(2)}, u32[]{:S(2)}) %collective-permute-start.1) | collective-permute-done | bytes 8224 | tf_op jit(solution)/shard_map/ppermute | solution.py:77
  18.0 0.8 collective-permute-start.2
  18.8 2.9 %collective-permute-done.2 = f32[16,128]{1,0:T(8,128)S(1)} collective-permute-done((f32[16,128]{1,0:T(8,128)S(1)}, f32[16,128]{1,0:T(8,128)S(1)}, u32[]{:S(2)}, u32[]{:S(2)}) %collective-permute-start.2) | collective-permute-done | bytes 8224 | tf_op jit(solution)/shard_map/ppermute | solution.py:77
  21.8 0.0 collective-permute-start.3
  21.8 2.5 %collective-permute-done.3 = f32[16,128]{1,0:T(8,128)S(1)} collective-permute-done((f32[16,128]{1,0:T(8,128)S(1)}, f32[16,128]{1,0:T(8,128)S(1)}, u32[]{:S(2)}, u32[]{:S(2)}) %collective-permute-start.3) | collective-permute-done | bytes 8224 | tf_op jit(solution)/shard_map/ppermute | solution.py:77
  24.3 1.0 collective-permute-start.4
  25.3 2.7 %collective-permute-done.4 = f32[16,128]{1,0:T(8,128)S(1)} collective-permute-done((f32[16,128]{1,0:T(8,128)S(1)}, f32[16,128]{1,0:T(8,128)S(1)}, u32[]{:S(2)}, u32[]{:S(2)}) %collective-permute-start.4) | collective-permute-done | bytes 8224 | tf_op jit(solution)/shard_map/ppermute | solution.py:77
  28.0 0.0 collective-permute-start.5
  28.0 2.5 %collective-permute-done.5 = f32[16,128]{1,0:T(8,128)S(1)} collective-permute-done((f32[16,128]{1,0:T(8,128)S(1)}, f32[16,128]{1,0:T(8,128)S(1)}, u32[]{:S(2)}, u32[]{:S(2)}) %collective-permute-start.5) | collective-permute-done | bytes 8224 | tf_op jit(solution)/shard_map/ppermute | solution.py:77
  30.5 1.5 %collective-permute-start.6 = (f32[16,128]{1,0:T(8,128)S(1)}, f32[16,128]{1,0:T(8,128)S(1)}, u32[]{:S(2)}, u32[]{:S(2)}) collective-permute-start(f32[16,128]{1,0:T(8,128)S(1)} %add.32), channel_id=1, source_target_pairs={{0,2},{1,3},{2,0},{3,1},{4,6},{5,7},{6,4},{7,5},{8,10},{9,11},{10,... | collective-permute-start | bytes 24584 | tf_op jit(solution)/shard_map/ppermute | solution.py:77
  32.0 1.9 %collective-permute-done.6 = f32[16,128]{1,0:T(8,128)S(1)} collective-permute-done((f32[16,128]{1,0:T(8,128)S(1)}, f32[16,128]{1,0:T(8,128)S(1)}, u32[]{:S(2)}, u32[]{:S(2)}) %collective-permute-start.6) | collective-permute-done | bytes 8224 | tf_op jit(solution)/shard_map/ppermute | solution.py:77
  33.9 4.4 %collective-permute-start.7 = (f32[16,128]{1,0:T(8,128)S(1)}, f32[16,128]{1,0:T(8,128)S(1)}, u32[]{:S(2)}, u32[]{:S(2)}) collective-permute-start(f32[16,128]{1,0:T(8,128)S(1)} %add.33), channel_id=1, source_target_pairs={{0,6},{1,7},{2,4},{3,5},{4,2},{5,3},{6,0},{7,1},{8,14},{9,15},{10,... | collective-permute-start | bytes 24584 | tf_op jit(solution)/shard_map/ppermute | solution.py:77
  38.3 1.0 collective-permute-done.7
  39.3 0.7 fusion
  40.0 2.7 %shard_map.101 = (f32[1,83034]{1,0:T(1,128)}, f32[1,83034]{1,0:T(1,128)}, bf16[656,128]{1,0:T(8,128)(2,1)}) custom-call(s32[7]{0:T(128)} %order_ref.3, f32[16,128]{1,0:T(8,128)} %get-tuple-element.23.total_ref, f32[1,83034]{1,0:T(1,128)} %w_ref.3, f32[656,128]{1,0:T(8,128)} %get-tuple-element.14.raw_ref), custom_call_target="tpu_custom_call" | custom-call | tf_op jit(solution)/shard_map/pallas_call | solution.py:233
  42.7 0.0 all-gather.3.cloned.1.call-update
  42.7 0.1 fusion.1
  42.8 0.7 select_reduce_fusion.1
  43.5 0.5 add_divide_fusion
  44.1 59.4 %all-gather.3.cloned.1.call-done = bf16[20992,128]{1,0:T(8,128)(2,1)} async-done(((bf16[656,128]{1,0:T(8,128)(2,1)}), bf16[20992,128]{1,0:T(8,128)(2,1)}) %all-gather.3.cloned.1.call-update) | async-done | bytes 5373968 | tf_op jit(solution)/shard_map/all_gather | solution.py:240
  103.5 13.0 %shard_map.102 = bf16[1,2657088]{1,0:T(2,128)(2,1)} custom-call(bf16[32,656,128]{2,1,0:T(8,128)(2,1)} %bitcast.1), custom_call_target="tpu_custom_call" | custom-call | tf_op jit(solution)/shard_map/pallas_call | solution.py:206
  (6 shorter events, 0.0 us)
Async XLA Ops:
  7.2 96.3 %all-gather.3.cloned.1.call-start = ((), (), s32[]{:S(2)}) async-start(), calls=%async_computation | async-start | bytes 5541888 | tf_op jit(solution)/shard_map/all_gather | solution.py:240
  10.6 4.2 %collective-permute-start = (f32[16,128]{1,0:T(8,128)}, f32[16,128]{1,0:T(8,128)S(1)}, u32[]{:S(2)}, u32[]{:S(2)}) collective-permute-start(f32[16,128]{1,0:T(8,128)} %get-tuple-element.13), channel_id=1, source_target_pairs={{0,8},{8,0},{16,24},{24,16},{32,40},{40,32},{48,56},{56,48},{64,72... | collective-permute-start | bytes 24584 | tf_op jit(solution)/shard_map/ppermute | solution.py:77
  15.5 2.5 %collective-permute-start.1 = (f32[16,128]{1,0:T(8,128)S(1)}, f32[16,128]{1,0:T(8,128)S(1)}, u32[]{:S(2)}, u32[]{:S(2)}) collective-permute-start(f32[16,128]{1,0:T(8,128)S(1)} %add.27), channel_id=1, source_target_pairs={{0,16},{8,24},{16,0},{24,8},{32,48},{40,56},{48,32},{56,40},{64,80... | collective-permute-start | bytes 24584 | tf_op jit(solution)/shard_map/ppermute | solution.py:77
  18.0 3.7 %collective-permute-start.2 = (f32[16,128]{1,0:T(8,128)S(1)}, f32[16,128]{1,0:T(8,128)S(1)}, u32[]{:S(2)}, u32[]{:S(2)}) collective-permute-start(f32[16,128]{1,0:T(8,128)S(1)} %add.28), channel_id=1, source_target_pairs={{0,48},{8,56},{16,32},{24,40},{32,16},{40,24},{48,0},{56,8},{64,11... | collective-permute-start | bytes 24584 | tf_op jit(solution)/shard_map/ppermute | solution.py:77
  21.8 2.5 %collective-permute-start.3 = (f32[16,128]{1,0:T(8,128)S(1)}, f32[16,128]{1,0:T(8,128)S(1)}, u32[]{:S(2)}, u32[]{:S(2)}) collective-permute-start(f32[16,128]{1,0:T(8,128)S(1)} %add.29), channel_id=1, source_target_pairs={{0,64},{8,72},{16,80},{24,88},{32,96},{40,104},{48,112},{56,120},{... | collective-permute-start | bytes 24584 | tf_op jit(solution)/shard_map/ppermute | solution.py:77
  24.3 3.7 %collective-permute-start.4 = (f32[16,128]{1,0:T(8,128)S(1)}, f32[16,128]{1,0:T(8,128)S(1)}, u32[]{:S(2)}, u32[]{:S(2)}) collective-permute-start(f32[16,128]{1,0:T(8,128)S(1)} %add.30), channel_id=1, source_target_pairs={{0,192},{8,200},{16,208},{24,216},{32,224},{40,232},{48,240},{56,2... | collective-permute-start | bytes 24584 | tf_op jit(solution)/shard_map/ppermute | solution.py:77
  28.0 2.5 %collective-permute-start.5 = (f32[16,128]{1,0:T(8,128)S(1)}, f32[16,128]{1,0:T(8,128)S(1)}, u32[]{:S(2)}, u32[]{:S(2)}) collective-permute-start(f32[16,128]{1,0:T(8,128)S(1)} %add.31), channel_id=1, source_target_pairs={{0,1},{1,0},{2,3},{3,2},{4,5},{5,4},{6,7},{7,6},{8,9},{9,8},{10,11... | collective-permute-start | bytes 24584 | tf_op jit(solution)/shard_map/ppermute | solution.py:77
  30.5 3.4 %collective-permute-start.6 = (f32[16,128]{1,0:T(8,128)S(1)}, f32[16,128]{1,0:T(8,128)S(1)}, u32[]{:S(2)}, u32[]{:S(2)}) collective-permute-start(f32[16,128]{1,0:T(8,128)S(1)} %add.32), channel_id=1, source_target_pairs={{0,2},{1,3},{2,0},{3,1},{4,6},{5,7},{6,4},{7,5},{8,10},{9,11},{10,... | collective-permute-start | bytes 24584 | tf_op jit(solution)/shard_map/ppermute | solution.py:77
  33.9 5.4 %collective-permute-start.7 = (f32[16,128]{1,0:T(8,128)S(1)}, f32[16,128]{1,0:T(8,128)S(1)}, u32[]{:S(2)}, u32[]{:S(2)}) collective-permute-start(f32[16,128]{1,0:T(8,128)S(1)} %add.33), channel_id=1, source_target_pairs={{0,6},{1,7},{2,4},{3,5},{4,2},{5,3},{6,0},{7,1},{8,14},{9,15},{10,... | collective-permute-start | bytes 24584 | tf_op jit(solution)/shard_map/ppermute | solution.py:77
Sparse Core Ops, SparseCore 0:
  42.8 60.5 all-gather.2

commit v15 on v14

--- a/solution.py
+++ b/solution.py
@@ -64,7 +64,7 @@
     return (y * 4 + x) * 2 + core
 
 
-def tree_sum(x, axis):
+def tree_sum(x, axis, keep_last=False):
     size = lax.axis_size(axis)
     step = 1
     while step < size:
@@ -74,7 +74,10 @@
             pairs = [(i, RING8.index(RING8[i] ^ step)) for i in range(size)]
         else:
             pairs = [(i, i ^ step) for i in range(size)]
-        x = x + lax.ppermute(x, axis, pairs)
+        received = lax.ppermute(x, axis, pairs)
+        if keep_last and step * 2 >= size:
+            return x, received
+        x = x + received
         step *= 2
     return x
 
@@ -150,10 +153,10 @@
         sums_ref[pl.ds(8 + number, 1), :] = jnp.sum(jnp.where(mask, usq, 0.0), axis=0, keepdims=True)
 
 
-def update_kernel(width, parts, order_ref, total_ref, w_ref, raw_ref, su_ref, nw_ref, tc_ref):
+def update_kernel(width, parts, order_ref, held_ref, received_ref, w_ref, raw_ref, su_ref, nw_ref, tc_ref):
     rows = raw_ref.shape[0]
     slot = slot_of(order_ref, width, parts, rows)
-    sums = jnp.sum(total_ref[...], axis=1, keepdims=True)
+    sums = jnp.sum(held_ref[...] + received_ref[...], axis=1, keepdims=True)
     trust = jnp.sqrt(sums[:8]) / (jnp.sqrt(sums[8:]) + 1e-06)
     factor = jnp.zeros((rows, 128), jnp.float32)
     for number in range(SLOTS):
@@ -229,17 +232,17 @@
         in_specs=[scalar_block, row_block, row_block, row_block, row_block],
         out_specs=(row_block, row_block, whole_block((rows, 128)), whole_block((16, 128))),
     )(tensor_order, weights, moment_first, moment_second, gradients)
-    total = tree_sum(tree_sum(sums, "dp"), "mp")
+    held, received = tree_sum(tree_sum(sums, "dp"), "mp", keep_last=True)
     scaled_update, new_weights, piece = pl.pallas_call(
         functools.partial(update_kernel, width, parts),
         grid=(1,),
         out_shape=(row, row, jax.ShapeDtypeStruct((rows, 128), jnp.bfloat16)),
-        in_specs=[scalar_block, whole_block((16, 128)), row_block, whole_block((rows, 128))],
+        in_specs=[scalar_block, whole_block((16, 128)), whole_block((16, 128)), row_block, whole_block((rows, 128))],
         out_specs=(row_block, row_block, whole_block((rows, 128))),
-    )(tensor_order, total, weights, raw)
+    )(tensor_order, held, received, weights, raw)
     whole = lax.all_gather(piece, "dp", axis=0, tiled=False)
     training_copy = assemble(whole, width)
-    sums_by_slot = jnp.sum(total, axis=1)
+    sums_by_slot = jnp.sum(held + received, axis=1)
     matches = tensor_order[:, None] == jnp.arange(SLOTS, dtype=jnp.int32)[None, :]
     wsq = jnp.sum(jnp.where(matches, sums_by_slot[:SLOTS, None], 0.0), axis=0)
     usq = jnp.sum(jnp.where(matches, sums_by_slot[8 : 8 + SLOTS, None], 0.0), axis=0)

time: 124 us -> 124 us (level)
  transfers between devices with their start and end apart: 9 -> 9, of which waited for: 9 -> 9; matrix products, arithmetic and copies ran while one was open for 1% -> 2% of each run, Pallas kernels for 0% -> 0%
where the time goes in v15:
time: 124 us; the launch traced here: 123 us
  waiting for transfers between devices  75.7 us (61%)
  Pallas kernels  19.1 us (15%)
  between operations  14.1 us (11%)
  starting transfers between devices  10.9 us (9%)
  other arithmetic  2.82 us (2%)
    all_gather x1, waiting for transfers between devices, on_device(): whole = lax.all_gather(piece, 'dp', axis=0, tiled=False)  58.6 us
    ppermute x8, waiting for transfers between devices, tree_sum(): received = lax.ppermute(x, axis, pairs)  17.1 us
    pallas_call x1, Pallas kernels, assemble(): pl.pallas_call(functools.partial(assemble_kernel, width), out_shape=jax.S...  13 us
    ppermute x8, starting transfers between devices, tree_sum(): received = lax.ppermute(x, axis, pairs)  10.9 us
    pallas_call x1, Pallas kernels, on_device(): pl.pallas_call(functools.partial(moments_kernel, width, parts), grid=(1,)...  3.39 us
    pallas_call x1, Pallas kernels, on_device(): pl.pallas_call(functools.partial(update_kernel, width, parts), grid=(1,),...  2.69 us
  transfers between devices with their start and end apart: 9, of which 9 were waited for; matrix products, arithmetic and copies ran while one was open for 2% of the time, Pallas kernels for 0%

profile of v15, /device:TPU:1, one launch (start us, length us, event | category | flops | bytes accessed | tf_op | source)
XLA Modules:
  0.0 123.2 jit_solution(13632156200432778003)
XLA Ops:
  7.2 0.0 all-gather.3.cloned.1.call-start
  7.2 3.4 %shard_map.100 = (f32[1,83034]{1,0:T(1,128)}, f32[1,83034]{1,0:T(1,128)}, f32[656,128]{1,0:T(8,128)}, f32[16,128]{1,0:T(8,128)}) custom-call(s32[7]{0:T(128)} %order_ref.3, f32[1,83034]{1,0:T(1,128)} %w_ref.3, f32[1,83034]{1,0:T(1,128)} %m1_ref.1, f32[1,83034]{1,0:T(1,128)} %m2_ref.1, bf16[1,83034]{1,0:T(2,128)(2,1)} %g_ref.1), custom_call_target="tpu_custom_call" | custom-call | tf_op jit(solution)/shard_map/pallas_call | solution.py:228
  10.6 3.2 %collective-permute-start = (f32[16,128]{1,0:T(8,128)}, f32[16,128]{1,0:T(8,128)S(1)}, u32[]{:S(2)}, u32[]{:S(2)}) collective-permute-start(f32[16,128]{1,0:T(8,128)} %get-tuple-element.13), channel_id=1, source_target_pairs={{0,8},{8,0},{16,24},{24,16},{32,40},{40,32},{48,56},{56,48},{64,72... | collective-permute-start | bytes 24584 | tf_op jit(solution)/shard_map/ppermute | solution.py:77
  13.8 1.0 collective-permute-done
  14.8 0.7 add.27
  15.5 0.0 collective-permute-start.1
  15.5 2.5 %collective-permute-done.1 = f32[16,128]{1,0:T(8,128)S(1)} collective-permute-done((f32[16,128]{1,0:T(8,128)S(1)}, f32[16,128]{1,0:T(8,128)S(1)}, u32[]{:S(2)}, u32[]{:S(2)}) %collective-permute-start.1) | collective-permute-done | bytes 8224 | tf_op jit(solution)/shard_map/ppermute | solution.py:77
  18.0 0.8 collective-permute-start.2
  18.8 2.9 %collective-permute-done.2 = f32[16,128]{1,0:T(8,128)S(1)} collective-permute-done((f32[16,128]{1,0:T(8,128)S(1)}, f32[16,128]{1,0:T(8,128)S(1)}, u32[]{:S(2)}, u32[]{:S(2)}) %collective-permute-start.2) | collective-permute-done | bytes 8224 | tf_op jit(solution)/shard_map/ppermute | solution.py:77
  21.8 0.0 collective-permute-start.3
  21.8 2.5 %collective-permute-done.3 = f32[16,128]{1,0:T(8,128)S(1)} collective-permute-done((f32[16,128]{1,0:T(8,128)S(1)}, f32[16,128]{1,0:T(8,128)S(1)}, u32[]{:S(2)}, u32[]{:S(2)}) %collective-permute-start.3) | collective-permute-done | bytes 8224 | tf_op jit(solution)/shard_map/ppermute | solution.py:77
  24.3 1.0 collective-permute-start.4
  25.3 2.7 %collective-permute-done.4 = f32[16,128]{1,0:T(8,128)S(1)} collective-permute-done((f32[16,128]{1,0:T(8,128)S(1)}, f32[16,128]{1,0:T(8,128)S(1)}, u32[]{:S(2)}, u32[]{:S(2)}) %collective-permute-start.4) | collective-permute-done | bytes 8224 | tf_op jit(solution)/shard_map/ppermute | solution.py:77
  28.0 0.0 collective-permute-start.5
  28.0 2.5 %collective-permute-done.5 = f32[16,128]{1,0:T(8,128)S(1)} collective-permute-done((f32[16,128]{1,0:T(8,128)S(1)}, f32[16,128]{1,0:T(8,128)S(1)}, u32[]{:S(2)}, u32[]{:S(2)}) %collective-permute-start.5) | collective-permute-done | bytes 8224 | tf_op jit(solution)/shard_map/ppermute | solution.py:77
  30.5 1.5 %collective-permute-start.6 = (f32[16,128]{1,0:T(8,128)S(1)}, f32[16,128]{1,0:T(8,128)S(1)}, u32[]{:S(2)}, u32[]{:S(2)}) collective-permute-start(f32[16,128]{1,0:T(8,128)S(1)} %add.32), channel_id=1, source_target_pairs={{0,2},{1,3},{2,0},{3,1},{4,6},{5,7},{6,4},{7,5},{8,10},{9,11},{10,... | collective-permute-start | bytes 24584 | tf_op jit(solution)/shard_map/ppermute | solution.py:77
  32.0 1.9 %collective-permute-done.6 = f32[16,128]{1,0:T(8,128)S(1)} collective-permute-done((f32[16,128]{1,0:T(8,128)S(1)}, f32[16,128]{1,0:T(8,128)S(1)}, u32[]{:S(2)}, u32[]{:S(2)}) %collective-permute-start.6) | collective-permute-done | bytes 8224 | tf_op jit(solution)/shard_map/ppermute | solution.py:77
  33.9 0.0 copy-start
  33.9 4.4 %collective-permute-start.7 = (f32[16,128]{1,0:T(8,128)S(1)}, f32[16,128]{1,0:T(8,128)S(1)}, u32[]{:S(2)}, u32[]{:S(2)}) collective-permute-start(f32[16,128]{1,0:T(8,128)S(1)} %add.33.held_ref), channel_id=1, source_target_pairs={{0,6},{1,7},{2,4},{3,5},{4,2},{5,3},{6,0},{7,1},{8,14},{9,15},{10,... | collective-permute-start | bytes 24584 | tf_op jit(solution)/shard_map/ppermute | solution.py:77
  38.3 1.0 collective-permute-done.7.received_ref
  39.3 0.0 copy-start.1
  39.3 0.0 copy-done
  39.3 0.6 copy-done.1
  39.9 2.7 %shard_map.101 = (f32[1,83034]{1,0:T(1,128)}, f32[1,83034]{1,0:T(1,128)}, bf16[656,128]{1,0:T(8,128)(2,1)}) custom-call(s32[7]{0:T(128)} %order_ref.3, f32[16,128]{1,0:T(8,128)} %copy-done, f32[16,128]{1,0:T(8,128)} %copy-done.1, f32[1,83034]{1,0:T(1,128)} %w_ref.3, f32[656,128]{1,0:T(8,128)} %get-tuple-element.14.raw_ref), custom_call_target="tpu_custom_call" | custom-call | tf_op jit(solution)/shard_map/pallas_call | solution.py:236
  42.6 0.0 all-gather.3.cloned.1.call-update
  42.6 0.8 add_reduce_fusion
  43.4 0.1 fusion
  43.5 0.7 select_reduce_fusion.1
  44.3 0.5 add_divide_fusion
  44.8 58.6 %all-gather.3.cloned.1.call-done = bf16[20992,128]{1,0:T(8,128)(2,1)} async-done(((bf16[656,128]{1,0:T(8,128)(2,1)}), bf16[20992,128]{1,0:T(8,128)(2,1)}) %all-gather.3.cloned.1.call-update) | async-done | bytes 5373968 | tf_op jit(solution)/shard_map/all_gather | solution.py:243
  103.4 13.0 %shard_map.102 = bf16[1,2657088]{1,0:T(2,128)(2,1)} custom-call(bf16[32,656,128]{2,1,0:T(8,128)(2,1)} %bitcast.1), custom_call_target="tpu_custom_call" | custom-call | tf_op jit(solution)/shard_map/pallas_call | solution.py:209
  (6 shorter events, 0.0 us)
Async XLA Ops:
  7.2 96.2 %all-gather.3.cloned.1.call-start = ((), (), s32[]{:S(2)}) async-start(), calls=%async_computation | async-start | bytes 5541888 | tf_op jit(solution)/shard_map/all_gather | solution.py:243
  10.6 4.2 %collective-permute-start = (f32[16,128]{1,0:T(8,128)}, f32[16,128]{1,0:T(8,128)S(1)}, u32[]{:S(2)}, u32[]{:S(2)}) collective-permute-start(f32[16,128]{1,0:T(8,128)} %get-tuple-element.13), channel_id=1, source_target_pairs={{0,8},{8,0},{16,24},{24,16},{32,40},{40,32},{48,56},{56,48},{64,72... | collective-permute-start | bytes 24584 | tf_op jit(solution)/shard_map/ppermute | solution.py:77
  15.5 2.5 %collective-permute-start.1 = (f32[16,128]{1,0:T(8,128)S(1)}, f32[16,128]{1,0:T(8,128)S(1)}, u32[]{:S(2)}, u32[]{:S(2)}) collective-permute-start(f32[16,128]{1,0:T(8,128)S(1)} %add.27), channel_id=1, source_target_pairs={{0,16},{8,24},{16,0},{24,8},{32,48},{40,56},{48,32},{56,40},{64,80... | collective-permute-start | bytes 24584 | tf_op jit(solution)/shard_map/ppermute | solution.py:77
  18.0 3.7 %collective-permute-start.2 = (f32[16,128]{1,0:T(8,128)S(1)}, f32[16,128]{1,0:T(8,128)S(1)}, u32[]{:S(2)}, u32[]{:S(2)}) collective-permute-start(f32[16,128]{1,0:T(8,128)S(1)} %add.28), channel_id=1, source_target_pairs={{0,48},{8,56},{16,32},{24,40},{32,16},{40,24},{48,0},{56,8},{64,11... | collective-permute-start | bytes 24584 | tf_op jit(solution)/shard_map/ppermute | solution.py:77
  21.8 2.5 %collective-permute-start.3 = (f32[16,128]{1,0:T(8,128)S(1)}, f32[16,128]{1,0:T(8,128)S(1)}, u32[]{:S(2)}, u32[]{:S(2)}) collective-permute-start(f32[16,128]{1,0:T(8,128)S(1)} %add.29), channel_id=1, source_target_pairs={{0,64},{8,72},{16,80},{24,88},{32,96},{40,104},{48,112},{56,120},{... | collective-permute-start | bytes 24584 | tf_op jit(solution)/shard_map/ppermute | solution.py:77
  24.3 3.7 %collective-permute-start.4 = (f32[16,128]{1,0:T(8,128)S(1)}, f32[16,128]{1,0:T(8,128)S(1)}, u32[]{:S(2)}, u32[]{:S(2)}) collective-permute-start(f32[16,128]{1,0:T(8,128)S(1)} %add.30), channel_id=1, source_target_pairs={{0,192},{8,200},{16,208},{24,216},{32,224},{40,232},{48,240},{56,2... | collective-permute-start | bytes 24584 | tf_op jit(solution)/shard_map/ppermute | solution.py:77
  28.0 2.5 %collective-permute-start.5 = (f32[16,128]{1,0:T(8,128)S(1)}, f32[16,128]{1,0:T(8,128)S(1)}, u32[]{:S(2)}, u32[]{:S(2)}) collective-permute-start(f32[16,128]{1,0:T(8,128)S(1)} %add.31), channel_id=1, source_target_pairs={{0,1},{1,0},{2,3},{3,2},{4,5},{5,4},{6,7},{7,6},{8,9},{9,8},{10,11... | collective-permute-start | bytes 24584 | tf_op jit(solution)/shard_map/ppermute | solution.py:77
  30.5 3.4 %collective-permute-start.6 = (f32[16,128]{1,0:T(8,128)S(1)}, f32[16,128]{1,0:T(8,128)S(1)}, u32[]{:S(2)}, u32[]{:S(2)}) collective-permute-start(f32[16,128]{1,0:T(8,128)S(1)} %add.32), channel_id=1, source_target_pairs={{0,2},{1,3},{2,0},{3,1},{4,6},{5,7},{6,4},{7,5},{8,10},{9,11},{10,... | collective-permute-start | bytes 24584 | tf_op jit(solution)/shard_map/ppermute | solution.py:77
  33.9 5.4 %copy-start = (f32[16,128]{1,0:T(8,128)}, f32[16,128]{1,0:T(8,128)S(1)}, u32[]{:S(2)}) copy-start(f32[16,128]{1,0:T(8,128)S(1)} %add.33.held_ref) | copy-start | bytes 24580
  33.9 5.4 %collective-permute-start.7 = (f32[16,128]{1,0:T(8,128)S(1)}, f32[16,128]{1,0:T(8,128)S(1)}, u32[]{:S(2)}, u32[]{:S(2)}) collective-permute-start(f32[16,128]{1,0:T(8,128)S(1)} %add.33.held_ref), channel_id=1, source_target_pairs={{0,6},{1,7},{2,4},{3,5},{4,2},{5,3},{6,0},{7,1},{8,14},{9,15},{10,... | collective-permute-start | bytes 24584 | tf_op jit(solution)/shard_map/ppermute | solution.py:77
  39.3 0.6 copy-start.1
Sparse Core Ops, SparseCore 0:
  42.7 60.5 all-gather.2
